TPU v7x, 512 devices: a whole 4x8x8 slice. The times are simulated.
512 devices in a mesh: lon: 16 (over x_hi, y), lat: 16 (over z, core), segment: 2 (over x_lo).
Axes of the slice: x: 4 (x_hi: 2, x_lo: 2; x = x_hi * 2 + x_lo), y: 8, z: 8, core: 2. Of those that a mesh axis runs over, the one named last changes fastest.
Arguments:
- initial_state: float32 [2, 32, 64, 8, 384], P(None, 'lat', 'lon'), may hold values from -6 to 6
- mask_ids: int32 [32, 64], P('lat', 'lon'), may hold values from 0 to 7
- lead_steps: int32 [2], replicated, may hold values from 0 to 7, as said below
- mask_table: float32 [2, 8, 384], P('segment'), may hold values from -3 to 3
- lead_table: float32 [2, 8, 384], P('segment'), may hold values from -3 to 3
- w_qkv: bfloat16 [2, 384, 1152], P('segment'), may hold values from -0.3125 to 0.3125
- w_out: bfloat16 [2, 384, 384], P('segment'), may hold values from -0.3125 to 0.3125
- w_up: bfloat16 [2, 384, 1536], P('segment'), may hold values from -0.3125 to 0.3125
- w_down: bfloat16 [2, 1536, 384], P('segment'), may hold values from -0.15625 to 0.15625
- norm_gains: float32 [2, 3, 384], P('segment'), may hold values from 0.5 to 1.5
- merid_taps: float32 [2, 5, 384], P('segment'), may hold values from -1.5 to 1.5
- score_bias: float32 [2, 12, 8, 64], P('segment'), may hold values from -4 to 250
Outputs:
- forecasts: float32 [2, 2, 32, 64, 8, 384], P('segment', None, 'lat', 'lon')
Inputs may be any that keep to these rules, and one draw needn't show every extreme that they name: `lead_steps`: the two rollout steps have different lead-time classes.
All inputs are finite; a program needn't handle non-finite values.
Results may differ from a plain program's by a relative error of at most 0.012.
Values may be sent and summed in bfloat16 or wider, within the bound.
No kernel may reach another device: no remote copies, remote signals or barrier semaphores. Data moves between devices by JAX's collectives and lax.ppermute only.
A program may use at most 64 MiB of HBM per device.

v0:
```python
import jax
import jax.numpy as jnp
from jax import lax
from jax.sharding import PartitionSpec as P

epsilon = 1e-05


def layer_norm(values, gain_row):
    mean_val = jnp.mean(values, axis=-1, keepdims=True)
    centered = values - mean_val
    variance = jnp.mean(centered * centered, axis=-1, keepdims=True)
    return centered * lax.rsqrt(variance + epsilon) * gain_row


def lat_halo(array, width):
    devices, length = lax.axis_size("lat"), array.shape[1]
    up = [(i, i + 1) for i in range(devices - 1)]
    down = [(j, i) for i, j in up]
    before = lax.ppermute(array[:, length - width :], "lat", up)
    after = lax.ppermute(array[:, :width], "lat", down)
    return jnp.concatenate([before, array, after], axis=1)


def head_bias(bias_segment, groups, lon_total, levels):
    heads_here = bias_segment.shape[0] // groups
    group = lax.axis_index("lon") // (lax.axis_size("lon") // groups)
    picked = lax.dynamic_slice_in_dim(bias_segment, group * heads_here, heads_here, axis=0)
    lhs = picked.reshape(heads_here * levels, lon_total)
    high = lhs.astype(jnp.bfloat16)
    rest = lhs - high.astype(jnp.float32)
    middle = rest.astype(jnp.bfloat16)
    low = (rest - middle.astype(jnp.float32)).astype(jnp.bfloat16)
    lon = jnp.arange(lon_total, dtype=jnp.int32)
    key_lon = jnp.repeat(lon, levels)
    offsets = jnp.mod(key_lon[None, :] - lon[:, None], lon_total)
    onehot = (lon[:, None, None] == offsets[None]).astype(jnp.bfloat16).reshape(lon_total, -1)
    parts = [
        jnp.dot(part, onehot, preferred_element_type=jnp.float32) for part in (high, middle, low)
    ]
    table = (parts[0] + parts[1]) + parts[2]
    table = table.reshape(heads_here, levels, lon_total, lon_total * levels)
    table = jnp.transpose(table, (0, 2, 1, 3))
    return table.reshape(heads_here, lon_total * levels, lon_total * levels)


def block(field, lead_index, mask_ids, params, bias_full):
    mask_tab, lead_tab, wqkv, wout, wup, wdown, gains, taps = params
    members, rows_lat, lon_local, levels, features = field.shape
    groups, _, group_width = wqkv.shape
    heads_here = bias_full.shape[0]
    head_dim = group_width // (3 * heads_here)
    lon_devices = lax.axis_size("lon")
    tokens_local = lon_local * levels
    combos = members * rows_lat

    mask_embed = jnp.take(mask_tab, mask_ids, axis=0)
    lead_row = lax.dynamic_index_in_dim(lead_tab, lead_index, axis=0, keepdims=False)
    hidden = field + mask_embed[None, :, :, None, :] + lead_row
    normed = layer_norm(hidden, gains[0]).astype(jnp.bfloat16)
    spread = jnp.broadcast_to(normed.reshape(1, -1, features), (groups, combos * tokens_local, features))
    projected = jnp.einsum(
        "gnc,gcf->gnf", spread, wqkv, preferred_element_type=jnp.float32
    ).astype(jnp.bfloat16)
    outgoing = projected.reshape(lon_devices, tokens_local, group_width)
    incoming = lax.all_to_all(outgoing, "lon", 0, 0, tiled=True)
    incoming = incoming.reshape(lon_devices * tokens_local, 3, heads_here, head_dim)
    queries, keys, values = incoming[:, 0], incoming[:, 1], incoming[:, 2]
    scores = jnp.einsum(
        "qhd,khd->hqk", queries, keys, preferred_element_type=jnp.float32
    ) * (head_dim ** (-0.5)) + bias_full
    row_max = jnp.max(scores, axis=-1, keepdims=True)
    weights = jnp.exp(scores - row_max)
    total = jnp.sum(weights, axis=-1, keepdims=True)
    summed = jnp.einsum(
        "hqk,khd->hqd", weights.astype(jnp.bfloat16), values, preferred_element_type=jnp.float32
    )
    attended = (summed / total).astype(jnp.bfloat16)
    back = jnp.transpose(attended, (1, 0, 2)).reshape(lon_devices, tokens_local, heads_here * head_dim)
    returned = lax.all_to_all(back, "lon", 0, 0, tiled=True)
    returned = returned.reshape(groups, combos * tokens_local, heads_here * head_dim)
    projected_out = jnp.einsum("gnf,gfo->no", returned, wout, preferred_element_type=jnp.float32)
    hidden2 = hidden + projected_out.reshape(hidden.shape)
    normed2 = layer_norm(hidden2, gains[1]).astype(jnp.bfloat16)
    padded = lat_halo(normed2, 2)
    window_sum = jnp.zeros_like(hidden2)
    for offset_row in range(5):
        window_sum = window_sum + taps[offset_row] * padded[:, offset_row : offset_row + rows_lat].astype(
            jnp.float32
        )
    hidden3 = hidden2 + window_sum
    normed3 = layer_norm(hidden3, gains[2]).astype(jnp.bfloat16)
    activated = jax.nn.gelu(
        jnp.dot(normed3.reshape(-1, features), wup, preferred_element_type=jnp.float32),
        approximate=True,
    ).astype(jnp.bfloat16)
    return hidden3 + jnp.dot(activated, wdown, preferred_element_type=jnp.float32).reshape(hidden.shape)


def from_partner(array):
    return lax.ppermute(array, "segment", [(i, i ^ 1) for i in range(lax.axis_size("segment"))])


def body(
    initial_state,
    mask_ids,
    lead_steps,
    mask_table,
    lead_table,
    w_qkv,
    w_out,
    w_up,
    w_down,
    norm_gains,
    merid_taps,
    score_bias,
):
    members, rows_lat = initial_state.shape[0], initial_state.shape[1]
    lon_local = initial_state.shape[2]
    lon_devices = lax.axis_size("lon")
    head_count = score_bias.shape[1]
    groups = lon_devices // (members * rows_lat)
    mask_tab, lead_tab, wqkv, wout, wup, wdown, gains, taps = tuple(
        item[0] for item in (mask_table, lead_table, w_qkv, w_out, w_up, w_down, norm_gains, merid_taps)
    )
    features = wqkv.shape[0]
    head_dim = features // head_count
    heads_here = head_count // groups
    wqkv = jnp.transpose(wqkv.reshape(features, 3, groups, heads_here * head_dim), (2, 0, 1, 3))
    wqkv = wqkv.reshape(groups, features, 3 * heads_here * head_dim)
    wout = wout.reshape(groups, heads_here * head_dim, features)
    params = (mask_tab, lead_tab, wqkv, wout, wup, wdown, gains, taps)
    bias_full = head_bias(score_bias[0], groups, lon_local * lon_devices, initial_state.shape[3])
    segment_first = lax.axis_index("segment") == 0
    current = initial_state
    first = None
    for tick_num in range(4):
        result = block(current, lead_steps[tick_num // 2], mask_ids, params, bias_full)
        if tick_num == 3:
            break
        current = from_partner(result)
        if tick_num == 1:
            first = current
    output = jnp.where(segment_first, first, result)
    return output[None]


def solution(mesh):
    in_specs = (
        P(None, "lat", "lon", None, None),
        P("lat", "lon"),
        P(),
        P("segment", None, None),
        P("segment", None, None),
        P("segment", None, None),
        P("segment", None, None),
        P("segment", None, None),
        P("segment", None, None),
        P("segment", None, None),
        P("segment", None, None),
        P("segment", None, None, None),
    )
    out_specs = P("segment", None, "lat", "lon", None, None)
    return jax.shard_map(body, mesh=mesh, in_specs=in_specs, out_specs=out_specs, check_vma=False)
```

profile of v0, /device:TPU:1, one launch (start us, length us, event | category | flops | bytes accessed | tf_op | source)
XLA Modules:
  0.0 257.3 jit_solution(16365511384648117639)
XLA Ops:
  16.0 10.3 %all-to-all-start = ((bf16[16,32,288]{2,1,0:T(8,128)(2,1)}), bf16[16,32,288]{2,1,0:T(8,128)(2,1)}, u32[]{:S(2)}, u32[]{:S(2)}) async-start(bf16[16,32,288]{2,1,0:T(8,128)(2,1)} %bitcast.6), calls=%async_computation | async-start | bytes 786432 | tf_op jit(solution)/shard_map/all_to_all | solution.py:66
  29.5 3.4 %convolution_add_fusion = f32[24,32768]{1,0:T(8,128)} fusion(f32[24,32768]{1,0:T(8,128)S(1)} %convolution_add_fusion.1, s32[32768]{0:T(1024)S(1)} %add_select_fusion, f32[1,12,8,64]{3,2,1,0:T(8,128)S(1)} %copy-done.34, s32[]{:T(128)S(6)} %select_n.49), kind=kOutput, calls=%fused_computation.1 | convolution fusion | flops 103557632 | bytes 6434820 | tf_op jit(solution)/shard_map/dot_general | solution.py:39
  32.9 3.6 %copy.122 = f32[3,512,512]{1,2,0:T(8,128)} copy(f32[3,512,512]{2,1,0:T(8,128)} %bitcast.255) | data formatting | bytes 6291456 | tf_op jit(solution)/shard_map/reshape | solution.py:44
  36.4 2.1 all-to-all-done
  38.6 2.1 copy.121
  41.9 2.5 fusion.173
  46.1 15.8 %all_to_all.40 = bf16[16,32,96]{2,1,0:T(8,128)(2,1)S(1)} all-to-all(bf16[16,32,96]{2,1,0:T(8,128)(2,1)S(1)} %copy.124), channel_id=1, replica_groups=mesh['lon'=16,'lat'=16,'segment'=2] {'lon'}, dimensions={0} | all-to-all | bytes 196608 | tf_op jit(solution)/shard_map/all_to_all | solution.py:80
  62.6 4.6 %collective-permute-start.1 = (bf16[2,2,4,8,384]{4,3,2,1,0:T(8,128)(2,1)S(1)}, bf16[2,2,4,8,384]{4,3,2,1,0:T(8,128)(2,1)S(1)}, u32[]{:S(2)}, u32[]{:S(2)}) collective-permute-start(bf16[2,2,4,8,384]{4,3,2,1,0:T(8,128)(2,1)S(1)} %multiply_convert_fusion.10), channel_id=1, source_target_pairs={{2,0},{4,2},{6,4},{8,6},{10,8},{12,10},{14,12},{16,14},{18,16},{20... | collective-permute-start | bytes 294920 | tf_op jit(solution)/shard_map/ppermute | solution.py:21
  67.1 4.1 %collective-permute-start = (bf16[2,2,4,8,384]{4,3,2,1,0:T(8,128)(2,1)S(1)}, bf16[2,2,4,8,384]{4,3,2,1,0:T(8,128)(2,1)S(1)}, u32[]{:S(2)}, u32[]{:S(2)}) collective-permute-start(bf16[2,2,4,8,384]{4,3,2,1,0:T(8,128)(2,1)S(1)} %multiply_convert_fusion.10), channel_id=1, source_target_pairs={{0,2},{2,4},{4,6},{6,8},{8,10},{10,12},{12,14},{14,16},{16,18},{18... | collective-permute-start | bytes 294920 | tf_op jit(solution)/shard_map/ppermute | solution.py:20
  74.0 2.2 collective-permute-start.2
  76.3 4.7 %collective-permute-done.2 = f32[2,2,4,8,384]{4,3,2,1,0:T(8,128)S(1)} collective-permute-done((f32[2,2,4,8,384]{4,3,2,1,0:T(8,128)S(1)}, f32[2,2,4,8,384]{4,3,2,1,0:T(8,128)S(1)}, u32[]{:S(2)}, u32[]{:S(2)}) %collective-permute-start.2) | collective-permute-done | bytes 196640 | tf_op jit(solution)/shard_map/ppermute | solution.py:101
  82.4 17.4 %all_to_all.41 = bf16[16,32,288]{2,1,0:T(8,128)(2,1)} all-to-all(bf16[16,32,288]{2,1,0:T(8,128)(2,1)S(1)} %bitcast.261), channel_id=1, replica_groups=mesh['lon'=16,'lat'=16,'segment'=2] {'lon'}, dimensions={0} | all-to-all | bytes 589824 | tf_op jit(solution)/shard_map/all_to_all | solution.py:66
  99.8 2.1 copy.126
  103.8 2.6 %fusion.174 = (f32[3,512]{1,0:T(4,128)S(1)}, f32[3,512,512]{1,2,0:T(8,128)S(1)}) fusion(f32[3,512,512]{1,2,0:T(8,128)} %copy.122, bf16[512,3,3,32]{0,3,2,1:T(8,128)(2,1)} %reshape.332), kind=kOutput, calls=%fused_computation.237 | convolution fusion | flops 52689408 | bytes 6494208 | tf_op jit(solution)/shard_map/qhd,khd->hqk/dot_general | solution.py:69
  109.1 13.3 %all_to_all.42 = bf16[16,32,96]{2,1,0:T(8,128)(2,1)S(1)} all-to-all(bf16[16,32,96]{2,1,0:T(8,128)(2,1)S(1)} %copy.129), channel_id=1, replica_groups=mesh['lon'=16,'lat'=16,'segment'=2] {'lon'}, dimensions={0} | all-to-all | bytes 196608 | tf_op jit(solution)/shard_map/all_to_all | solution.py:80
  123.1 3.9 %collective-permute-start.4 = (bf16[2,2,4,8,384]{4,3,2,1,0:T(8,128)(2,1)S(1)}, bf16[2,2,4,8,384]{4,3,2,1,0:T(8,128)(2,1)S(1)}, u32[]{:S(2)}, u32[]{:S(2)}) collective-permute-start(bf16[2,2,4,8,384]{4,3,2,1,0:T(8,128)(2,1)S(1)} %multiply_convert_fusion.7), channel_id=1, source_target_pairs={{2,0},{4,2},{6,4},{8,6},{10,8},{12,10},{14,12},{16,14},{18,16},{20... | collective-permute-start | bytes 294920 | tf_op jit(solution)/shard_map/ppermute | solution.py:21
  127.0 5.6 %collective-permute-start.3 = (bf16[2,2,4,8,384]{4,3,2,1,0:T(8,128)(2,1)S(1)}, bf16[2,2,4,8,384]{4,3,2,1,0:T(8,128)(2,1)S(1)}, u32[]{:S(2)}, u32[]{:S(2)}) collective-permute-start(bf16[2,2,4,8,384]{4,3,2,1,0:T(8,128)(2,1)S(1)} %multiply_convert_fusion.7), channel_id=1, source_target_pairs={{0,2},{2,4},{4,6},{6,8},{8,10},{10,12},{12,14},{14,16},{16,18},{18... | collective-permute-start | bytes 294920 | tf_op jit(solution)/shard_map/ppermute | solution.py:20
  135.6 2.1 collective-permute-start.5
  137.7 4.3 %collective-permute-done.5 = f32[2,2,4,8,384]{4,3,2,1,0:T(8,128)S(1)} collective-permute-done((f32[2,2,4,8,384]{4,3,2,1,0:T(8,128)S(1)}, f32[2,2,4,8,384]{4,3,2,1,0:T(8,128)S(1)}, u32[]{:S(2)}, u32[]{:S(2)}) %collective-permute-start.5) | collective-permute-done | bytes 196640 | tf_op jit(solution)/shard_map/ppermute | solution.py:101
  143.1 15.4 %all_to_all.43 = bf16[16,32,288]{2,1,0:T(8,128)(2,1)} all-to-all(bf16[16,32,288]{2,1,0:T(8,128)(2,1)S(1)} %bitcast.262), channel_id=1, replica_groups=mesh['lon'=16,'lat'=16,'segment'=2] {'lon'}, dimensions={0} | all-to-all | bytes 589824 | tf_op jit(solution)/shard_map/all_to_all | solution.py:66
  158.5 2.1 copy.131
  160.6 1.9 reshape.337
  162.6 2.6 %fusion.175 = (f32[3,512]{1,0:T(4,128)S(1)}, f32[3,512,512]{1,2,0:T(8,128)S(1)}) fusion(f32[3,512,512]{1,2,0:T(8,128)} %copy.122, bf16[512,3,3,32]{0,3,2,1:T(8,128)(2,1)} %reshape.337), kind=kOutput, calls=%fused_computation.238 | convolution fusion | flops 52689408 | bytes 6494208 | tf_op jit(solution)/shard_map/qhd,khd->hqk/dot_general | solution.py:69
  167.7 13.5 %all_to_all.44 = bf16[16,32,96]{2,1,0:T(8,128)(2,1)S(1)} all-to-all(bf16[16,32,96]{2,1,0:T(8,128)(2,1)S(1)} %copy.134), channel_id=1, replica_groups=mesh['lon'=16,'lat'=16,'segment'=2] {'lon'}, dimensions={0} | all-to-all | bytes 196608 | tf_op jit(solution)/shard_map/all_to_all | solution.py:80
  181.9 3.1 %collective-permute-start.7 = (bf16[2,2,4,8,384]{4,3,2,1,0:T(8,128)(2,1)S(1)}, bf16[2,2,4,8,384]{4,3,2,1,0:T(8,128)(2,1)S(1)}, u32[]{:S(2)}, u32[]{:S(2)}) collective-permute-start(bf16[2,2,4,8,384]{4,3,2,1,0:T(8,128)(2,1)S(1)} %multiply_convert_fusion.4), channel_id=1, source_target_pairs={{2,0},{4,2},{6,4},{8,6},{10,8},{12,10},{14,12},{16,14},{18,16},{20... | collective-permute-start | bytes 294920 | tf_op jit(solution)/shard_map/ppermute | solution.py:21
  185.0 8.5 %collective-permute-start.6 = (bf16[2,2,4,8,384]{4,3,2,1,0:T(8,128)(2,1)S(1)}, bf16[2,2,4,8,384]{4,3,2,1,0:T(8,128)(2,1)S(1)}, u32[]{:S(2)}, u32[]{:S(2)}) collective-permute-start(bf16[2,2,4,8,384]{4,3,2,1,0:T(8,128)(2,1)S(1)} %multiply_convert_fusion.4), channel_id=1, source_target_pairs={{0,2},{2,4},{4,6},{6,8},{8,10},{10,12},{12,14},{14,16},{16,18},{18... | collective-permute-start | bytes 294920 | tf_op jit(solution)/shard_map/ppermute | solution.py:20
  196.5 2.1 collective-permute-start.8
  198.6 4.3 %collective-permute-done.8 = f32[2,2,4,8,384]{4,3,2,1,0:T(8,128)S(1)} collective-permute-done((f32[2,2,4,8,384]{4,3,2,1,0:T(8,128)S(1)}, f32[2,2,4,8,384]{4,3,2,1,0:T(8,128)S(1)}, u32[]{:S(2)}, u32[]{:S(2)}) %collective-permute-start.8) | collective-permute-done | bytes 196640 | tf_op jit(solution)/shard_map/ppermute | solution.py:101
  204.0 13.6 %all_to_all.45 = bf16[16,32,288]{2,1,0:T(8,128)(2,1)S(1)} all-to-all(bf16[16,32,288]{2,1,0:T(8,128)(2,1)S(1)} %bitcast.263), channel_id=1, replica_groups=mesh['lon'=16,'lat'=16,'segment'=2] {'lon'}, dimensions={0} | all-to-all | bytes 589824 | tf_op jit(solution)/shard_map/all_to_all | solution.py:66
  220.0 2.5 fusion.176
  224.8 13.1 %all_to_all.46 = bf16[16,32,96]{2,1,0:T(8,128)(2,1)S(1)} all-to-all(bf16[16,32,96]{2,1,0:T(8,128)(2,1)} %copy.139), channel_id=1, replica_groups=mesh['lon'=16,'lat'=16,'segment'=2] {'lon'}, dimensions={0} | all-to-all | bytes 196608 | tf_op jit(solution)/shard_map/all_to_all | solution.py:80
  240.5 13.1 %collective-permute-start.9 = (bf16[2,2,4,8,384]{4,3,2,1,0:T(8,128)(2,1)S(1)}, bf16[2,2,4,8,384]{4,3,2,1,0:T(8,128)(2,1)S(1)}, u32[]{:S(2)}, u32[]{:S(2)}) collective-permute-start(bf16[2,2,4,8,384]{4,3,2,1,0:T(8,128)(2,1)S(1)} %multiply_convert_fusion.1), channel_id=1, source_target_pairs={{0,2},{2,4},{4,6},{6,8},{8,10},{10,12},{12,14},{14,16},{16,18},{18... | collective-permute-start | bytes 294920 | tf_op jit(solution)/shard_map/ppermute | solution.py:20
  (199 shorter events, 49.8 us)
Async XLA Ops:
  0.0 73.2 %copy-start = (bf16[1,384,1536]{2,1,0:T(8,128)(2,1)S(1)}, bf16[1,384,1536]{2,1,0:T(8,128)(2,1)}, u32[]{:S(2)}) copy-start(bf16[1,384,1536]{2,1,0:T(8,128)(2,1)} %param.21) | copy-start | bytes 3538948
  16.0 22.5 %all-to-all-start = ((bf16[16,32,288]{2,1,0:T(8,128)(2,1)}), bf16[16,32,288]{2,1,0:T(8,128)(2,1)}, u32[]{:S(2)}, u32[]{:S(2)}) async-start(bf16[16,32,288]{2,1,0:T(8,128)(2,1)} %bitcast.6), calls=%async_computation | async-start | bytes 786432 | tf_op jit(solution)/shard_map/all_to_all | solution.py:66
  44.4 17.4 %copy-start.1 = (bf16[1,384,384]{2,1,0:T(8,128)(2,1)S(1)}, bf16[1,384,384]{2,1,0:T(8,128)(2,1)}, u32[]{:S(2)}) copy-start(bf16[1,384,384]{2,1,0:T(8,128)(2,1)} %param.20) | copy-start | bytes 884740
  44.8 17.2 %copy-start.5 = (f32[2,2,4,8,384]{4,3,2,1,0:T(8,128)S(1)}, f32[2,2,4,8,384]{4,3,2,1,0:T(8,128)}, u32[]{:S(2)}) copy-start(f32[2,2,4,8,384]{4,3,2,1,0:T(8,128)} %param.14) | copy-start | bytes 589828
  44.9 17.2 %copy-start.15 = (f32[384]{0:T(512)S(1)}, f32[384]{0:T(512)}, u32[]{:S(2)}) copy-start(f32[384]{0:T(512)} %copy-done.14) | copy-start | bytes 4612
  44.9 17.6 %copy-start.29 = (f32[384]{0:T(512)S(1)}, f32[384]{0:T(512)}, u32[]{:S(2)}) copy-start(f32[384]{0:T(512)} %get-tuple-element.15) | copy-start | bytes 4612
  45.5 27.6 %copy-start.27 = (f32[384]{0:T(512)S(1)}, f32[384]{0:T(512)}, u32[]{:S(2)}) copy-start(f32[384]{0:T(512)} %get-tuple-element.13) | copy-start | bytes 4612
  46.0 27.6 %copy-start.10 = (bf16[1,1536,384]{2,1,0:T(8,128)(2,1)S(1)}, bf16[1,1536,384]{2,1,0:T(8,128)(2,1)}, u32[]{:S(2)}) copy-start(bf16[1,1536,384]{2,1,0:T(8,128)(2,1)} %param.22) | copy-start | bytes 3538948
  62.6 9.5 %collective-permute-start.1 = (bf16[2,2,4,8,384]{4,3,2,1,0:T(8,128)(2,1)S(1)}, bf16[2,2,4,8,384]{4,3,2,1,0:T(8,128)(2,1)S(1)}, u32[]{:S(2)}, u32[]{:S(2)}) collective-permute-start(bf16[2,2,4,8,384]{4,3,2,1,0:T(8,128)(2,1)S(1)} %multiply_convert_fusion.10), channel_id=1, source_target_pairs={{2,0},{4,2},{6,4},{8,6},{10,8},{12,10},{14,12},{16,14},{18,16},{20... | collective-permute-start | bytes 294920 | tf_op jit(solution)/shard_map/ppermute | solution.py:21
  67.1 5.5 %collective-permute-start = (bf16[2,2,4,8,384]{4,3,2,1,0:T(8,128)(2,1)S(1)}, bf16[2,2,4,8,384]{4,3,2,1,0:T(8,128)(2,1)S(1)}, u32[]{:S(2)}, u32[]{:S(2)}) collective-permute-start(bf16[2,2,4,8,384]{4,3,2,1,0:T(8,128)(2,1)S(1)} %multiply_convert_fusion.10), channel_id=1, source_target_pairs={{0,2},{2,4},{4,6},{6,8},{8,10},{10,12},{12,14},{14,16},{16,18},{18... | collective-permute-start | bytes 294920 | tf_op jit(solution)/shard_map/ppermute | solution.py:20
  74.0 6.9 %collective-permute-start.2 = (f32[2,2,4,8,384]{4,3,2,1,0:T(8,128)S(1)}, f32[2,2,4,8,384]{4,3,2,1,0:T(8,128)S(1)}, u32[]{:S(2)}, u32[]{:S(2)}) collective-permute-start(f32[2,2,4,8,384]{4,3,2,1,0:T(8,128)S(1)} %fusion.40), channel_id=1, source_target_pairs={{0,1},{1,0},{2,3},{3,2},{4,5},{5,4},{6,7},{7,6},{8,9},{9,8},{10,11... | collective-permute-start | bytes 589832 | tf_op jit(solution)/shard_map/ppermute | solution.py:101
  106.9 15.8 %copy-start.9 = (f32[2,2,4,8,384]{4,3,2,1,0:T(8,128)S(1)}, f32[2,2,4,8,384]{4,3,2,1,0:T(8,128)}, u32[]{:S(2)}) copy-start(f32[2,2,4,8,384]{4,3,2,1,0:T(8,128)} %copy-done.8) | copy-start | bytes 589828
  106.9 15.8 %copy-start.16 = (f32[384]{0:T(512)S(1)}, f32[384]{0:T(512)}, u32[]{:S(2)}) copy-start(f32[384]{0:T(512)} %copy-done.14) | copy-start | bytes 4612
  106.9 16.1 %copy-start.30 = (f32[384]{0:T(512)S(1)}, f32[384]{0:T(512)}, u32[]{:S(2)}) copy-start(f32[384]{0:T(512)} %get-tuple-element.15) | copy-start | bytes 4612
  106.9 27.3 %copy-start.18 = (f32[384]{0:T(512)S(1)}, f32[384]{0:T(512)}, u32[]{:S(2)}) copy-start(f32[384]{0:T(512)} %copy-done.17) | copy-start | bytes 4612
  106.9 27.3 %copy-start.20 = (f32[384]{0:T(512)S(1)}, f32[384]{0:T(512)}, u32[]{:S(2)}) copy-start(f32[384]{0:T(512)} %copy-done.19) | copy-start | bytes 4612
  106.9 27.3 %copy-start.22 = (f32[384]{0:T(512)S(1)}, f32[384]{0:T(512)}, u32[]{:S(2)}) copy-start(f32[384]{0:T(512)} %copy-done.21) | copy-start | bytes 4612
  106.9 27.3 %copy-start.24 = (f32[384]{0:T(512)S(1)}, f32[384]{0:T(512)}, u32[]{:S(2)}) copy-start(f32[384]{0:T(512)} %copy-done.23) | copy-start | bytes 4612
  106.9 27.3 %copy-start.26 = (f32[384]{0:T(512)S(1)}, f32[384]{0:T(512)}, u32[]{:S(2)}) copy-start(f32[384]{0:T(512)} %copy-done.25) | copy-start | bytes 4612
  106.9 27.7 %copy-start.28 = (f32[384]{0:T(512)S(1)}, f32[384]{0:T(512)}, u32[]{:S(2)}) copy-start(f32[384]{0:T(512)} %get-tuple-element.13) | copy-start | bytes 4612
  109.1 26.2 %copy-start.11 = (bf16[1,1536,384]{2,1,0:T(8,128)(2,1)S(1)}, bf16[1,1536,384]{2,1,0:T(8,128)(2,1)}, u32[]{:S(2)}) copy-start(bf16[1,1536,384]{2,1,0:T(8,128)(2,1)} %param.22) | copy-start | bytes 3538948
  123.1 9.8 %collective-permute-start.4 = (bf16[2,2,4,8,384]{4,3,2,1,0:T(8,128)(2,1)S(1)}, bf16[2,2,4,8,384]{4,3,2,1,0:T(8,128)(2,1)S(1)}, u32[]{:S(2)}, u32[]{:S(2)}) collective-permute-start(bf16[2,2,4,8,384]{4,3,2,1,0:T(8,128)(2,1)S(1)} %multiply_convert_fusion.7), channel_id=1, source_target_pairs={{2,0},{4,2},{6,4},{8,6},{10,8},{12,10},{14,12},{16,14},{18,16},{20... | collective-permute-start | bytes 294920 | tf_op jit(solution)/shard_map/ppermute | solution.py:21
  127.0 7.2 %collective-permute-start.3 = (bf16[2,2,4,8,384]{4,3,2,1,0:T(8,128)(2,1)S(1)}, bf16[2,2,4,8,384]{4,3,2,1,0:T(8,128)(2,1)S(1)}, u32[]{:S(2)}, u32[]{:S(2)}) collective-permute-start(bf16[2,2,4,8,384]{4,3,2,1,0:T(8,128)(2,1)S(1)} %multiply_convert_fusion.7), channel_id=1, source_target_pairs={{0,2},{2,4},{4,6},{6,8},{8,10},{10,12},{12,14},{14,16},{16,18},{18... | collective-permute-start | bytes 294920 | tf_op jit(solution)/shard_map/ppermute | solution.py:20
  135.6 6.4 %collective-permute-start.5 = (f32[2,2,4,8,384]{4,3,2,1,0:T(8,128)S(1)}, f32[2,2,4,8,384]{4,3,2,1,0:T(8,128)S(1)}, u32[]{:S(2)}, u32[]{:S(2)}) collective-permute-start(f32[2,2,4,8,384]{4,3,2,1,0:T(8,128)S(1)} %fusion.43), channel_id=1, source_target_pairs={{0,1},{1,0},{2,3},{3,2},{4,5},{5,4},{6,7},{7,6},{8,9},{9,8},{10,11... | collective-permute-start | bytes 589832 | tf_op jit(solution)/shard_map/ppermute | solution.py:101
  165.2 16.0 %copy-start.2 = (bf16[1,384,384]{2,1,0:T(8,128)(2,1)S(1)}, bf16[1,384,384]{2,1,0:T(8,128)(2,1)}, u32[]{:S(2)}) copy-start(bf16[1,384,384]{2,1,0:T(8,128)(2,1)} %param.20) | copy-start | bytes 884740
  167.7 28.4 %copy-start.12 = (bf16[1,1536,384]{2,1,0:T(8,128)(2,1)S(1)}, bf16[1,1536,384]{2,1,0:T(8,128)(2,1)}, u32[]{:S(2)}) copy-start(bf16[1,1536,384]{2,1,0:T(8,128)(2,1)} %param.22) | copy-start | bytes 3538948
  181.9 12.0 %collective-permute-start.7 = (bf16[2,2,4,8,384]{4,3,2,1,0:T(8,128)(2,1)S(1)}, bf16[2,2,4,8,384]{4,3,2,1,0:T(8,128)(2,1)S(1)}, u32[]{:S(2)}, u32[]{:S(2)}) collective-permute-start(bf16[2,2,4,8,384]{4,3,2,1,0:T(8,128)(2,1)S(1)} %multiply_convert_fusion.4), channel_id=1, source_target_pairs={{2,0},{4,2},{6,4},{8,6},{10,8},{12,10},{14,12},{16,14},{18,16},{20... | collective-permute-start | bytes 294920 | tf_op jit(solution)/shard_map/ppermute | solution.py:21
  185.0 10.1 %collective-permute-start.6 = (bf16[2,2,4,8,384]{4,3,2,1,0:T(8,128)(2,1)S(1)}, bf16[2,2,4,8,384]{4,3,2,1,0:T(8,128)(2,1)S(1)}, u32[]{:S(2)}, u32[]{:S(2)}) collective-permute-start(bf16[2,2,4,8,384]{4,3,2,1,0:T(8,128)(2,1)S(1)} %multiply_convert_fusion.4), channel_id=1, source_target_pairs={{0,2},{2,4},{4,6},{6,8},{8,10},{10,12},{12,14},{14,16},{16,18},{18... | collective-permute-start | bytes 294920 | tf_op jit(solution)/shard_map/ppermute | solution.py:20
  196.5 6.4 %collective-permute-start.8 = (f32[2,2,4,8,384]{4,3,2,1,0:T(8,128)S(1)}, f32[2,2,4,8,384]{4,3,2,1,0:T(8,128)S(1)}, u32[]{:S(2)}, u32[]{:S(2)}) collective-permute-start(f32[2,2,4,8,384]{4,3,2,1,0:T(8,128)S(1)} %fusion.46), channel_id=1, source_target_pairs={{0,1},{1,0},{2,3},{3,2},{4,5},{5,4},{6,7},{7,6},{8,9},{9,8},{10,11... | collective-permute-start | bytes 589832 | tf_op jit(solution)/shard_map/ppermute | solution.py:101
  224.8 31.4 %copy-start.13 = (bf16[1,1536,384]{2,1,0:T(8,128)(2,1)S(1)}, bf16[1,1536,384]{2,1,0:T(8,128)(2,1)}, u32[]{:S(2)}) copy-start(bf16[1,1536,384]{2,1,0:T(8,128)(2,1)} %param.22) | copy-start | bytes 3538948
  238.6 15.4 %collective-permute-start.10 = (bf16[2,2,4,8,384]{4,3,2,1,0:T(8,128)(2,1)S(1)}, bf16[2,2,4,8,384]{4,3,2,1,0:T(8,128)(2,1)S(1)}, u32[]{:S(2)}, u32[]{:S(2)}) collective-permute-start(bf16[2,2,4,8,384]{4,3,2,1,0:T(8,128)(2,1)S(1)} %multiply_convert_fusion.1), channel_id=1, source_target_pairs={{2,0},{4,2},{6,4},{8,6},{10,8},{12,10},{14,12},{16,14},{18,16},{20... | collective-permute-start | bytes 294920 | tf_op jit(solution)/shard_map/ppermute | solution.py:21
  240.5 14.8 %collective-permute-start.9 = (bf16[2,2,4,8,384]{4,3,2,1,0:T(8,128)(2,1)S(1)}, bf16[2,2,4,8,384]{4,3,2,1,0:T(8,128)(2,1)S(1)}, u32[]{:S(2)}, u32[]{:S(2)}) collective-permute-start(bf16[2,2,4,8,384]{4,3,2,1,0:T(8,128)(2,1)S(1)} %multiply_convert_fusion.1), channel_id=1, source_target_pairs={{0,2},{2,4},{4,6},{6,8},{8,10},{10,12},{12,14},{14,16},{16,18},{18... | collective-permute-start | bytes 294920 | tf_op jit(solution)/shard_map/ppermute | solution.py:20
  (15 other events, 135.3 us)
where the time goes:
time: 259 us; the launch traced here: 257 us
  blocking collectives  102 us (39%)
  starting transfers between devices  61.4 us (24%)
  local copies, waits for them, and re-layouts  29.8 us (12%)
  matrix products  27.5 us (11%)
  waiting for transfers between devices  20.9 us (8%)
  other arithmetic  10.6 us (4%)
  between operations  5.08 us (2%)
    all_to_all x4, blocking collectives, block(): returned = lax.all_to_all(back, 'lon', 0, 0, tiled=True)  55.6 us
    all_to_all x3, blocking collectives, block(): incoming = lax.all_to_all(outgoing, 'lon', 0, 0, tiled=True)  46.5 us
    ppermute x4, starting transfers between devices, lat_halo(): before = lax.ppermute(array[:, length - width:], 'lat', up)  31.3 us
    ppermute x4, starting transfers between devices, lat_halo(): after = lax.ppermute(array[:, :width], 'lat', down)  13.4 us
    ppermute x3, waiting for transfers between devices, from_partner(): lax.ppermute(array, 'segment', [(i, i ^ 1) for i in range(lax.axis_size('...  13.4 us
    dot_general x4, matrix products, block(): jnp.einsum('qhd,khd->hqk', queries, keys, preferred_element_type=jnp.floa...  10.3 us
    all_to_all x1, starting transfers between devices, block(): incoming = lax.all_to_all(outgoing, 'lon', 0, 0, tiled=True)  10.3 us
    all_to_all x4, local copies, waits for them, and re-layouts, block(): incoming = lax.all_to_all(outgoing, 'lon', 0, 0, tiled=True)  7.38 us
  transfers between devices with their start and end apart: 12, of which 11 were waited for; matrix products, arithmetic and copies ran while one was open for 4% of the time, Pallas kernels for 0%

commit v1 on v0

--- a/solution.py
+++ b/solution.py
@@ -1,6 +1,10 @@
+import functools
+
 import jax
 import jax.numpy as jnp
 from jax import lax
+from jax.experimental import pallas as pl
+from jax.experimental.pallas import tpu as pltpu
 from jax.sharding import PartitionSpec as P
 
 epsilon = 1e-05
@@ -44,6 +48,32 @@
     return table.reshape(heads_here, lon_total * levels, lon_total * levels)
 
 
+def attention_kernel(x_ref, bias_ref, o_ref, *, heads, head_dim):
+    width = heads * head_dim
+    for h in range(heads):
+        cols = slice(h * head_dim, (h + 1) * head_dim)
+        q = x_ref[:, cols]
+        k = x_ref[:, width + h * head_dim : width + (h + 1) * head_dim]
+        v = x_ref[:, 2 * width + h * head_dim : 2 * width + (h + 1) * head_dim]
+        s = lax.dot_general(q, k, (((1,), (1,)), ((), ())), preferred_element_type=jnp.float32)
+        s = s * (head_dim ** (-0.5)) + bias_ref[h]
+        row_max = jnp.max(s, axis=-1, keepdims=True)
+        weights = jnp.exp(s - row_max)
+        total = jnp.sum(weights, axis=-1, keepdims=True)
+        summed = jnp.dot(weights.astype(jnp.bfloat16), v, preferred_element_type=jnp.float32)
+        o_ref[:, cols] = (summed / total).astype(o_ref.dtype)
+
+
+def attend(x, bias_full, head_dim):
+    heads = bias_full.shape[0]
+    return pl.pallas_call(
+        functools.partial(attention_kernel, heads=heads, head_dim=head_dim),
+        out_shape=jax.ShapeDtypeStruct((x.shape[0], heads * head_dim), jnp.bfloat16),
+        in_specs=[pl.BlockSpec(memory_space=pltpu.VMEM)] * 2,
+        out_specs=pl.BlockSpec(memory_space=pltpu.VMEM),
+    )(x, bias_full)
+
+
 def block(field, lead_index, mask_ids, params, bias_full):
     mask_tab, lead_tab, wqkv, wout, wup, wdown, gains, taps = params
     members, rows_lat, lon_local, levels, features = field.shape
@@ -64,19 +94,8 @@
     ).astype(jnp.bfloat16)
     outgoing = projected.reshape(lon_devices, tokens_local, group_width)
     incoming = lax.all_to_all(outgoing, "lon", 0, 0, tiled=True)
-    incoming = incoming.reshape(lon_devices * tokens_local, 3, heads_here, head_dim)
-    queries, keys, values = incoming[:, 0], incoming[:, 1], incoming[:, 2]
-    scores = jnp.einsum(
-        "qhd,khd->hqk", queries, keys, preferred_element_type=jnp.float32
-    ) * (head_dim ** (-0.5)) + bias_full
-    row_max = jnp.max(scores, axis=-1, keepdims=True)
-    weights = jnp.exp(scores - row_max)
-    total = jnp.sum(weights, axis=-1, keepdims=True)
-    summed = jnp.einsum(
-        "hqk,khd->hqd", weights.astype(jnp.bfloat16), values, preferred_element_type=jnp.float32
-    )
-    attended = (summed / total).astype(jnp.bfloat16)
-    back = jnp.transpose(attended, (1, 0, 2)).reshape(lon_devices, tokens_local, heads_here * head_dim)
+    attended = attend(incoming.reshape(lon_devices * tokens_local, group_width), bias_full, head_dim)
+    back = attended.reshape(lon_devices, tokens_local, heads_here * head_dim)
     returned = lax.all_to_all(back, "lon", 0, 0, tiled=True)
     returned = returned.reshape(groups, combos * tokens_local, heads_here * head_dim)
     projected_out = jnp.einsum("gnf,gfo->no", returned, wout, preferred_element_type=jnp.float32)

time: 259 us -> 248 us (0.958)
  Pallas kernels: 0 us -> 19 us
  local copies, waits for them, and re-layouts: 29.8 us -> 11.9 us
  matrix products: 27.5 us -> 12.2 us
  waiting for transfers between devices: 20.9 us -> 25.1 us
    pallas_call x0 -> x4, Pallas kernels: none -> 19 us  [attend(): pl.pallas_call(functools.partial(attention_kernel, heads=heads, head_dim=...]
    dot_general x8 -> x0, matrix products: 14.5 us -> none  [the longest x4 10.3 us: block(): jnp.einsum('qhd,khd->hqk', queries, keys, preferred_element_type=jnp.floa...]
    reshape x13 -> x0, local copies, waits for them, and re-layouts: 12.7 us -> none  [the longest x4 6.27 us: block(): incoming.reshape(lon_devices * tokens_local, 3, heads_here, head_dim)]
    all_to_all x4 -> x0, local copies, waits for them, and re-layouts: 7.38 us -> none  [block(): incoming = lax.all_to_all(outgoing, 'lon', 0, 0, tiled=True)]
    all_to_all x1, waiting for transfers between devices: 2.11 us -> 5.68 us  [block(): incoming = lax.all_to_all(outgoing, 'lon', 0, 0, tiled=True)]
    unnamed x72 -> x24, local copies, waits for them, and re-layouts: 2.26 us -> 4.88 us
  transfers between devices with their start and end apart: 12 -> 12, of which waited for: 11 -> 12; matrix products, arithmetic and copies ran while one was open for 4% -> 3% of each run, Pallas kernels for 0% -> 0%
where the time goes in v1:
time: 248 us; the launch traced here: 246 us
  blocking collectives  102 us (41%)
  starting transfers between devices  61.5 us (25%)
  waiting for transfers between devices  25.1 us (10%)
  Pallas kernels  19 us (8%)
  matrix products  12.2 us (5%)
  local copies, waits for them, and re-layouts  11.9 us (5%)
  other arithmetic  9.76 us (4%)
  between operations  4.81 us (2%)
    all_to_all x4, blocking collectives, block(): returned = lax.all_to_all(back, 'lon', 0, 0, tiled=True)  55.4 us
    all_to_all x3, blocking collectives, block(): incoming = lax.all_to_all(outgoing, 'lon', 0, 0, tiled=True)  46.7 us
    ppermute x4, starting transfers between devices, lat_halo(): before = lax.ppermute(array[:, length - width:], 'lat', up)  31.5 us
    pallas_call x4, Pallas kernels, attend(): pl.pallas_call(functools.partial(attention_kernel, heads=heads, head_dim=...  19 us
    ppermute x4, starting transfers between devices, lat_halo(): after = lax.ppermute(array[:, :width], 'lat', down)  13.1 us
    ppermute x3, waiting for transfers between devices, from_partner(): lax.ppermute(array, 'segment', [(i, i ^ 1) for i in range(lax.axis_size('...  13 us
    all_to_all x1, starting transfers between devices, block(): incoming = lax.all_to_all(outgoing, 'lon', 0, 0, tiled=True)  10.2 us
    ppermute x3, starting transfers between devices, from_partner(): lax.ppermute(array, 'segment', [(i, i ^ 1) for i in range(lax.axis_size('...  6.64 us
  transfers between devices with their start and end apart: 12, of which 12 were waited for; matrix products, arithmetic and copies ran while one was open for 3% of the time, Pallas kernels for 0%

profile of v1, /device:TPU:1, one launch (start us, length us, event | category | flops | bytes accessed | tf_op | source)
XLA Modules:
  0.0 246.3 jit_solution(17517083227413098523)
XLA Ops:
  1.5 1.4 fusion.113
  6.5 1.3 gather_fusion
  15.6 10.2 %all-to-all-start = ((bf16[16,32,288]{2,1,0:T(8,128)(2,1)}), bf16[16,32,288]{2,1,0:T(8,128)(2,1)S(1)}, u32[]{:S(2)}, u32[]{:S(2)}) async-start(bf16[16,32,288]{2,1,0:T(8,128)(2,1)} %bitcast.6), calls=%async_computation | async-start | bytes 786432 | tf_op jit(solution)/shard_map/all_to_all | solution.py:96
  26.1 1.3 fusion
  27.4 1.6 convolution_add_fusion.1
  29.1 3.3 %convolution_add_fusion = f32[24,32768]{1,0:T(8,128)} fusion(f32[24,32768]{1,0:T(8,128)S(1)} %convolution_add_fusion.1, s32[32768]{0:T(1024)S(1)} %add_select_fusion, f32[1,12,8,64]{3,2,1,0:T(8,128)S(1)} %copy-done.5, s32[]{:T(128)S(6)} %select_n.49), kind=kOutput, calls=%fused_computation.1 | convolution fusion | flops 103557632 | bytes 6434820 | tf_op jit(solution)/shard_map/dot_general | solution.py:43
  32.4 5.7 %all-to-all-done = bf16[16,32,288]{2,1,0:T(8,128)(2,1)S(1)} async-done(((bf16[16,32,288]{2,1,0:T(8,128)(2,1)}), bf16[16,32,288]{2,1,0:T(8,128)(2,1)S(1)}, u32[]{:S(2)}, u32[]{:S(2)}) %all-to-all-start) | async-done | bytes 294944 | tf_op jit(solution)/shard_map/all_to_all | solution.py:96
  38.8 4.8 %shard_map.118 = bf16[512,96]{1,0:T(8,128)(2,1)} custom-call(bf16[512,288]{1,0:T(8,128)(2,1)} %bitcast.176, f32[3,512,512]{2,1,0:T(8,128)} %bitcast.163), custom_call_target="tpu_custom_call" | custom-call | tf_op jit(solution)/shard_map/pallas_call | solution.py:69
  43.6 15.5 %all_to_all.40 = bf16[16,32,96]{2,1,0:T(8,128)(2,1)S(1)} all-to-all(bf16[16,32,96]{2,1,0:T(8,128)(2,1)} %bitcast.185), channel_id=1, replica_groups=mesh['lon'=16,'lat'=16,'segment'=2] {'lon'}, dimensions={0} | all-to-all | bytes 196608 | tf_op jit(solution)/shard_map/all_to_all | solution.py:99
  59.8 4.3 %collective-permute-start.1 = (bf16[2,2,4,8,384]{4,3,1,0,2:T(8,128)(2,1)S(1)}, bf16[2,2,4,8,384]{4,3,1,0,2:T(8,128)(2,1)S(1)}, u32[]{:S(2)}, u32[]{:S(2)}) collective-permute-start(bf16[2,2,4,8,384]{4,3,1,0,2:T(8,128)(2,1)S(1)} %multiply_convert_fusion.10), channel_id=1, source_target_pairs={{2,0},{4,2},{6,4},{8,6},{10,8},{12,10},{14,12},{16,14},{18,16},{20... | collective-permute-start | bytes 294920 | tf_op jit(solution)/shard_map/ppermute | solution.py:25
  64.1 3.9 %collective-permute-start = (bf16[2,2,4,8,384]{4,3,1,0,2:T(8,128)(2,1)S(1)}, bf16[2,2,4,8,384]{4,3,1,0,2:T(8,128)(2,1)S(1)}, u32[]{:S(2)}, u32[]{:S(2)}) collective-permute-start(bf16[2,2,4,8,384]{4,3,1,0,2:T(8,128)(2,1)S(1)} %multiply_convert_fusion.10), channel_id=1, source_target_pairs={{0,2},{2,4},{4,6},{6,8},{8,10},{10,12},{12,14},{14,16},{16,18},{18... | collective-permute-start | bytes 294920 | tf_op jit(solution)/shard_map/ppermute | solution.py:24
  71.8 2.2 collective-permute-start.2
  74.1 4.6 %collective-permute-done.2 = f32[2,2,4,8,384]{4,3,1,0,2:T(8,128)S(1)} collective-permute-done((f32[2,2,4,8,384]{4,3,1,0,2:T(8,128)S(1)}, f32[2,2,4,8,384]{4,3,1,0,2:T(8,128)S(1)}, u32[]{:S(2)}, u32[]{:S(2)}) %collective-permute-start.2) | collective-permute-done | bytes 196640 | tf_op jit(solution)/shard_map/ppermute | solution.py:120
  79.7 17.3 %all_to_all.41 = bf16[16,32,288]{2,1,0:T(8,128)(2,1)} all-to-all(bf16[16,32,288]{2,1,0:T(8,128)(2,1)S(1)} %bitcast.180), channel_id=1, replica_groups=mesh['lon'=16,'lat'=16,'segment'=2] {'lon'}, dimensions={0} | all-to-all | bytes 589824 | tf_op jit(solution)/shard_map/all_to_all | solution.py:96
  97.0 4.7 %shard_map.119 = bf16[512,96]{1,0:T(8,128)(2,1)} custom-call(bf16[512,288]{1,0:T(8,128)(2,1)} %bitcast.178, f32[3,512,512]{2,1,0:T(8,128)} %bitcast.164), custom_call_target="tpu_custom_call" | custom-call | tf_op jit(solution)/shard_map/pallas_call | solution.py:69
  101.8 13.4 %all_to_all.42 = bf16[16,32,96]{2,1,0:T(8,128)(2,1)S(1)} all-to-all(bf16[16,32,96]{2,1,0:T(8,128)(2,1)} %bitcast.187), channel_id=1, replica_groups=mesh['lon'=16,'lat'=16,'segment'=2] {'lon'}, dimensions={0} | all-to-all | bytes 196608 | tf_op jit(solution)/shard_map/all_to_all | solution.py:99
  115.9 3.9 %collective-permute-start.4 = (bf16[2,2,4,8,384]{4,3,1,0,2:T(8,128)(2,1)S(1)}, bf16[2,2,4,8,384]{4,3,1,0,2:T(8,128)(2,1)S(1)}, u32[]{:S(2)}, u32[]{:S(2)}) collective-permute-start(bf16[2,2,4,8,384]{4,3,1,0,2:T(8,128)(2,1)S(1)} %multiply_convert_fusion.7), channel_id=1, source_target_pairs={{2,0},{4,2},{6,4},{8,6},{10,8},{12,10},{14,12},{16,14},{18,16},{20... | collective-permute-start | bytes 294920 | tf_op jit(solution)/shard_map/ppermute | solution.py:25
  119.8 5.6 %collective-permute-start.3 = (bf16[2,2,4,8,384]{4,3,1,0,2:T(8,128)(2,1)S(1)}, bf16[2,2,4,8,384]{4,3,1,0,2:T(8,128)(2,1)S(1)}, u32[]{:S(2)}, u32[]{:S(2)}) collective-permute-start(bf16[2,2,4,8,384]{4,3,1,0,2:T(8,128)(2,1)S(1)} %multiply_convert_fusion.7), channel_id=1, source_target_pairs={{0,2},{2,4},{4,6},{6,8},{8,10},{10,12},{12,14},{14,16},{16,18},{18... | collective-permute-start | bytes 294920 | tf_op jit(solution)/shard_map/ppermute | solution.py:24
  129.2 2.2 collective-permute-start.5
  131.4 4.2 %collective-permute-done.5 = f32[2,2,4,8,384]{4,3,1,0,2:T(8,128)S(1)} collective-permute-done((f32[2,2,4,8,384]{4,3,1,0,2:T(8,128)S(1)}, f32[2,2,4,8,384]{4,3,1,0,2:T(8,128)S(1)}, u32[]{:S(2)}, u32[]{:S(2)}) %collective-permute-start.5) | collective-permute-done | bytes 196640 | tf_op jit(solution)/shard_map/ppermute | solution.py:120
  136.7 15.4 %all_to_all.43 = bf16[16,32,288]{2,1,0:T(8,128)(2,1)} all-to-all(bf16[16,32,288]{2,1,0:T(8,128)(2,1)S(1)} %bitcast.181), channel_id=1, replica_groups=mesh['lon'=16,'lat'=16,'segment'=2] {'lon'}, dimensions={0} | all-to-all | bytes 589824 | tf_op jit(solution)/shard_map/all_to_all | solution.py:96
  152.1 4.7 %shard_map.120 = bf16[512,96]{1,0:T(8,128)(2,1)} custom-call(bf16[512,288]{1,0:T(8,128)(2,1)} %bitcast.179, f32[3,512,512]{2,1,0:T(8,128)} %bitcast.165), custom_call_target="tpu_custom_call" | custom-call | tf_op jit(solution)/shard_map/pallas_call | solution.py:69
  156.8 13.6 %all_to_all.44 = bf16[16,32,96]{2,1,0:T(8,128)(2,1)S(1)} all-to-all(bf16[16,32,96]{2,1,0:T(8,128)(2,1)} %bitcast.189), channel_id=1, replica_groups=mesh['lon'=16,'lat'=16,'segment'=2] {'lon'}, dimensions={0} | all-to-all | bytes 196608 | tf_op jit(solution)/shard_map/all_to_all | solution.py:99
  171.1 3.1 %collective-permute-start.7 = (bf16[2,2,4,8,384]{4,3,1,0,2:T(8,128)(2,1)S(1)}, bf16[2,2,4,8,384]{4,3,1,0,2:T(8,128)(2,1)S(1)}, u32[]{:S(2)}, u32[]{:S(2)}) collective-permute-start(bf16[2,2,4,8,384]{4,3,1,0,2:T(8,128)(2,1)S(1)} %multiply_convert_fusion.4), channel_id=1, source_target_pairs={{2,0},{4,2},{6,4},{8,6},{10,8},{12,10},{14,12},{16,14},{18,16},{20... | collective-permute-start | bytes 294920 | tf_op jit(solution)/shard_map/ppermute | solution.py:25
  174.2 8.6 %collective-permute-start.6 = (bf16[2,2,4,8,384]{4,3,1,0,2:T(8,128)(2,1)S(1)}, bf16[2,2,4,8,384]{4,3,1,0,2:T(8,128)(2,1)S(1)}, u32[]{:S(2)}, u32[]{:S(2)}) collective-permute-start(bf16[2,2,4,8,384]{4,3,1,0,2:T(8,128)(2,1)S(1)} %multiply_convert_fusion.4), channel_id=1, source_target_pairs={{0,2},{2,4},{4,6},{6,8},{8,10},{10,12},{12,14},{14,16},{16,18},{18... | collective-permute-start | bytes 294920 | tf_op jit(solution)/shard_map/ppermute | solution.py:24
  186.6 2.2 collective-permute-start.8
  188.8 4.2 %collective-permute-done.8 = f32[2,2,4,8,384]{4,3,1,0,2:T(8,128)S(1)} collective-permute-done((f32[2,2,4,8,384]{4,3,1,0,2:T(8,128)S(1)}, f32[2,2,4,8,384]{4,3,1,0,2:T(8,128)S(1)}, u32[]{:S(2)}, u32[]{:S(2)}) %collective-permute-start.8) | collective-permute-done | bytes 196640 | tf_op jit(solution)/shard_map/ppermute | solution.py:120
  194.1 14.0 %all_to_all.45 = bf16[16,32,288]{2,1,0:T(8,128)(2,1)} all-to-all(bf16[16,32,288]{2,1,0:T(8,128)(2,1)S(1)} %bitcast.182), channel_id=1, replica_groups=mesh['lon'=16,'lat'=16,'segment'=2] {'lon'}, dimensions={0} | all-to-all | bytes 589824 | tf_op jit(solution)/shard_map/all_to_all | solution.py:96
  208.0 4.7 %shard_map.121 = bf16[512,96]{1,0:T(8,128)(2,1)} custom-call(bf16[512,288]{1,0:T(8,128)(2,1)} %bitcast.177, f32[3,512,512]{2,1,0:T(8,128)} %bitcast.166), custom_call_target="tpu_custom_call" | custom-call | tf_op jit(solution)/shard_map/pallas_call | solution.py:69
  212.8 12.9 %all_to_all.46 = bf16[16,32,96]{2,1,0:T(8,128)(2,1)S(1)} all-to-all(bf16[16,32,96]{2,1,0:T(8,128)(2,1)} %bitcast.184), channel_id=1, replica_groups=mesh['lon'=16,'lat'=16,'segment'=2] {'lon'}, dimensions={0} | all-to-all | bytes 196608 | tf_op jit(solution)/shard_map/all_to_all | solution.py:99
  226.4 1.9 collective-permute-start.10
  228.4 13.4 %collective-permute-start.9 = (bf16[2,2,4,8,384]{4,3,1,0,2:T(8,128)(2,1)S(1)}, bf16[2,2,4,8,384]{4,3,1,0,2:T(8,128)(2,1)S(1)}, u32[]{:S(2)}, u32[]{:S(2)}) collective-permute-start(bf16[2,2,4,8,384]{4,3,1,0,2:T(8,128)(2,1)S(1)} %multiply_convert_fusion.1), channel_id=1, source_target_pairs={{0,2},{2,4},{4,6},{6,8},{8,10},{10,12},{12,14},{14,16},{16,18},{18... | collective-permute-start | bytes 294920 | tf_op jit(solution)/shard_map/ppermute | solution.py:24
  (136 shorter events, 31.3 us)
Async XLA Ops:
  0.0 70.2 %copy-start = (bf16[1,384,1536]{2,1,0:T(8,128)(2,1)S(1)}, bf16[1,384,1536]{2,1,0:T(8,128)(2,1)}, u32[]{:S(2)}) copy-start(bf16[1,384,1536]{2,1,0:T(8,128)(2,1)} %param.21) | copy-start | bytes 3538948
  0.0 13.3 %copy-start.4 = (bf16[1,384,1152]{2,1,0:T(8,128)(2,1)S(1)}, bf16[1,384,1152]{2,1,0:T(8,128)(2,1)}, u32[]{:S(2)}) copy-start(bf16[1,384,1152]{2,1,0:T(8,128)(2,1)} %param.19) | copy-start | bytes 2654212
  14.7 11.4 %copy-start.5 = (f32[1,12,8,64]{3,2,1,0:T(8,128)S(1)}, f32[1,12,8,64]{3,2,1,0:T(8,128)}, u32[]{:S(2)}) copy-start(f32[1,12,8,64]{3,2,1,0:T(8,128)} %param.25) | copy-start | bytes 73732
  15.6 22.5 %all-to-all-start = ((bf16[16,32,288]{2,1,0:T(8,128)(2,1)}), bf16[16,32,288]{2,1,0:T(8,128)(2,1)S(1)}, u32[]{:S(2)}, u32[]{:S(2)}) async-start(bf16[16,32,288]{2,1,0:T(8,128)(2,1)} %bitcast.6), calls=%async_computation | async-start | bytes 786432 | tf_op jit(solution)/shard_map/all_to_all | solution.py:96
  38.1 0.7 copy-start.3
  38.8 20.3 %copy-start.1 = (bf16[1,384,384]{2,1,0:T(8,128)(2,1)S(1)}, bf16[1,384,384]{2,1,0:T(8,128)(2,1)}, u32[]{:S(2)}) copy-start(bf16[1,384,384]{2,1,0:T(8,128)(2,1)} %param.20) | copy-start | bytes 884740
  38.8 20.6 %copy-start.2 = (f32[2,2,4,8,384]{4,3,2,1,0:T(8,128)S(1)}, f32[2,2,4,8,384]{4,3,2,1,0:T(8,128)}, u32[]{:S(2)}) copy-start(f32[2,2,4,8,384]{4,3,2,1,0:T(8,128)} %param.14) | copy-start | bytes 589828
  43.6 24.4 %copy-start.6 = (f32[1,5,384]{2,0,1:T(1,128)S(1)}, f32[1,5,384]{2,0,1:T(1,128)}, u32[]{:S(2)}) copy-start(f32[1,5,384]{2,0,1:T(1,128)} %param.24) | copy-start | bytes 23044
  59.8 8.5 %collective-permute-start.1 = (bf16[2,2,4,8,384]{4,3,1,0,2:T(8,128)(2,1)S(1)}, bf16[2,2,4,8,384]{4,3,1,0,2:T(8,128)(2,1)S(1)}, u32[]{:S(2)}, u32[]{:S(2)}) collective-permute-start(bf16[2,2,4,8,384]{4,3,1,0,2:T(8,128)(2,1)S(1)} %multiply_convert_fusion.10), channel_id=1, source_target_pairs={{2,0},{4,2},{6,4},{8,6},{10,8},{12,10},{14,12},{16,14},{18,16},{20... | collective-permute-start | bytes 294920 | tf_op jit(solution)/shard_map/ppermute | solution.py:25
  64.1 5.5 %collective-permute-start = (bf16[2,2,4,8,384]{4,3,1,0,2:T(8,128)(2,1)S(1)}, bf16[2,2,4,8,384]{4,3,1,0,2:T(8,128)(2,1)S(1)}, u32[]{:S(2)}, u32[]{:S(2)}) collective-permute-start(bf16[2,2,4,8,384]{4,3,1,0,2:T(8,128)(2,1)S(1)} %multiply_convert_fusion.10), channel_id=1, source_target_pairs={{0,2},{2,4},{4,6},{6,8},{8,10},{10,12},{12,14},{14,16},{16,18},{18... | collective-permute-start | bytes 294920 | tf_op jit(solution)/shard_map/ppermute | solution.py:24
  70.2 1.3 copy-start.7
  71.8 6.8 %collective-permute-start.2 = (f32[2,2,4,8,384]{4,3,1,0,2:T(8,128)S(1)}, f32[2,2,4,8,384]{4,3,1,0,2:T(8,128)S(1)}, u32[]{:S(2)}, u32[]{:S(2)}) collective-permute-start(f32[2,2,4,8,384]{4,3,1,0,2:T(8,128)S(1)} %fusion.20), channel_id=1, source_target_pairs={{0,1},{1,0},{2,3},{3,2},{4,5},{5,4},{6,7},{7,6},{8,9},{9,8},{10,11... | collective-permute-start | bytes 589832 | tf_op jit(solution)/shard_map/ppermute | solution.py:120
  115.9 9.9 %collective-permute-start.4 = (bf16[2,2,4,8,384]{4,3,1,0,2:T(8,128)(2,1)S(1)}, bf16[2,2,4,8,384]{4,3,1,0,2:T(8,128)(2,1)S(1)}, u32[]{:S(2)}, u32[]{:S(2)}) collective-permute-start(bf16[2,2,4,8,384]{4,3,1,0,2:T(8,128)(2,1)S(1)} %multiply_convert_fusion.7), channel_id=1, source_target_pairs={{2,0},{4,2},{6,4},{8,6},{10,8},{12,10},{14,12},{16,14},{18,16},{20... | collective-permute-start | bytes 294920 | tf_op jit(solution)/shard_map/ppermute | solution.py:25
  119.8 7.2 %collective-permute-start.3 = (bf16[2,2,4,8,384]{4,3,1,0,2:T(8,128)(2,1)S(1)}, bf16[2,2,4,8,384]{4,3,1,0,2:T(8,128)(2,1)S(1)}, u32[]{:S(2)}, u32[]{:S(2)}) collective-permute-start(bf16[2,2,4,8,384]{4,3,1,0,2:T(8,128)(2,1)S(1)} %multiply_convert_fusion.7), channel_id=1, source_target_pairs={{0,2},{2,4},{4,6},{6,8},{8,10},{10,12},{12,14},{14,16},{16,18},{18... | collective-permute-start | bytes 294920 | tf_op jit(solution)/shard_map/ppermute | solution.py:24
  127.5 1.3 copy-start.8
  129.2 6.4 %collective-permute-start.5 = (f32[2,2,4,8,384]{4,3,1,0,2:T(8,128)S(1)}, f32[2,2,4,8,384]{4,3,1,0,2:T(8,128)S(1)}, u32[]{:S(2)}, u32[]{:S(2)}) collective-permute-start(f32[2,2,4,8,384]{4,3,1,0,2:T(8,128)S(1)} %fusion.23), channel_id=1, source_target_pairs={{0,1},{1,0},{2,3},{3,2},{4,5},{5,4},{6,7},{7,6},{8,9},{9,8},{10,11... | collective-permute-start | bytes 589832 | tf_op jit(solution)/shard_map/ppermute | solution.py:120
  171.1 12.0 %collective-permute-start.7 = (bf16[2,2,4,8,384]{4,3,1,0,2:T(8,128)(2,1)S(1)}, bf16[2,2,4,8,384]{4,3,1,0,2:T(8,128)(2,1)S(1)}, u32[]{:S(2)}, u32[]{:S(2)}) collective-permute-start(bf16[2,2,4,8,384]{4,3,1,0,2:T(8,128)(2,1)S(1)} %multiply_convert_fusion.4), channel_id=1, source_target_pairs={{2,0},{4,2},{6,4},{8,6},{10,8},{12,10},{14,12},{16,14},{18,16},{20... | collective-permute-start | bytes 294920 | tf_op jit(solution)/shard_map/ppermute | solution.py:25
  174.2 10.2 %collective-permute-start.6 = (bf16[2,2,4,8,384]{4,3,1,0,2:T(8,128)(2,1)S(1)}, bf16[2,2,4,8,384]{4,3,1,0,2:T(8,128)(2,1)S(1)}, u32[]{:S(2)}, u32[]{:S(2)}) collective-permute-start(bf16[2,2,4,8,384]{4,3,1,0,2:T(8,128)(2,1)S(1)} %multiply_convert_fusion.4), channel_id=1, source_target_pairs={{0,2},{2,4},{4,6},{6,8},{8,10},{10,12},{12,14},{14,16},{16,18},{18... | collective-permute-start | bytes 294920 | tf_op jit(solution)/shard_map/ppermute | solution.py:24
  184.9 1.3 copy-start.9
  186.6 6.4 %collective-permute-start.8 = (f32[2,2,4,8,384]{4,3,1,0,2:T(8,128)S(1)}, f32[2,2,4,8,384]{4,3,1,0,2:T(8,128)S(1)}, u32[]{:S(2)}, u32[]{:S(2)}) collective-permute-start(f32[2,2,4,8,384]{4,3,1,0,2:T(8,128)S(1)} %fusion.26), channel_id=1, source_target_pairs={{0,1},{1,0},{2,3},{3,2},{4,5},{5,4},{6,7},{7,6},{8,9},{9,8},{10,11... | collective-permute-start | bytes 589832 | tf_op jit(solution)/shard_map/ppermute | solution.py:120
  226.4 15.7 %collective-permute-start.10 = (bf16[2,2,4,8,384]{4,3,1,0,2:T(8,128)(2,1)S(1)}, bf16[2,2,4,8,384]{4,3,1,0,2:T(8,128)(2,1)S(1)}, u32[]{:S(2)}, u32[]{:S(2)}) collective-permute-start(bf16[2,2,4,8,384]{4,3,1,0,2:T(8,128)(2,1)S(1)} %multiply_convert_fusion.1), channel_id=1, source_target_pairs={{2,0},{4,2},{6,4},{8,6},{10,8},{12,10},{14,12},{16,14},{18,16},{20... | collective-permute-start | bytes 294920 | tf_op jit(solution)/shard_map/ppermute | solution.py:25
  228.4 15.1 %collective-permute-start.9 = (bf16[2,2,4,8,384]{4,3,1,0,2:T(8,128)(2,1)S(1)}, bf16[2,2,4,8,384]{4,3,1,0,2:T(8,128)(2,1)S(1)}, u32[]{:S(2)}, u32[]{:S(2)}) collective-permute-start(bf16[2,2,4,8,384]{4,3,1,0,2:T(8,128)(2,1)S(1)} %multiply_convert_fusion.1), channel_id=1, source_target_pairs={{0,2},{2,4},{4,6},{6,8},{8,10},{10,12},{12,14},{14,16},{16,18},{18... | collective-permute-start | bytes 294920 | tf_op jit(solution)/shard_map/ppermute | solution.py:24
  244.0 1.3 copy-start.10

commit v2 on v1

--- a/solution.py
+++ b/solution.py
@@ -120,6 +120,18 @@
     return lax.ppermute(array, "segment", [(i, i ^ 1) for i in range(lax.axis_size("segment"))])
 
 
+def fetch_split(array):
+    lat_devices = lax.axis_size("lat")
+    core = lax.axis_index("lat") % 2
+    half = array.shape[0] // 2
+    mine = lax.dynamic_slice_in_dim(array, core * half, half, axis=0)
+    got = from_partner(mine)
+    neighbour = lax.ppermute(got, "lat", [(i, i ^ 1) for i in range(lat_devices)])
+    low = jnp.where(core == 0, got, neighbour)
+    high = jnp.where(core == 0, neighbour, got)
+    return jnp.concatenate([low, high], axis=0)
+
+
 def body(
     initial_state,
     mask_ids,
@@ -139,28 +151,34 @@
     lon_devices = lax.axis_size("lon")
     head_count = score_bias.shape[1]
     groups = lon_devices // (members * rows_lat)
-    mask_tab, lead_tab, wqkv, wout, wup, wdown, gains, taps = tuple(
+    own_raw = tuple(
         item[0] for item in (mask_table, lead_table, w_qkv, w_out, w_up, w_down, norm_gains, merid_taps)
     )
-    features = wqkv.shape[0]
-    head_dim = features // head_count
-    heads_here = head_count // groups
-    wqkv = jnp.transpose(wqkv.reshape(features, 3, groups, heads_here * head_dim), (2, 0, 1, 3))
-    wqkv = wqkv.reshape(groups, features, 3 * heads_here * head_dim)
-    wout = wout.reshape(groups, heads_here * head_dim, features)
-    params = (mask_tab, lead_tab, wqkv, wout, wup, wdown, gains, taps)
-    bias_full = head_bias(score_bias[0], groups, lon_local * lon_devices, initial_state.shape[3])
+    other_raw = tuple(
+        fetch_split(item) if item.dtype == jnp.bfloat16 else from_partner(item) for item in own_raw
+    )
+    other_bias = from_partner(score_bias[0])
+    levels = initial_state.shape[3]
+
+    def prepare(raw, bias_segment):
+        mask_tab, lead_tab, wqkv, wout, wup, wdown, gains, taps = raw
+        features = wqkv.shape[0]
+        head_dim = features // head_count
+        heads_here = head_count // groups
+        wqkv = jnp.transpose(wqkv.reshape(features, 3, groups, heads_here * head_dim), (2, 0, 1, 3))
+        wqkv = wqkv.reshape(groups, features, 3 * heads_here * head_dim)
+        wout = wout.reshape(groups, heads_here * head_dim, features)
+        params = (mask_tab, lead_tab, wqkv, wout, wup, wdown, gains, taps)
+        return params, head_bias(bias_segment, groups, lon_local * lon_devices, levels)
+
+    own = prepare(own_raw, score_bias[0])
+    other = prepare(other_raw, other_bias)
     segment_first = lax.axis_index("segment") == 0
-    current = initial_state
-    first = None
-    for tick_num in range(4):
-        result = block(current, lead_steps[tick_num // 2], mask_ids, params, bias_full)
-        if tick_num == 3:
-            break
-        current = from_partner(result)
-        if tick_num == 1:
-            first = current
-    output = jnp.where(segment_first, first, result)
+    out0 = block(initial_state, lead_steps[0], mask_ids, *own)
+    first = block(out0, lead_steps[0], mask_ids, *other)
+    out2 = block(from_partner(first), lead_steps[1], mask_ids, *other)
+    second = block(out2, lead_steps[1], mask_ids, *own)
+    output = jnp.where(segment_first, first, second)
     return output[None]
 
 

time: 248 us -> 294 us (1.19)
  blocking collectives: 102 us -> 60.2 us
  starting transfers between devices: 61.5 us -> 102 us
  matrix products: 12.2 us -> 34.5 us
  local copies, waits for them, and re-layouts: 11.9 us -> 27.8 us
  other arithmetic: 9.76 us -> 20.4 us
    all_to_all x4 -> x2, blocking collectives: 55.4 us -> 28.5 us  [block(): returned = lax.all_to_all(back, 'lon', 0, 0, tiled=True)]
    ppermute x3 -> x10, starting transfers between devices: 6.64 us -> 26.6 us  [from_partner(): lax.ppermute(array, 'segment', [(i, i ^ 1) for i in range(lax.axis_size('...]
    all_to_all x0 -> x2, starting transfers between devices: none -> 15.9 us  [block(): returned = lax.all_to_all(back, 'lon', 0, 0, tiled=True)]
    all_to_all x3 -> x2, blocking collectives: 46.7 us -> 31.7 us  [block(): incoming = lax.all_to_all(outgoing, 'lon', 0, 0, tiled=True)]
    dot_general x3 -> x6, matrix products: 6.29 us -> 20.8 us  [head_bias(): jnp.dot(part, onehot, preferred_element_type=jnp.float32)]
    all_to_all x0 -> x2, waiting for transfers between devices: none -> 12 us  [block(): returned = lax.all_to_all(back, 'lon', 0, 0, tiled=True)]
    ppermute x4, starting transfers between devices: 31.5 us -> 21.1 us  [lat_halo(): before = lax.ppermute(array[:, length - width:], 'lat', up)]
    ppermute x0 -> x4, starting transfers between devices: none -> 8.91 us  [fetch_split(): lax.ppermute(got, 'lat', [(i, i ^ 1) for i in range(lat_devices)])]
  transfers between devices with their start and end apart: 12 -> 26, of which waited for: 12 -> 9; matrix products, arithmetic and copies ran while one was open for 3% -> 22% of each run, Pallas kernels for 0% -> 3%
where the time goes in v2:
time: 294 us; the launch traced here: 292 us
  starting transfers between devices  102 us (35%)
  blocking collectives  60.2 us (20%)
  matrix products  34.5 us (12%)
  local copies, waits for them, and re-layouts  27.8 us (9%)
  waiting for transfers between devices  22.7 us (8%)
  other arithmetic  20.4 us (7%)
  Pallas kernels  19 us (6%)
  between operations  4.62 us (2%)
    all_to_all x2, blocking collectives, block(): incoming = lax.all_to_all(outgoing, 'lon', 0, 0, tiled=True)  31.7 us
    all_to_all x2, blocking collectives, block(): returned = lax.all_to_all(back, 'lon', 0, 0, tiled=True)  28.5 us
    ppermute x10, starting transfers between devices, from_partner(): lax.ppermute(array, 'segment', [(i, i ^ 1) for i in range(lax.axis_size('...  26.6 us
    ppermute x4, starting transfers between devices, lat_halo(): before = lax.ppermute(array[:, length - width:], 'lat', up)  21.1 us
    dot_general x6, matrix products, head_bias(): jnp.dot(part, onehot, preferred_element_type=jnp.float32)  20.8 us
    pallas_call x4, Pallas kernels, attend(): pl.pallas_call(functools.partial(attention_kernel, heads=heads, head_dim=...  19 us
    ppermute x4, starting transfers between devices, lat_halo(): after = lax.ppermute(array[:, :width], 'lat', down)  16.5 us
    all_to_all x2, starting transfers between devices, block(): returned = lax.all_to_all(back, 'lon', 0, 0, tiled=True)  15.9 us
  transfers between devices with their start and end apart: 26, of which 9 were waited for; matrix products, arithmetic and copies ran while one was open for 22% of the time, Pallas kernels for 3%

profile of v2, /device:TPU:1, one launch (start us, length us, event | category | flops | bytes accessed | tf_op | source)
XLA Modules:
  0.0 291.5 jit_solution(9317223965586960536)
XLA Ops:
  1.4 3.9 %collective-permute-start.4 = (f32[3,384]{1,0:T(4,128)}, f32[3,384]{1,0:T(4,128)}, u32[]{:S(2)}, u32[]{:S(2)}) collective-permute-start(f32[3,384]{1,0:T(4,128)} %bitcast.195), channel_id=1, source_target_pairs={{0,1},{1,0},{2,3},{3,2},{4,5},{5,4},{6,7},{7,6},{8,9},{9,8},{10,11... | collective-permute-start | bytes 13832 | tf_op jit(solution)/shard_map/ppermute | solution.py:120
  7.9 3.4 %collective-permute-start.2 = (f32[8,384]{1,0:T(8,128)}, f32[8,384]{1,0:T(8,128)S(1)}, u32[]{:S(2)}, u32[]{:S(2)}) collective-permute-start(f32[8,384]{1,0:T(8,128)} %bitcast.217), channel_id=1, source_target_pairs={{0,1},{1,0},{2,3},{3,2},{4,5},{5,4},{6,7},{7,6},{8,9},{9,8},{10,11... | collective-permute-start | bytes 36872 | tf_op jit(solution)/shard_map/ppermute | solution.py:120
  13.2 3.4 %collective-permute-start.7 = (f32[12,8,64]{2,1,0:T(8,128)}, f32[12,8,64]{2,1,0:T(8,128)}, u32[]{:S(2)}, u32[]{:S(2)}) collective-permute-start(f32[12,8,64]{2,1,0:T(8,128)} %bitcast.239), channel_id=1, source_target_pairs={{0,1},{1,0},{2,3},{3,2},{4,5},{5,4},{6,7},{7,6},{8,9},{9,8},{10,11... | collective-permute-start | bytes 73736 | tf_op jit(solution)/shard_map/ppermute | solution.py:120
  27.5 3.3 %convolution_add_fusion.1 = f32[24,32768]{1,0:T(8,128)} fusion(f32[24,32768]{1,0:T(8,128)S(1)} %convolution_add_fusion.2, s32[32768]{0:T(1024)S(1)} %add_select_fusion, f32[1,12,8,64]{3,2,1,0:T(8,128)S(1)} %copy-done.12, s32[]{:T(128)S(6)} %select_n.127), kind=kOutput, calls=%fused_computation.4 | convolution fusion | flops 103557632 | bytes 6434820 | tf_op jit(solution)/shard_map/dot_general | solution.py:43
  48.8 9.7 %all-to-all-start = ((bf16[16,32,288]{2,1,0:T(8,128)(2,1)}), bf16[16,32,288]{2,1,0:T(8,128)(2,1)}, u32[]{:S(2)}, u32[]{:S(2)}) async-start(bf16[16,32,288]{2,1,0:T(8,128)(2,1)} %bitcast.213), calls=%async_computation | async-start | bytes 786432 | tf_op jit(solution)/shard_map/all_to_all | solution.py:96
  63.0 3.1 %collective-permute-start.13 = (bf16[192,1536]{1,0:T(8,128)(2,1)}, bf16[192,1536]{1,0:T(8,128)(2,1)}, u32[]{:S(2)}, u32[]{:S(2)}) collective-permute-start(bf16[192,1536]{1,0:T(8,128)(2,1)} %dynamic-slice_bitcast_fusion.1), channel_id=1, source_target_pairs={{0,1},{1,0},{2,3},{3,2},{4,5},{5,4},{6,7},{7,6},{8,9},{9,8},{10,11... | collective-permute-start | bytes 1769480 | tf_op jit(solution)/shard_map/ppermute | solution.py:120
  69.3 4.7 %shard_map.118 = bf16[512,96]{1,0:T(8,128)(2,1)} custom-call(bf16[512,288]{1,0:T(8,128)(2,1)} %bitcast.7.x_ref, f32[3,512,512]{2,1,0:T(8,128)} %bitcast.196), custom_call_target="tpu_custom_call" | custom-call | tf_op jit(solution)/shard_map/pallas_call | solution.py:69
  74.1 8.2 %all-to-all-start.1 = ((bf16[16,32,96]{2,1,0:T(8,128)(2,1)}), bf16[16,32,96]{2,1,0:T(8,128)(2,1)}, u32[]{:S(2)}, u32[]{:S(2)}) async-start(bf16[16,32,96]{2,1,0:T(8,128)(2,1)} %bitcast.221), calls=%async_computation.1 | async-start | bytes 262144 | tf_op jit(solution)/shard_map/all_to_all | solution.py:99
  82.3 3.8 %fusion.1 = f32[24,32768]{1,0:T(8,128)} fusion(s32[32768]{0:T(1024)S(1)} %add_select_fusion, f32[12,8,64]{2,1,0:T(8,128)} %collective-permute-done.7, s32[]{:T(128)S(6)} %select_n.127), kind=kOutput, calls=%fused_computation.7 | convolution fusion | flops 102771200 | bytes 3289092 | tf_op jit(solution)/shard_map/dot_general | solution.py:43
  86.0 5.3 %all-to-all-done.1 = bf16[16,32,96]{2,1,0:T(8,128)(2,1)} async-done(((bf16[16,32,96]{2,1,0:T(8,128)(2,1)}), bf16[16,32,96]{2,1,0:T(8,128)(2,1)}, u32[]{:S(2)}, u32[]{:S(2)}) %all-to-all-start.1) | async-done | bytes 98336 | tf_op jit(solution)/shard_map/all_to_all | solution.py:99
  94.5 6.7 %collective-permute-start.1 = (bf16[2,2,4,8,384]{4,3,2,1,0:T(8,128)(2,1)S(1)}, bf16[2,2,4,8,384]{4,3,2,1,0:T(8,128)(2,1)}, u32[]{:S(2)}, u32[]{:S(2)}) collective-permute-start(bf16[2,2,4,8,384]{4,3,2,1,0:T(8,128)(2,1)S(1)} %multiply_convert_fusion.10), channel_id=1, source_target_pairs={{2,0},{4,2},{6,4},{8,6},{10,8},{12,10},{14,12},{16,14},{18,16},{20... | collective-permute-start | bytes 294920 | tf_op jit(solution)/shard_map/ppermute | solution.py:25
  101.2 4.1 %collective-permute-start = (bf16[2,2,4,8,384]{4,3,2,1,0:T(8,128)(2,1)S(1)}, bf16[2,2,4,8,384]{4,3,2,1,0:T(8,128)(2,1)}, u32[]{:S(2)}, u32[]{:S(2)}) collective-permute-start(bf16[2,2,4,8,384]{4,3,2,1,0:T(8,128)(2,1)S(1)} %multiply_convert_fusion.10), channel_id=1, source_target_pairs={{0,2},{2,4},{4,6},{6,8},{8,10},{10,12},{12,14},{14,16},{16,18},{18... | collective-permute-start | bytes 294920 | tf_op jit(solution)/shard_map/ppermute | solution.py:24
  105.3 3.8 %fusion.2 = f32[24,32768]{1,0:T(8,128)} fusion(s32[32768]{0:T(1024)S(1)} %add_select_fusion, f32[12,8,64]{2,1,0:T(8,128)} %collective-permute-done.7, s32[]{:T(128)S(6)} %select_n.127), kind=kOutput, calls=%fused_computation.8 | convolution fusion | flops 102766592 | bytes 3289092 | tf_op jit(solution)/shard_map/dot_general | solution.py:43
  127.1 3.6 %all-to-all-start.2 = ((bf16[16,32,288]{2,1,0:T(8,128)(2,1)}), bf16[16,32,288]{2,1,0:T(8,128)(2,1)S(1)}, u32[]{:S(2)}, u32[]{:S(2)}) async-start(bf16[16,32,288]{2,1,0:T(8,128)(2,1)} %bitcast.214), calls=%async_computation.2 | async-start | bytes 786432 | tf_op jit(solution)/shard_map/all_to_all | solution.py:96
  130.7 6.3 %fusion = f32[24,32768]{1,0:T(8,128)} fusion(f32[24,32768]{1,0:T(8,128)} %fusion.1, f32[24,32768]{1,0:T(8,128)} %fusion.2, s32[32768]{0:T(1024)S(1)} %add_select_fusion, f32[12,8,64]{2,1,0:T(8,128)} %collective-permute-done.7, s32[]{:T(128)S(6)} %select_n.127), kind=kOutput, calls=%fused_computation.3 | convolution fusion | flops 104333312 | bytes 9574404 | tf_op jit(solution)/shard_map/dot_general | solution.py:43
  143.9 4.7 %shard_map.119 = bf16[512,96]{1,0:T(8,128)(2,1)} custom-call(bf16[512,288]{1,0:T(8,128)(2,1)} %bitcast.210, f32[3,512,512]{2,1,0:T(8,128)} %bitcast.198), custom_call_target="tpu_custom_call" | custom-call | tf_op jit(solution)/shard_map/pallas_call | solution.py:69
  148.7 7.7 %all-to-all-start.3 = ((bf16[16,32,96]{2,1,0:T(8,128)(2,1)}), bf16[16,32,96]{2,1,0:T(8,128)(2,1)S(1)}, u32[]{:S(2)}, u32[]{:S(2)}) async-start(bf16[16,32,96]{2,1,0:T(8,128)(2,1)} %bitcast.220), calls=%async_computation.3 | async-start | bytes 262144 | tf_op jit(solution)/shard_map/all_to_all | solution.py:99
  158.8 6.7 %all-to-all-done.3 = bf16[16,32,96]{2,1,0:T(8,128)(2,1)S(1)} async-done(((bf16[16,32,96]{2,1,0:T(8,128)(2,1)}), bf16[16,32,96]{2,1,0:T(8,128)(2,1)S(1)}, u32[]{:S(2)}, u32[]{:S(2)}) %all-to-all-start.3) | async-done | bytes 98336 | tf_op jit(solution)/shard_map/all_to_all | solution.py:99
  167.2 3.4 %collective-permute-start.12 = (bf16[2,2,4,8,384]{4,3,2,1,0:T(8,128)(2,1)S(1)}, bf16[2,2,4,8,384]{4,3,2,1,0:T(8,128)(2,1)S(1)}, u32[]{:S(2)}, u32[]{:S(2)}) collective-permute-start(bf16[2,2,4,8,384]{4,3,2,1,0:T(8,128)(2,1)S(1)} %multiply_convert_fusion.7), channel_id=1, source_target_pairs={{2,0},{4,2},{6,4},{8,6},{10,8},{12,10},{14,12},{16,14},{18,16},{20... | collective-permute-start | bytes 294920 | tf_op jit(solution)/shard_map/ppermute | solution.py:25
  170.5 3.9 %collective-permute-start.11 = (bf16[2,2,4,8,384]{4,3,2,1,0:T(8,128)(2,1)S(1)}, bf16[2,2,4,8,384]{4,3,2,1,0:T(8,128)(2,1)S(1)}, u32[]{:S(2)}, u32[]{:S(2)}) collective-permute-start(bf16[2,2,4,8,384]{4,3,2,1,0:T(8,128)(2,1)S(1)} %multiply_convert_fusion.7), channel_id=1, source_target_pairs={{0,2},{2,4},{4,6},{6,8},{8,10},{10,12},{12,14},{14,16},{16,18},{18... | collective-permute-start | bytes 294920 | tf_op jit(solution)/shard_map/ppermute | solution.py:24
  177.4 3.0 %fusion.77 = f32[128,384]{1,0:T(8,128)} fusion(bf16[768,384]{1,0:T(8,128)(2,1)} %get-tuple-element.47, bf16[768,384]{1,0:T(8,128)(2,1)} %get-tuple-element.46, bf16[128,384]{1,0:T(8,128)(2,1)S(1)} %bitcast.236, bf16[192,1536]{1,0:T(8,128)(2,1)} %get-tuple-element.45, bf16[192,1536]{1,0:T(8,128)(2,1)} %get-tuple-element.44), kind=kOutput, calls=%fused_computation.74 | convolution fusion | flops 308477952 | bytes 2654208 | tf_op jit(solution)/shard_map/dot_general | solution.py:116
  181.3 2.7 collective-permute-start.17
  184.0 4.8 %collective-permute-done.17 = f32[2,2,4,8,384]{4,3,2,1,0:T(8,128)S(1)} collective-permute-done((f32[2,2,4,8,384]{4,3,2,1,0:T(8,128)S(1)}, f32[2,2,4,8,384]{4,3,2,1,0:T(8,128)S(1)}, u32[]{:S(2)}, u32[]{:S(2)}) %collective-permute-start.17) | collective-permute-done | bytes 196640 | tf_op jit(solution)/shard_map/ppermute | solution.py:120
  191.5 17.0 %all_to_all.40 = bf16[16,32,288]{2,1,0:T(8,128)(2,1)} all-to-all(bf16[16,32,288]{2,1,0:T(8,128)(2,1)S(1)} %bitcast.215), channel_id=1, replica_groups=mesh['lon'=16,'lat'=16,'segment'=2] {'lon'}, dimensions={0} | all-to-all | bytes 589824 | tf_op jit(solution)/shard_map/all_to_all | solution.py:96
  208.5 4.8 %shard_map.120 = bf16[512,96]{1,0:T(8,128)(2,1)} custom-call(bf16[512,288]{1,0:T(8,128)(2,1)} %bitcast.211, f32[3,512,512]{2,1,0:T(8,128)} %bitcast.199), custom_call_target="tpu_custom_call" | custom-call | tf_op jit(solution)/shard_map/pallas_call | solution.py:69
  213.3 14.5 %all_to_all.41 = bf16[16,32,96]{2,1,0:T(8,128)(2,1)S(1)} all-to-all(bf16[16,32,96]{2,1,0:T(8,128)(2,1)} %bitcast.222), channel_id=1, replica_groups=mesh['lon'=16,'lat'=16,'segment'=2] {'lon'}, dimensions={0} | all-to-all | bytes 196608 | tf_op jit(solution)/shard_map/all_to_all | solution.py:99
  228.5 4.0 %collective-permute-start.19 = (bf16[2,2,4,8,384]{4,3,2,1,0:T(8,128)(2,1)S(1)}, bf16[2,2,4,8,384]{4,3,2,1,0:T(8,128)(2,1)S(1)}, u32[]{:S(2)}, u32[]{:S(2)}) collective-permute-start(bf16[2,2,4,8,384]{4,3,2,1,0:T(8,128)(2,1)S(1)} %multiply_convert_fusion.4), channel_id=1, source_target_pairs={{2,0},{4,2},{6,4},{8,6},{10,8},{12,10},{14,12},{16,14},{18,16},{20... | collective-permute-start | bytes 294920 | tf_op jit(solution)/shard_map/ppermute | solution.py:25
  232.6 4.9 %collective-permute-start.18 = (bf16[2,2,4,8,384]{4,3,2,1,0:T(8,128)(2,1)S(1)}, bf16[2,2,4,8,384]{4,3,2,1,0:T(8,128)(2,1)S(1)}, u32[]{:S(2)}, u32[]{:S(2)}) collective-permute-start(bf16[2,2,4,8,384]{4,3,2,1,0:T(8,128)(2,1)S(1)} %multiply_convert_fusion.4), channel_id=1, source_target_pairs={{0,2},{2,4},{4,6},{6,8},{8,10},{10,12},{12,14},{14,16},{16,18},{18... | collective-permute-start | bytes 294920 | tf_op jit(solution)/shard_map/ppermute | solution.py:24
  243.1 14.7 %all_to_all.42 = bf16[16,32,288]{2,1,0:T(8,128)(2,1)} all-to-all(bf16[16,32,288]{2,1,0:T(8,128)(2,1)S(1)} %bitcast.216), channel_id=1, replica_groups=mesh['lon'=16,'lat'=16,'segment'=2] {'lon'}, dimensions={0} | all-to-all | bytes 589824 | tf_op jit(solution)/shard_map/all_to_all | solution.py:96
  257.8 4.8 %shard_map.121 = bf16[512,96]{1,0:T(8,128)(2,1)} custom-call(bf16[512,288]{1,0:T(8,128)(2,1)} %bitcast.212, f32[3,512,512]{2,1,0:T(8,128)} %bitcast.197), custom_call_target="tpu_custom_call" | custom-call | tf_op jit(solution)/shard_map/pallas_call | solution.py:69
  262.5 14.0 %all_to_all.43 = bf16[16,32,96]{2,1,0:T(8,128)(2,1)S(1)} all-to-all(bf16[16,32,96]{2,1,0:T(8,128)(2,1)} %bitcast.224), channel_id=1, replica_groups=mesh['lon'=16,'lat'=16,'segment'=2] {'lon'}, dimensions={0} | all-to-all | bytes 196608 | tf_op jit(solution)/shard_map/all_to_all | solution.py:99
  279.7 8.2 %collective-permute-start.20 = (bf16[2,2,4,8,384]{4,3,2,1,0:T(8,128)(2,1)S(1)}, bf16[2,2,4,8,384]{4,3,2,1,0:T(8,128)(2,1)S(1)}, u32[]{:S(2)}, u32[]{:S(2)}) collective-permute-start(bf16[2,2,4,8,384]{4,3,2,1,0:T(8,128)(2,1)S(1)} %multiply_convert_fusion.1), channel_id=1, source_target_pairs={{0,2},{2,4},{4,6},{6,8},{8,10},{10,12},{12,14},{14,16},{16,18},{18... | collective-permute-start | bytes 294920 | tf_op jit(solution)/shard_map/ppermute | solution.py:24
  (194 shorter events, 90.0 us)
Async XLA Ops:
  0.0 58.5 %copy-start = (bf16[1,384,1536]{2,1,0:T(8,128)(2,1)S(1)}, bf16[1,384,1536]{2,1,0:T(8,128)(2,1)}, u32[]{:S(2)}) copy-start(bf16[1,384,1536]{2,1,0:T(8,128)(2,1)} %param.21) | copy-start | bytes 3538948
  1.4 58.0 %collective-permute-start.4 = (f32[3,384]{1,0:T(4,128)}, f32[3,384]{1,0:T(4,128)}, u32[]{:S(2)}, u32[]{:S(2)}) collective-permute-start(f32[3,384]{1,0:T(4,128)} %bitcast.195), channel_id=1, source_target_pairs={{0,1},{1,0},{2,3},{3,2},{4,5},{5,4},{6,7},{7,6},{8,9},{9,8},{10,11... | collective-permute-start | bytes 13832 | tf_op jit(solution)/shard_map/ppermute | solution.py:120
  6.0 57.0 %collective-permute-start.10 = (f32[5,384]{1,0:T(8,128)S(1)}, f32[5,384]{1,0:T(8,128)}, u32[]{:S(2)}, u32[]{:S(2)}) collective-permute-start(f32[5,384]{1,0:T(8,128)S(1)} %bitcast.240), channel_id=1, source_target_pairs={{0,1},{1,0},{2,3},{3,2},{4,5},{5,4},{6,7},{7,6},{8,9},{9,8},{10,11... | collective-permute-start | bytes 23048 | tf_op jit(solution)/shard_map/ppermute | solution.py:120
  7.9 32.0 %collective-permute-start.2 = (f32[8,384]{1,0:T(8,128)}, f32[8,384]{1,0:T(8,128)S(1)}, u32[]{:S(2)}, u32[]{:S(2)}) collective-permute-start(f32[8,384]{1,0:T(8,128)} %bitcast.217), channel_id=1, source_target_pairs={{0,1},{1,0},{2,3},{3,2},{4,5},{5,4},{6,7},{7,6},{8,9},{9,8},{10,11... | collective-permute-start | bytes 36872 | tf_op jit(solution)/shard_map/ppermute | solution.py:120
  11.3 55.7 %collective-permute-start.3 = (f32[8,384]{1,0:T(8,128)}, f32[8,384]{1,0:T(8,128)}, u32[]{:S(2)}, u32[]{:S(2)}) collective-permute-start(f32[8,384]{1,0:T(8,128)} %bitcast.241), channel_id=1, source_target_pairs={{0,1},{1,0},{2,3},{3,2},{4,5},{5,4},{6,7},{7,6},{8,9},{9,8},{10,11... | collective-permute-start | bytes 36872 | tf_op jit(solution)/shard_map/ppermute | solution.py:120
  13.2 69.0 %collective-permute-start.7 = (f32[12,8,64]{2,1,0:T(8,128)}, f32[12,8,64]{2,1,0:T(8,128)}, u32[]{:S(2)}, u32[]{:S(2)}) collective-permute-start(f32[12,8,64]{2,1,0:T(8,128)} %bitcast.239), channel_id=1, source_target_pairs={{0,1},{1,0},{2,3},{3,2},{4,5},{5,4},{6,7},{7,6},{8,9},{9,8},{10,11... | collective-permute-start | bytes 73736 | tf_op jit(solution)/shard_map/ppermute | solution.py:120
  18.7 26.0 %copy-start.13 = (f32[384]{0:T(512)}, f32[384]{0:T(512)S(1)}, u32[]{:S(2)}) copy-start(f32[384]{0:T(512)S(1)} %get-tuple-element.25) | copy-start | bytes 4612
  40.0 69.1 %collective-permute-start.8 = (bf16[192,384]{1,0:T(8,128)(2,1)}, bf16[192,384]{1,0:T(8,128)(2,1)}, u32[]{:S(2)}, u32[]{:S(2)}) collective-permute-start(bf16[192,384]{1,0:T(8,128)(2,1)} %dynamic-slice_bitcast_fusion.3), channel_id=1, source_target_pairs={{0,1},{1,0},{2,3},{3,2},{4,5},{5,4},{6,7},{7,6},{8,9},{9,8},{10,11... | collective-permute-start | bytes 442376 | tf_op jit(solution)/shard_map/ppermute | solution.py:120
  48.8 20.5 %all-to-all-start = ((bf16[16,32,288]{2,1,0:T(8,128)(2,1)}), bf16[16,32,288]{2,1,0:T(8,128)(2,1)}, u32[]{:S(2)}, u32[]{:S(2)}) async-start(bf16[16,32,288]{2,1,0:T(8,128)(2,1)} %bitcast.213), calls=%async_computation | async-start | bytes 786432 | tf_op jit(solution)/shard_map/all_to_all | solution.py:96
  59.4 51.9 %collective-permute-start.5 = (bf16[192,1152]{1,0:T(8,128)(2,1)}, bf16[192,1152]{1,0:T(8,128)(2,1)}, u32[]{:S(2)}, u32[]{:S(2)}) collective-permute-start(bf16[192,1152]{1,0:T(8,128)(2,1)} %dynamic-slice_bitcast_fusion.2), channel_id=1, source_target_pairs={{0,1},{1,0},{2,3},{3,2},{4,5},{5,4},{6,7},{7,6},{8,9},{9,8},{10,11... | collective-permute-start | bytes 1327112 | tf_op jit(solution)/shard_map/ppermute | solution.py:120
  63.0 52.2 %collective-permute-start.13 = (bf16[192,1536]{1,0:T(8,128)(2,1)}, bf16[192,1536]{1,0:T(8,128)(2,1)}, u32[]{:S(2)}, u32[]{:S(2)}) collective-permute-start(bf16[192,1536]{1,0:T(8,128)(2,1)} %dynamic-slice_bitcast_fusion.1), channel_id=1, source_target_pairs={{0,1},{1,0},{2,3},{3,2},{4,5},{5,4},{6,7},{7,6},{8,9},{9,8},{10,11... | collective-permute-start | bytes 1769480 | tf_op jit(solution)/shard_map/ppermute | solution.py:120
  74.1 17.3 %all-to-all-start.1 = ((bf16[16,32,96]{2,1,0:T(8,128)(2,1)}), bf16[16,32,96]{2,1,0:T(8,128)(2,1)}, u32[]{:S(2)}, u32[]{:S(2)}) async-start(bf16[16,32,96]{2,1,0:T(8,128)(2,1)} %bitcast.221), calls=%async_computation.1 | async-start | bytes 262144 | tf_op jit(solution)/shard_map/all_to_all | solution.py:99
  94.5 23.2 %collective-permute-start.1 = (bf16[2,2,4,8,384]{4,3,2,1,0:T(8,128)(2,1)S(1)}, bf16[2,2,4,8,384]{4,3,2,1,0:T(8,128)(2,1)}, u32[]{:S(2)}, u32[]{:S(2)}) collective-permute-start(bf16[2,2,4,8,384]{4,3,2,1,0:T(8,128)(2,1)S(1)} %multiply_convert_fusion.10), channel_id=1, source_target_pairs={{2,0},{4,2},{6,4},{8,6},{10,8},{12,10},{14,12},{16,14},{18,16},{20... | collective-permute-start | bytes 294920 | tf_op jit(solution)/shard_map/ppermute | solution.py:25
  101.2 18.4 %collective-permute-start = (bf16[2,2,4,8,384]{4,3,2,1,0:T(8,128)(2,1)S(1)}, bf16[2,2,4,8,384]{4,3,2,1,0:T(8,128)(2,1)}, u32[]{:S(2)}, u32[]{:S(2)}) collective-permute-start(bf16[2,2,4,8,384]{4,3,2,1,0:T(8,128)(2,1)S(1)} %multiply_convert_fusion.10), channel_id=1, source_target_pairs={{0,2},{2,4},{4,6},{6,8},{8,10},{10,12},{12,14},{14,16},{16,18},{18... | collective-permute-start | bytes 294920 | tf_op jit(solution)/shard_map/ppermute | solution.py:24
  109.1 29.7 %collective-permute-start.15 = (bf16[768,384]{1,0:T(8,128)(2,1)}, bf16[768,384]{1,0:T(8,128)(2,1)}, u32[]{:S(2)}, u32[]{:S(2)}) collective-permute-start(bf16[768,384]{1,0:T(8,128)(2,1)} %dynamic-slice_bitcast_fusion), channel_id=1, source_target_pairs={{0,1},{1,0},{2,3},{3,2},{4,5},{5,4},{6,7},{7,6},{8,9},{9,8},{10,11... | collective-permute-start | bytes 1769480 | tf_op jit(solution)/shard_map/ppermute | solution.py:120
  111.3 25.7 %collective-permute-start.9 = (bf16[192,384]{1,0:T(8,128)(2,1)}, bf16[192,384]{1,0:T(8,128)(2,1)}, u32[]{:S(2)}, u32[]{:S(2)}) collective-permute-start(bf16[192,384]{1,0:T(8,128)(2,1)} %collective-permute-done.8), channel_id=1, source_target_pairs={{0,2},{2,0},{4,6},{6,4},{8,10},{10,8},{12,14},{14,12},{16,18},{18,... | collective-permute-start | bytes 442376 | tf_op jit(solution)/shard_map/ppermute | solution.py:129
  115.3 7.7 %collective-permute-start.6 = (bf16[192,1152]{1,0:T(8,128)(2,1)}, bf16[192,1152]{1,0:T(8,128)(2,1)}, u32[]{:S(2)}, u32[]{:S(2)}) collective-permute-start(bf16[192,1152]{1,0:T(8,128)(2,1)} %collective-permute-done.5), channel_id=1, source_target_pairs={{0,2},{2,0},{4,6},{6,4},{8,10},{10,8},{12,14},{14,12},{16,18},{18,... | collective-permute-start | bytes 1327112 | tf_op jit(solution)/shard_map/ppermute | solution.py:129
  117.7 38.7 %collective-permute-start.14 = (bf16[192,1536]{1,0:T(8,128)(2,1)}, bf16[192,1536]{1,0:T(8,128)(2,1)}, u32[]{:S(2)}, u32[]{:S(2)}) collective-permute-start(bf16[192,1536]{1,0:T(8,128)(2,1)} %collective-permute-done.13), channel_id=1, source_target_pairs={{0,2},{2,0},{4,6},{6,4},{8,10},{10,8},{12,14},{14,12},{16,18},{18,... | collective-permute-start | bytes 1769480 | tf_op jit(solution)/shard_map/ppermute | solution.py:129
  127.1 16.0 %all-to-all-start.2 = ((bf16[16,32,288]{2,1,0:T(8,128)(2,1)}), bf16[16,32,288]{2,1,0:T(8,128)(2,1)S(1)}, u32[]{:S(2)}, u32[]{:S(2)}) async-start(bf16[16,32,288]{2,1,0:T(8,128)(2,1)} %bitcast.214), calls=%async_computation.2 | async-start | bytes 786432 | tf_op jit(solution)/shard_map/all_to_all | solution.py:96
  138.7 35.7 %collective-permute-start.16 = (bf16[768,384]{1,0:T(8,128)(2,1)}, bf16[768,384]{1,0:T(8,128)(2,1)}, u32[]{:S(2)}, u32[]{:S(2)}) collective-permute-start(bf16[768,384]{1,0:T(8,128)(2,1)} %collective-permute-done.15), channel_id=1, source_target_pairs={{0,2},{2,0},{4,6},{6,4},{8,10},{10,8},{12,14},{14,12},{16,18},{18,... | collective-permute-start | bytes 1769480 | tf_op jit(solution)/shard_map/ppermute | solution.py:129
  148.7 18.4 %copy-start.16 = (f32[384]{0:T(512)S(1)}, f32[384]{0:T(512)}, u32[]{:S(2)}) copy-start(f32[384]{0:T(512)} %get-tuple-element.21) | copy-start | bytes 4612
  148.7 16.8 %all-to-all-start.3 = ((bf16[16,32,96]{2,1,0:T(8,128)(2,1)}), bf16[16,32,96]{2,1,0:T(8,128)(2,1)S(1)}, u32[]{:S(2)}, u32[]{:S(2)}) async-start(bf16[16,32,96]{2,1,0:T(8,128)(2,1)} %bitcast.220), calls=%async_computation.3 | async-start | bytes 262144 | tf_op jit(solution)/shard_map/all_to_all | solution.py:99
  167.2 9.7 %collective-permute-start.12 = (bf16[2,2,4,8,384]{4,3,2,1,0:T(8,128)(2,1)S(1)}, bf16[2,2,4,8,384]{4,3,2,1,0:T(8,128)(2,1)S(1)}, u32[]{:S(2)}, u32[]{:S(2)}) collective-permute-start(bf16[2,2,4,8,384]{4,3,2,1,0:T(8,128)(2,1)S(1)} %multiply_convert_fusion.7), channel_id=1, source_target_pairs={{2,0},{4,2},{6,4},{8,6},{10,8},{12,10},{14,12},{16,14},{18,16},{20... | collective-permute-start | bytes 294920 | tf_op jit(solution)/shard_map/ppermute | solution.py:25
  170.5 6.3 %collective-permute-start.11 = (bf16[2,2,4,8,384]{4,3,2,1,0:T(8,128)(2,1)S(1)}, bf16[2,2,4,8,384]{4,3,2,1,0:T(8,128)(2,1)S(1)}, u32[]{:S(2)}, u32[]{:S(2)}) collective-permute-start(bf16[2,2,4,8,384]{4,3,2,1,0:T(8,128)(2,1)S(1)} %multiply_convert_fusion.7), channel_id=1, source_target_pairs={{0,2},{2,4},{4,6},{6,8},{8,10},{10,12},{12,14},{14,16},{16,18},{18... | collective-permute-start | bytes 294920 | tf_op jit(solution)/shard_map/ppermute | solution.py:24
  181.3 7.5 %collective-permute-start.17 = (f32[2,2,4,8,384]{4,3,2,1,0:T(8,128)S(1)}, f32[2,2,4,8,384]{4,3,2,1,0:T(8,128)S(1)}, u32[]{:S(2)}, u32[]{:S(2)}) collective-permute-start(f32[2,2,4,8,384]{4,3,2,1,0:T(8,128)S(1)} %add.381), channel_id=1, source_target_pairs={{0,1},{1,0},{2,3},{3,2},{4,5},{5,4},{6,7},{7,6},{8,9},{9,8},{10,11... | collective-permute-start | bytes 589832 | tf_op jit(solution)/shard_map/ppermute | solution.py:120
  208.5 19.3 %copy-start.6 = (bf16[384,384]{1,0:T(8,128)(2,1)S(1)}, bf16[384,384]{1,0:T(8,128)(2,1)}, u32[]{:S(2)}) copy-start(bf16[384,384]{1,0:T(8,128)(2,1)} %pad_maximum_fusion.15) | copy-start | bytes 884740
  208.5 19.9 %copy-start.17 = (f32[384]{0:T(512)S(1)}, f32[384]{0:T(512)}, u32[]{:S(2)}) copy-start(f32[384]{0:T(512)} %get-tuple-element.21) | copy-start | bytes 4612
  228.5 9.3 %collective-permute-start.19 = (bf16[2,2,4,8,384]{4,3,2,1,0:T(8,128)(2,1)S(1)}, bf16[2,2,4,8,384]{4,3,2,1,0:T(8,128)(2,1)S(1)}, u32[]{:S(2)}, u32[]{:S(2)}) collective-permute-start(bf16[2,2,4,8,384]{4,3,2,1,0:T(8,128)(2,1)S(1)} %multiply_convert_fusion.4), channel_id=1, source_target_pairs={{2,0},{4,2},{6,4},{8,6},{10,8},{12,10},{14,12},{16,14},{18,16},{20... | collective-permute-start | bytes 294920 | tf_op jit(solution)/shard_map/ppermute | solution.py:25
  232.6 6.6 %collective-permute-start.18 = (bf16[2,2,4,8,384]{4,3,2,1,0:T(8,128)(2,1)S(1)}, bf16[2,2,4,8,384]{4,3,2,1,0:T(8,128)(2,1)S(1)}, u32[]{:S(2)}, u32[]{:S(2)}) collective-permute-start(bf16[2,2,4,8,384]{4,3,2,1,0:T(8,128)(2,1)S(1)} %multiply_convert_fusion.4), channel_id=1, source_target_pairs={{0,2},{2,4},{4,6},{6,8},{8,10},{10,12},{12,14},{14,16},{16,18},{18... | collective-permute-start | bytes 294920 | tf_op jit(solution)/shard_map/ppermute | solution.py:24
  257.8 18.8 %copy-start.8 = (bf16[1,384,384]{2,1,0:T(8,128)(2,1)S(1)}, bf16[1,384,384]{2,1,0:T(8,128)(2,1)}, u32[]{:S(2)}) copy-start(bf16[1,384,384]{2,1,0:T(8,128)(2,1)} %param.20) | copy-start | bytes 884740
  277.3 11.0 %collective-permute-start.21 = (bf16[2,2,4,8,384]{4,3,2,1,0:T(8,128)(2,1)S(1)}, bf16[2,2,4,8,384]{4,3,2,1,0:T(8,128)(2,1)S(1)}, u32[]{:S(2)}, u32[]{:S(2)}) collective-permute-start(bf16[2,2,4,8,384]{4,3,2,1,0:T(8,128)(2,1)S(1)} %multiply_convert_fusion.1), channel_id=1, source_target_pairs={{2,0},{4,2},{6,4},{8,6},{10,8},{12,10},{14,12},{16,14},{18,16},{20... | collective-permute-start | bytes 294920 | tf_op jit(solution)/shard_map/ppermute | solution.py:25
  279.7 9.8 %collective-permute-start.20 = (bf16[2,2,4,8,384]{4,3,2,1,0:T(8,128)(2,1)S(1)}, bf16[2,2,4,8,384]{4,3,2,1,0:T(8,128)(2,1)S(1)}, u32[]{:S(2)}, u32[]{:S(2)}) collective-permute-start(bf16[2,2,4,8,384]{4,3,2,1,0:T(8,128)(2,1)S(1)} %multiply_convert_fusion.1), channel_id=1, source_target_pairs={{0,2},{2,4},{4,6},{6,8},{8,10},{10,12},{12,14},{14,16},{16,18},{18... | collective-permute-start | bytes 294920 | tf_op jit(solution)/shard_map/ppermute | solution.py:24
  (16 other events, 101.8 us)

commit v3 on v1

--- a/solution.py
+++ b/solution.py
@@ -154,7 +154,12 @@
     current = initial_state
     first = None
     for tick_num in range(4):
-        result = block(current, lead_steps[tick_num // 2], mask_ids, params, bias_full)
+        result = lax.cond(
+            lax.axis_index("segment") == tick_num % 2,
+            lambda state: block(state, lead_steps[tick_num // 2], mask_ids, params, bias_full),
+            lambda state: state,
+            current,
+        )
         if tick_num == 3:
             break
         current = from_partner(result)

time: 248 us -> 300 us (1.21)
  the two profiles are of different devices: /device:TPU:1 before, /device:TPU:195 now
where the time goes in v3:
time: 300 us; the launch traced here: 299 us
  starting transfers between devices  161 us (54%)
  blocking collectives  60.2 us (20%)
  waiting for transfers between devices  21.1 us (7%)
  local copies, waits for them, and re-layouts  20.5 us (7%)
  matrix products  16.1 us (5%)
  other arithmetic  7.96 us (3%)
  Pallas kernels  7.43 us (2%)
  loops' own time  4.47 us (1%)
    ppermute x3, starting transfers between devices, from_partner(): lax.ppermute(array, 'segment', [(i, i ^ 1) for i in range(lax.axis_size('...  140 us
    all_to_all x2, blocking collectives, block(): incoming = lax.all_to_all(outgoing, 'lon', 0, 0, tiled=True)  31.6 us
    all_to_all x2, blocking collectives, block(): returned = lax.all_to_all(back, 'lon', 0, 0, tiled=True)  28.6 us
    ppermute x2, starting transfers between devices, lat_halo(): before = lax.ppermute(array[:, length - width:], 'lat', up)  16.5 us
    ppermute x3, waiting for transfers between devices, from_partner(): lax.ppermute(array, 'segment', [(i, i ^ 1) for i in range(lax.axis_size('...  10.8 us
    ppermute x2, waiting for transfers between devices, lat_halo(): after = lax.ppermute(array[:, :width], 'lat', down)  10.3 us
    pallas_call x2, Pallas kernels, attend(): pl.pallas_call(functools.partial(attention_kernel, heads=heads, head_dim=...  7.43 us
  transfers between devices with their start and end apart: 7, of which 5 were waited for; matrix products, arithmetic and copies ran while one was open for 0% of the time, Pallas kernels for 0%

profile of v3, /device:TPU:195, one launch (start us, length us, event | category | flops | bytes accessed | tf_op | source)
XLA Modules:
  0.0 298.7 jit_solution(2677688259054949097)
XLA Ops:
  0.2 2.1 fusion.90
  2.4 1.6 convolution_add_fusion.1
  4.0 1.6 convolution_add_fusion
  5.6 2.2 copy.67
  7.9 2.3 copy.68
  11.4 72.2 %collective-permute-start.8 = (f32[2,2,4,8,384]{4,3,1,0,2:T(8,128)S(1)}, f32[2,2,4,8,384]{4,3,1,0,2:T(8,128)S(1)}, u32[]{:S(2)}, u32[]{:S(2)}) collective-permute-start(f32[2,2,4,8,384]{4,3,1,0,2:T(8,128)S(1)} %get-tuple-element.273), channel_id=1, source_target_pairs={{0,1},{1,0},{2,3},{3,2},{4,5},{5,4},{6,7},{7,6},{8,9},{9,8},{10,11... | collective-permute-start | bytes 589832 | tf_op jit(solution)/shard_map/ppermute | solution.py:120
  83.6 3.0 %collective-permute-done.8 = f32[2,2,4,8,384]{4,3,1,0,2:T(8,128)S(1)} collective-permute-done((f32[2,2,4,8,384]{4,3,1,0,2:T(8,128)S(1)}, f32[2,2,4,8,384]{4,3,1,0,2:T(8,128)S(1)}, u32[]{:S(2)}, u32[]{:S(2)}) %collective-permute-start.8) | collective-permute-done | bytes 196640 | tf_op jit(solution)/shard_map/ppermute | solution.py:120
  86.6 64.4 %conditional.5 = (f32[2,2,4,8,384]{4,3,1,0,2:T(8,128)S(1)}) conditional(s32[]{:T(128)} %convert_element_type.144, f32[2,2,4,8,384]{4,3,1,0,2:T(8,128)S(1)} %collective-permute-done.8, (f32[8,384]{1,0:T(8,128)S(1)}, s32[2,4]{1,0:T(2,128)S(1)}, f32[2,2,4,8,384]{4,3,1,0,2:T(8,128)S(1)}, s32[2]{0:T(128)}, f32[8,384]{1,0:T(8,128)}, ...), branch_computations={%region_8.10_spmd, %region_9.17_spmd} | conditional | flops 457413056 | bytes 10841014 | solution.py:157
  91.3 2.3 convolution_convert_fusion.1
  93.6 1.9 copy.49
  95.5 15.8 %all_to_all.34 = bf16[16,32,288]{2,1,0:T(8,128)(2,1)} all-to-all(bf16[16,32,288]{2,1,0:T(8,128)(2,1)} %bitcast.168), channel_id=1, replica_groups=mesh['lon'=16,'lat'=16,'segment'=2] {'lon'}, dimensions={0} | all-to-all | bytes 589824 | tf_op jit(solution)/shard_map/cond/branch_1_fun/all_to_all | solution.py:96
  111.3 3.7 %branch_1_fun.5 = bf16[512,96]{1,0:T(8,128)(2,1)} custom-call(bf16[512,288]{1,0:T(8,128)(2,1)} %bitcast.164, f32[3,512,512]{2,1,0:T(8,128)S(1)} %get-tuple-element.137.bias_ref), custom_call_target="tpu_custom_call" | custom-call | tf_op jit(solution)/shard_map/cond/branch_1_fun/pallas_call | solution.py:69
  115.0 14.3 %all_to_all.35 = bf16[16,32,96]{2,1,0:T(8,128)(2,1)S(1)} all-to-all(bf16[16,32,96]{2,1,0:T(8,128)(2,1)} %bitcast.173), channel_id=1, replica_groups=mesh['lon'=16,'lat'=16,'segment'=2] {'lon'}, dimensions={0} | all-to-all | bytes 196608 | tf_op jit(solution)/shard_map/cond/branch_1_fun/all_to_all | solution.py:99
  131.0 8.2 %collective-permute-start.2 = (bf16[2,2,4,8,384]{4,3,1,0,2:T(8,128)(2,1)S(1)}, bf16[2,2,4,8,384]{4,3,1,0,2:T(8,128)(2,1)S(1)}, u32[]{:S(2)}, u32[]{:S(2)}) collective-permute-start(bf16[2,2,4,8,384]{4,3,1,0,2:T(8,128)(2,1)S(1)} %multiply_convert_fusion.4), channel_id=1, source_target_pairs={{0,2},{2,4},{4,6},{6,8},{8,10},{10,12},{12,14},{14,16},{16,18},{18... | collective-permute-start | bytes 294920 | tf_op jit(solution)/shard_map/cond/branch_1_fun/ppermute | solution.py:24
  139.2 1.9 collective-permute-start.3
  141.2 5.2 %collective-permute-done.3 = bf16[2,2,4,8,384]{4,3,1,0,2:T(8,128)(2,1)S(1)} collective-permute-done((bf16[2,2,4,8,384]{4,3,1,0,2:T(8,128)(2,1)S(1)}, bf16[2,2,4,8,384]{4,3,1,0,2:T(8,128)(2,1)S(1)}, u32[]{:S(2)}, u32[]{:S(2)}) %collective-permute-start.3) | collective-permute-done | bytes 98336 | tf_op jit(solution)/shard_map/cond/branch_1_fun/ppermute | solution.py:25
  146.9 3.0 %fusion.31 = f32[128,384]{1,0:T(8,128)} fusion(bf16[1536,384]{1,0:T(8,128)(2,1)} %get-tuple-element.141, bf16[128,384]{1,0:T(8,128)(2,1)S(1)} %bitcast.193, bf16[384,1536]{1,0:T(8,128)(2,1)} %get-tuple-element.140), kind=kOutput, calls=%fused_computation.69 | convolution fusion | flops 303759360 | bytes 2654208 | tf_op jit(solution)/shard_map/cond/branch_1_fun/dot_general | solution.py:116
  151.1 1.9 collective-permute-start.9
  153.0 4.5 %collective-permute-done.9 = f32[2,2,4,8,384]{4,3,2,1,0:T(8,128)S(1)} collective-permute-done((f32[2,2,4,8,384]{4,3,2,1,0:T(8,128)S(1)}, f32[2,2,4,8,384]{4,3,2,1,0:T(8,128)S(1)}, u32[]{:S(2)}, u32[]{:S(2)}) %collective-permute-start.9) | collective-permute-done | bytes 196640 | tf_op jit(solution)/shard_map/ppermute | solution.py:120
  158.2 66.2 %collective-permute-start.10 = (f32[2,2,4,8,384]{4,3,1,0,2:T(8,128)}, f32[2,2,4,8,384]{4,3,1,0,2:T(8,128)S(1)}, u32[]{:S(2)}, u32[]{:S(2)}) collective-permute-start(f32[2,2,4,8,384]{4,3,1,0,2:T(8,128)} %get-tuple-element.275), channel_id=1, source_target_pairs={{0,1},{1,0},{2,3},{3,2},{4,5},{5,4},{6,7},{7,6},{8,9},{9,8},{10,11... | collective-permute-start | bytes 589832 | tf_op jit(solution)/shard_map/ppermute | solution.py:120
  224.4 3.3 %collective-permute-done.10 = f32[2,2,4,8,384]{4,3,1,0,2:T(8,128)S(1)} collective-permute-done((f32[2,2,4,8,384]{4,3,1,0,2:T(8,128)}, f32[2,2,4,8,384]{4,3,1,0,2:T(8,128)S(1)}, u32[]{:S(2)}, u32[]{:S(2)}) %collective-permute-start.10) | collective-permute-done | bytes 196640 | tf_op jit(solution)/shard_map/ppermute | solution.py:120
  227.7 69.4 %conditional.7 = (f32[2,2,4,8,384]{4,3,2,1,0:T(8,128)}) conditional(s32[]{:T(128)} %convert_element_type.144, f32[2,2,4,8,384]{4,3,1,0,2:T(8,128)S(1)} %collective-permute-done.10, (f32[8,384]{1,0:T(8,128)S(1)}, s32[2,4]{1,0:T(2,128)S(1)}, f32[2,2,4,8,384]{4,3,1,0,2:T(8,128)S(1)}, s32[2]{0:T(128)}, f32[8,384]{1,0:T(8,128)}, ...), branch_computations={%region_24.26_spmd, %region_25.33_spmd} | conditional | flops 457413056 | bytes 20677650 | solution.py:157
  237.9 1.4 slice_reduce_fusion.24
  239.8 2.3 convolution_convert_fusion.3
  242.1 1.9 copy.63
  244.0 15.8 %all_to_all.38 = bf16[16,32,288]{2,1,0:T(8,128)(2,1)} all-to-all(bf16[16,32,288]{2,1,0:T(8,128)(2,1)} %bitcast.170), channel_id=1, replica_groups=mesh['lon'=16,'lat'=16,'segment'=2] {'lon'}, dimensions={0} | all-to-all | bytes 589824 | tf_op jit(solution)/shard_map/cond/branch_1_fun/all_to_all | solution.py:96
  259.8 3.7 %branch_1_fun.7 = bf16[512,96]{1,0:T(8,128)(2,1)} custom-call(bf16[512,288]{1,0:T(8,128)(2,1)} %bitcast.166, f32[3,512,512]{2,1,0:T(8,128)S(1)} %get-tuple-element.161.bias_ref), custom_call_target="tpu_custom_call" | custom-call | tf_op jit(solution)/shard_map/cond/branch_1_fun/pallas_call | solution.py:69
  263.5 14.3 %all_to_all.39 = bf16[16,32,96]{2,1,0:T(8,128)(2,1)S(1)} all-to-all(bf16[16,32,96]{2,1,0:T(8,128)(2,1)} %bitcast.177), channel_id=1, replica_groups=mesh['lon'=16,'lat'=16,'segment'=2] {'lon'}, dimensions={0} | all-to-all | bytes 196608 | tf_op jit(solution)/shard_map/cond/branch_1_fun/all_to_all | solution.py:99
  279.5 8.4 %collective-permute-start.6 = (bf16[2,2,4,8,384]{4,3,1,0,2:T(8,128)(2,1)S(1)}, bf16[2,2,4,8,384]{4,3,1,0,2:T(8,128)(2,1)S(1)}, u32[]{:S(2)}, u32[]{:S(2)}) collective-permute-start(bf16[2,2,4,8,384]{4,3,1,0,2:T(8,128)(2,1)S(1)} %multiply_convert_fusion.10), channel_id=1, source_target_pairs={{0,2},{2,4},{4,6},{6,8},{8,10},{10,12},{12,14},{14,16},{16,18},{18... | collective-permute-start | bytes 294920 | tf_op jit(solution)/shard_map/cond/branch_1_fun/ppermute | solution.py:24
  287.9 1.9 collective-permute-start.7
  289.9 5.2 %collective-permute-done.7 = bf16[2,2,4,8,384]{4,3,1,0,2:T(8,128)(2,1)S(1)} collective-permute-done((bf16[2,2,4,8,384]{4,3,1,0,2:T(8,128)(2,1)S(1)}, bf16[2,2,4,8,384]{4,3,1,0,2:T(8,128)(2,1)S(1)}, u32[]{:S(2)}, u32[]{:S(2)}) %collective-permute-start.7) | collective-permute-done | bytes 98336 | tf_op jit(solution)/shard_map/cond/branch_1_fun/ppermute | solution.py:25
  297.1 1.6 select_bitcast_fusion
  (100 shorter events, 21.1 us)
Async XLA Ops:
  0.2 2.1 copy-start.6
  7.9 2.3 copy-start.12
  7.9 2.9 copy-start.13
  7.9 3.5 %copy-start = (f32[1,8,384]{2,1,0:T(8,128)S(1)}, f32[1,8,384]{2,1,0:T(8,128)}, u32[]{:S(2)}) copy-start(f32[1,8,384]{2,1,0:T(8,128)} %param.25) | copy-start | bytes 36868
  7.9 3.5 %copy-start.1 = (f32[2,2,4,8,384]{4,3,2,1,0:T(8,128)S(1)}, f32[2,2,4,8,384]{4,3,2,1,0:T(8,128)}, u32[]{:S(2)}) copy-start(f32[2,2,4,8,384]{4,3,2,1,0:T(8,128)} %param.22) | copy-start | bytes 589828
  7.9 3.5 %copy-start.7 = (s32[2,4]{1,0:T(2,128)S(1)}, s32[2,4]{1,0:T(2,128)}, u32[]{:S(2)}) copy-start(s32[2,4]{1,0:T(2,128)} %param.23) | copy-start | bytes 100
  11.4 75.2 %collective-permute-start.8 = (f32[2,2,4,8,384]{4,3,1,0,2:T(8,128)S(1)}, f32[2,2,4,8,384]{4,3,1,0,2:T(8,128)S(1)}, u32[]{:S(2)}, u32[]{:S(2)}) collective-permute-start(f32[2,2,4,8,384]{4,3,1,0,2:T(8,128)S(1)} %get-tuple-element.273), channel_id=1, source_target_pairs={{0,1},{1,0},{2,3},{3,2},{4,5},{5,4},{6,7},{7,6},{8,9},{9,8},{10,11... | collective-permute-start | bytes 589832 | tf_op jit(solution)/shard_map/ppermute | solution.py:120
  115.0 26.1 %copy-start.3 = (f32[5,384]{1,0:T(8,128)S(1)}, f32[5,384]{1,0:T(8,128)}, u32[]{:S(2)}) copy-start(f32[5,384]{1,0:T(8,128)} %get-tuple-element.139) | copy-start | bytes 23044 | tf_op jit(solution)/shard_map/cond
  130.6 16.2 %copy-start.8 = (f32[384]{0:T(512)S(1)}, f32[384]{0:T(512)}, u32[]{:S(2)}) copy-start(f32[384]{0:T(512)} %get-tuple-element.232) | copy-start | bytes 4612 | tf_op jit(solution)/shard_map/cond
  131.0 10.2 %collective-permute-start.2 = (bf16[2,2,4,8,384]{4,3,1,0,2:T(8,128)(2,1)S(1)}, bf16[2,2,4,8,384]{4,3,1,0,2:T(8,128)(2,1)S(1)}, u32[]{:S(2)}, u32[]{:S(2)}) collective-permute-start(bf16[2,2,4,8,384]{4,3,1,0,2:T(8,128)(2,1)S(1)} %multiply_convert_fusion.4), channel_id=1, source_target_pairs={{0,2},{2,4},{4,6},{6,8},{8,10},{10,12},{12,14},{14,16},{16,18},{18... | collective-permute-start | bytes 294920 | tf_op jit(solution)/shard_map/cond/branch_1_fun/ppermute | solution.py:24
  139.2 7.1 %collective-permute-start.3 = (bf16[2,2,4,8,384]{4,3,1,0,2:T(8,128)(2,1)S(1)}, bf16[2,2,4,8,384]{4,3,1,0,2:T(8,128)(2,1)S(1)}, u32[]{:S(2)}, u32[]{:S(2)}) collective-permute-start(bf16[2,2,4,8,384]{4,3,1,0,2:T(8,128)(2,1)S(1)} %multiply_convert_fusion.4), channel_id=1, source_target_pairs={{2,0},{4,2},{6,4},{8,6},{10,8},{12,10},{14,12},{16,14},{18,16},{20... | collective-permute-start | bytes 294920 | tf_op jit(solution)/shard_map/cond/branch_1_fun/ppermute | solution.py:25
  151.1 6.4 %collective-permute-start.9 = (f32[2,2,4,8,384]{4,3,2,1,0:T(8,128)S(1)}, f32[2,2,4,8,384]{4,3,2,1,0:T(8,128)S(1)}, u32[]{:S(2)}, u32[]{:S(2)}) collective-permute-start(f32[2,2,4,8,384]{4,3,2,1,0:T(8,128)S(1)} %copy.71), channel_id=1, source_target_pairs={{0,1},{1,0},{2,3},{3,2},{4,5},{5,4},{6,7},{7,6},{8,9},{9,8},{10,11... | collective-permute-start | bytes 589832 | tf_op jit(solution)/shard_map/ppermute | solution.py:120
  158.2 69.5 %collective-permute-start.10 = (f32[2,2,4,8,384]{4,3,1,0,2:T(8,128)}, f32[2,2,4,8,384]{4,3,1,0,2:T(8,128)S(1)}, u32[]{:S(2)}, u32[]{:S(2)}) collective-permute-start(f32[2,2,4,8,384]{4,3,1,0,2:T(8,128)} %get-tuple-element.275), channel_id=1, source_target_pairs={{0,1},{1,0},{2,3},{3,2},{4,5},{5,4},{6,7},{7,6},{8,9},{9,8},{10,11... | collective-permute-start | bytes 589832 | tf_op jit(solution)/shard_map/ppermute | solution.py:120
  263.5 15.9 %copy-start.11 = (f32[384]{0:T(512)S(1)}, f32[384]{0:T(512)}, u32[]{:S(2)}) copy-start(f32[384]{0:T(512)} %get-tuple-element.249) | copy-start | bytes 4612 | tf_op jit(solution)/shard_map/cond
  263.5 26.4 %copy-start.5 = (f32[5,384]{1,0:T(8,128)S(1)}, f32[5,384]{1,0:T(8,128)}, u32[]{:S(2)}) copy-start(f32[5,384]{1,0:T(8,128)} %get-tuple-element.163) | copy-start | bytes 23044 | tf_op jit(solution)/shard_map/cond
  279.0 16.4 %copy-start.10 = (f32[384]{0:T(512)S(1)}, f32[384]{0:T(512)}, u32[]{:S(2)}) copy-start(f32[384]{0:T(512)} %get-tuple-element.248) | copy-start | bytes 4612 | tf_op jit(solution)/shard_map/cond
  279.0 16.6 %copy-start.15 = (bf16[1536,384]{1,0:T(8,128)(2,1)S(1)}, bf16[1536,384]{1,0:T(8,128)(2,1)}, u32[]{:S(2)}) copy-start(bf16[1536,384]{1,0:T(8,128)(2,1)} %get-tuple-element.165) | copy-start | bytes 3538948 | tf_op jit(solution)/shard_map/cond
  279.2 16.4 %copy-start.14 = (bf16[384,1536]{1,0:T(8,128)(2,1)S(1)}, bf16[384,1536]{1,0:T(8,128)(2,1)}, u32[]{:S(2)}) copy-start(bf16[384,1536]{1,0:T(8,128)(2,1)} %get-tuple-element.164) | copy-start | bytes 3538948 | tf_op jit(solution)/shard_map/cond
  279.5 10.4 %collective-permute-start.6 = (bf16[2,2,4,8,384]{4,3,1,0,2:T(8,128)(2,1)S(1)}, bf16[2,2,4,8,384]{4,3,1,0,2:T(8,128)(2,1)S(1)}, u32[]{:S(2)}, u32[]{:S(2)}) collective-permute-start(bf16[2,2,4,8,384]{4,3,1,0,2:T(8,128)(2,1)S(1)} %multiply_convert_fusion.10), channel_id=1, source_target_pairs={{0,2},{2,4},{4,6},{6,8},{8,10},{10,12},{12,14},{14,16},{16,18},{18... | collective-permute-start | bytes 294920 | tf_op jit(solution)/shard_map/cond/branch_1_fun/ppermute | solution.py:24
  287.9 7.1 %collective-permute-start.7 = (bf16[2,2,4,8,384]{4,3,1,0,2:T(8,128)(2,1)S(1)}, bf16[2,2,4,8,384]{4,3,1,0,2:T(8,128)(2,1)S(1)}, u32[]{:S(2)}, u32[]{:S(2)}) collective-permute-start(bf16[2,2,4,8,384]{4,3,1,0,2:T(8,128)(2,1)S(1)} %multiply_convert_fusion.10), channel_id=1, source_target_pairs={{2,0},{4,2},{6,4},{8,6},{10,8},{12,10},{14,12},{16,14},{18,16},{20... | collective-permute-start | bytes 294920 | tf_op jit(solution)/shard_map/cond/branch_1_fun/ppermute | solution.py:25

commit v4 on v1

--- a/solution.py
+++ b/solution.py
@@ -50,27 +50,35 @@
 
 def attention_kernel(x_ref, bias_ref, o_ref, *, heads, head_dim):
     width = heads * head_dim
+    step = pl.program_id(0)
     for h in range(heads):
-        cols = slice(h * head_dim, (h + 1) * head_dim)
-        q = x_ref[:, cols]
-        k = x_ref[:, width + h * head_dim : width + (h + 1) * head_dim]
-        v = x_ref[:, 2 * width + h * head_dim : 2 * width + (h + 1) * head_dim]
-        s = lax.dot_general(q, k, (((1,), (1,)), ((), ())), preferred_element_type=jnp.float32)
-        s = s * (head_dim ** (-0.5)) + bias_ref[h]
-        row_max = jnp.max(s, axis=-1, keepdims=True)
-        weights = jnp.exp(s - row_max)
-        total = jnp.sum(weights, axis=-1, keepdims=True)
-        summed = jnp.dot(weights.astype(jnp.bfloat16), v, preferred_element_type=jnp.float32)
-        o_ref[:, cols] = (summed / total).astype(o_ref.dtype)
+
+        @pl.when(step == h)
+        def _():
+            cols = slice(h * head_dim, (h + 1) * head_dim)
+            q = x_ref[:, cols]
+            k = x_ref[:, width + h * head_dim : width + (h + 1) * head_dim]
+            v = x_ref[:, 2 * width + h * head_dim : 2 * width + (h + 1) * head_dim]
+            s = lax.dot_general(q, k, (((1,), (1,)), ((), ())), preferred_element_type=jnp.float32)
+            s = s * (head_dim ** (-0.5)) + bias_ref[0]
+            row_max = jnp.max(s, axis=-1, keepdims=True)
+            weights = jnp.exp(s - row_max)
+            total = jnp.sum(weights, axis=-1, keepdims=True)
+            summed = jnp.dot(weights.astype(jnp.bfloat16), v, preferred_element_type=jnp.float32)
+            o_ref[:, cols] = (summed / total).astype(o_ref.dtype)
 
 
 def attend(x, bias_full, head_dim):
-    heads = bias_full.shape[0]
+    heads, queries, keys = bias_full.shape
     return pl.pallas_call(
         functools.partial(attention_kernel, heads=heads, head_dim=head_dim),
         out_shape=jax.ShapeDtypeStruct((x.shape[0], heads * head_dim), jnp.bfloat16),
-        in_specs=[pl.BlockSpec(memory_space=pltpu.VMEM)] * 2,
-        out_specs=pl.BlockSpec(memory_space=pltpu.VMEM),
+        grid=(heads,),
+        in_specs=[
+            pl.BlockSpec(x.shape, lambda h: (0, 0)),
+            pl.BlockSpec((1, queries, keys), lambda h: (h, 0, 0)),
+        ],
+        out_specs=pl.BlockSpec((x.shape[0], heads * head_dim), lambda h: (0, 0)),
     )(x, bias_full)
 
 
@@ -84,7 +92,9 @@
     tokens_local = lon_local * levels
     combos = members * rows_lat
 
-    mask_embed = jnp.take(mask_tab, mask_ids, axis=0)
+    kinds = mask_tab.shape[0]
+    mask_onehot = (mask_ids[..., None] == jnp.arange(kinds, dtype=jnp.int32)).astype(jnp.float32)
+    mask_embed = jnp.dot(mask_onehot, mask_tab, precision=lax.Precision.HIGHEST)
     lead_row = lax.dynamic_index_in_dim(lead_tab, lead_index, axis=0, keepdims=False)
     hidden = field + mask_embed[None, :, :, None, :] + lead_row
     normed = layer_norm(hidden, gains[0]).astype(jnp.bfloat16)

time: 248 us -> 248 us (level)
  no operation moved by 1% of the time
where the time goes in v4:
time: 248 us; the launch traced here: 246 us
  blocking collectives  102 us (41%)
  starting transfers between devices  61.6 us (25%)
  waiting for transfers between devices  25.2 us (10%)
  Pallas kernels  20.2 us (8%)
  matrix products  13 us (5%)
  local copies, waits for them, and re-layouts  10.5 us (4%)
  other arithmetic  8.92 us (4%)
  between operations  4.81 us (2%)
    all_to_all x4, blocking collectives, block(): returned = lax.all_to_all(back, 'lon', 0, 0, tiled=True)  55.3 us
    all_to_all x3, blocking collectives, block(): incoming = lax.all_to_all(outgoing, 'lon', 0, 0, tiled=True)  46.6 us
    ppermute x4, starting transfers between devices, lat_halo(): before = lax.ppermute(array[:, length - width:], 'lat', up)  31.7 us
    pallas_call x4, Pallas kernels, attend(): pl.pallas_call(functools.partial(attention_kernel, heads=heads, head_dim=...  20.2 us
    ppermute x4, starting transfers between devices, lat_halo(): after = lax.ppermute(array[:, :width], 'lat', down)  13.2 us
    ppermute x3, waiting for transfers between devices, from_partner(): lax.ppermute(array, 'segment', [(i, i ^ 1) for i in range(lax.axis_size('...  13.1 us
    all_to_all x1, starting transfers between devices, block(): incoming = lax.all_to_all(outgoing, 'lon', 0, 0, tiled=True)  10.2 us
    ppermute x3, starting transfers between devices, from_partner(): lax.ppermute(array, 'segment', [(i, i ^ 1) for i in range(lax.axis_size('...  6.47 us
  transfers between devices with their start and end apart: 12, of which 12 were waited for; matrix products, arithmetic and copies ran while one was open for 3% of the time, Pallas kernels for 0%

profile of v4, /device:TPU:1, one launch (start us, length us, event | category | flops | bytes accessed | tf_op | source)
XLA Modules:
  0.0 246.2 jit_solution(1829102189551351521)
XLA Ops:
  0.0 1.5 fusion.116
  14.2 10.2 %all-to-all-start = ((bf16[16,32,288]{2,1,0:T(8,128)(2,1)}), bf16[16,32,288]{2,1,0:T(8,128)(2,1)S(1)}, u32[]{:S(2)}, u32[]{:S(2)}) async-start(bf16[16,32,288]{2,1,0:T(8,128)(2,1)} %bitcast.7), calls=%async_computation | async-start | bytes 786432 | tf_op jit(solution)/shard_map/all_to_all | solution.py:106
  24.7 1.3 fusion
  26.1 1.6 convolution_add_fusion.1
  27.7 3.3 %convolution_add_fusion = f32[24,32768]{1,0:T(8,128)} fusion(f32[24,32768]{1,0:T(8,128)S(1)} %convolution_add_fusion.1, s32[32768]{0:T(1024)S(1)} %add_select_fusion, f32[1,12,8,64]{3,2,1,0:T(8,128)S(1)} %copy-done.5, s32[]{:T(128)S(6)} %select_n.42), kind=kOutput, calls=%fused_computation | convolution fusion | flops 103557632 | bytes 6434820 | tf_op jit(solution)/shard_map/dot_general | solution.py:43
  31.0 5.7 %all-to-all-done = bf16[16,32,288]{2,1,0:T(8,128)(2,1)S(1)} async-done(((bf16[16,32,288]{2,1,0:T(8,128)(2,1)}), bf16[16,32,288]{2,1,0:T(8,128)(2,1)S(1)}, u32[]{:S(2)}, u32[]{:S(2)}) %all-to-all-start) | async-done | bytes 294944 | tf_op jit(solution)/shard_map/all_to_all | solution.py:106
  37.4 5.1 %shard_map.118 = bf16[512,96]{1,0:T(8,128)(2,1)} custom-call(bf16[512,288]{1,0:T(8,128)(2,1)} %bitcast.179, f32[3,512,512]{2,1,0:T(8,128)} %bitcast.166), custom_call_target="tpu_custom_call" | custom-call | tf_op jit(solution)/shard_map/pallas_call | solution.py:73
  42.5 15.4 %all_to_all.40 = bf16[16,32,96]{2,1,0:T(8,128)(2,1)S(1)} all-to-all(bf16[16,32,96]{2,1,0:T(8,128)(2,1)} %bitcast.187), channel_id=1, replica_groups=mesh['lon'=16,'lat'=16,'segment'=2] {'lon'}, dimensions={0} | all-to-all | bytes 196608 | tf_op jit(solution)/shard_map/all_to_all | solution.py:109
  58.7 4.4 %collective-permute-start.1 = (bf16[2,2,4,8,384]{4,3,1,0,2:T(8,128)(2,1)S(1)}, bf16[2,2,4,8,384]{4,3,1,0,2:T(8,128)(2,1)S(1)}, u32[]{:S(2)}, u32[]{:S(2)}) collective-permute-start(bf16[2,2,4,8,384]{4,3,1,0,2:T(8,128)(2,1)S(1)} %multiply_convert_fusion.10), channel_id=1, source_target_pairs={{2,0},{4,2},{6,4},{8,6},{10,8},{12,10},{14,12},{16,14},{18,16},{20... | collective-permute-start | bytes 294920 | tf_op jit(solution)/shard_map/ppermute | solution.py:25
  63.1 3.9 %collective-permute-start = (bf16[2,2,4,8,384]{4,3,1,0,2:T(8,128)(2,1)S(1)}, bf16[2,2,4,8,384]{4,3,1,0,2:T(8,128)(2,1)S(1)}, u32[]{:S(2)}, u32[]{:S(2)}) collective-permute-start(bf16[2,2,4,8,384]{4,3,1,0,2:T(8,128)(2,1)S(1)} %multiply_convert_fusion.10), channel_id=1, source_target_pairs={{0,2},{2,4},{4,6},{6,8},{8,10},{10,12},{12,14},{14,16},{16,18},{18... | collective-permute-start | bytes 294920 | tf_op jit(solution)/shard_map/ppermute | solution.py:24
  67.3 1.3 collective-permute-done
  70.8 2.2 collective-permute-start.2
  73.0 4.6 %collective-permute-done.2 = f32[2,2,4,8,384]{4,3,1,0,2:T(8,128)S(1)} collective-permute-done((f32[2,2,4,8,384]{4,3,1,0,2:T(8,128)S(1)}, f32[2,2,4,8,384]{4,3,1,0,2:T(8,128)S(1)}, u32[]{:S(2)}, u32[]{:S(2)}) %collective-permute-start.2) | collective-permute-done | bytes 196640 | tf_op jit(solution)/shard_map/ppermute | solution.py:130
  78.7 17.3 %all_to_all.41 = bf16[16,32,288]{2,1,0:T(8,128)(2,1)} all-to-all(bf16[16,32,288]{2,1,0:T(8,128)(2,1)S(1)} %bitcast.183), channel_id=1, replica_groups=mesh['lon'=16,'lat'=16,'segment'=2] {'lon'}, dimensions={0} | all-to-all | bytes 589824 | tf_op jit(solution)/shard_map/all_to_all | solution.py:106
  95.9 5.0 %shard_map.119 = bf16[512,96]{1,0:T(8,128)(2,1)} custom-call(bf16[512,288]{1,0:T(8,128)(2,1)} %bitcast.181, f32[3,512,512]{2,1,0:T(8,128)} %bitcast.167), custom_call_target="tpu_custom_call" | custom-call | tf_op jit(solution)/shard_map/pallas_call | solution.py:73
  101.0 13.4 %all_to_all.42 = bf16[16,32,96]{2,1,0:T(8,128)(2,1)S(1)} all-to-all(bf16[16,32,96]{2,1,0:T(8,128)(2,1)} %bitcast.189), channel_id=1, replica_groups=mesh['lon'=16,'lat'=16,'segment'=2] {'lon'}, dimensions={0} | all-to-all | bytes 196608 | tf_op jit(solution)/shard_map/all_to_all | solution.py:109
  115.1 3.9 %collective-permute-start.4 = (bf16[2,2,4,8,384]{4,3,1,0,2:T(8,128)(2,1)S(1)}, bf16[2,2,4,8,384]{4,3,1,0,2:T(8,128)(2,1)S(1)}, u32[]{:S(2)}, u32[]{:S(2)}) collective-permute-start(bf16[2,2,4,8,384]{4,3,1,0,2:T(8,128)(2,1)S(1)} %multiply_convert_fusion.7), channel_id=1, source_target_pairs={{2,0},{4,2},{6,4},{8,6},{10,8},{12,10},{14,12},{16,14},{18,16},{20... | collective-permute-start | bytes 294920 | tf_op jit(solution)/shard_map/ppermute | solution.py:25
  119.0 5.6 %collective-permute-start.3 = (bf16[2,2,4,8,384]{4,3,1,0,2:T(8,128)(2,1)S(1)}, bf16[2,2,4,8,384]{4,3,1,0,2:T(8,128)(2,1)S(1)}, u32[]{:S(2)}, u32[]{:S(2)}) collective-permute-start(bf16[2,2,4,8,384]{4,3,1,0,2:T(8,128)(2,1)S(1)} %multiply_convert_fusion.7), channel_id=1, source_target_pairs={{0,2},{2,4},{4,6},{6,8},{8,10},{10,12},{12,14},{14,16},{16,18},{18... | collective-permute-start | bytes 294920 | tf_op jit(solution)/shard_map/ppermute | solution.py:24
  128.4 2.2 collective-permute-start.5
  130.6 4.2 %collective-permute-done.5 = f32[2,2,4,8,384]{4,3,1,0,2:T(8,128)S(1)} collective-permute-done((f32[2,2,4,8,384]{4,3,1,0,2:T(8,128)S(1)}, f32[2,2,4,8,384]{4,3,1,0,2:T(8,128)S(1)}, u32[]{:S(2)}, u32[]{:S(2)}) %collective-permute-start.5) | collective-permute-done | bytes 196640 | tf_op jit(solution)/shard_map/ppermute | solution.py:130
  135.9 15.4 %all_to_all.43 = bf16[16,32,288]{2,1,0:T(8,128)(2,1)} all-to-all(bf16[16,32,288]{2,1,0:T(8,128)(2,1)S(1)} %bitcast.184), channel_id=1, replica_groups=mesh['lon'=16,'lat'=16,'segment'=2] {'lon'}, dimensions={0} | all-to-all | bytes 589824 | tf_op jit(solution)/shard_map/all_to_all | solution.py:106
  151.3 5.0 %shard_map.120 = bf16[512,96]{1,0:T(8,128)(2,1)} custom-call(bf16[512,288]{1,0:T(8,128)(2,1)} %bitcast.182, f32[3,512,512]{2,1,0:T(8,128)} %bitcast.168), custom_call_target="tpu_custom_call" | custom-call | tf_op jit(solution)/shard_map/pallas_call | solution.py:73
  156.3 13.6 %all_to_all.44 = bf16[16,32,96]{2,1,0:T(8,128)(2,1)S(1)} all-to-all(bf16[16,32,96]{2,1,0:T(8,128)(2,1)} %bitcast.191), channel_id=1, replica_groups=mesh['lon'=16,'lat'=16,'segment'=2] {'lon'}, dimensions={0} | all-to-all | bytes 196608 | tf_op jit(solution)/shard_map/all_to_all | solution.py:109
  170.6 3.1 %collective-permute-start.7 = (bf16[2,2,4,8,384]{4,3,1,0,2:T(8,128)(2,1)S(1)}, bf16[2,2,4,8,384]{4,3,1,0,2:T(8,128)(2,1)S(1)}, u32[]{:S(2)}, u32[]{:S(2)}) collective-permute-start(bf16[2,2,4,8,384]{4,3,1,0,2:T(8,128)(2,1)S(1)} %multiply_convert_fusion.4), channel_id=1, source_target_pairs={{2,0},{4,2},{6,4},{8,6},{10,8},{12,10},{14,12},{16,14},{18,16},{20... | collective-permute-start | bytes 294920 | tf_op jit(solution)/shard_map/ppermute | solution.py:25
  173.7 8.8 %collective-permute-start.6 = (bf16[2,2,4,8,384]{4,3,1,0,2:T(8,128)(2,1)S(1)}, bf16[2,2,4,8,384]{4,3,1,0,2:T(8,128)(2,1)S(1)}, u32[]{:S(2)}, u32[]{:S(2)}) collective-permute-start(bf16[2,2,4,8,384]{4,3,1,0,2:T(8,128)(2,1)S(1)} %multiply_convert_fusion.4), channel_id=1, source_target_pairs={{0,2},{2,4},{4,6},{6,8},{8,10},{10,12},{12,14},{14,16},{16,18},{18... | collective-permute-start | bytes 294920 | tf_op jit(solution)/shard_map/ppermute | solution.py:24
  186.2 2.0 collective-permute-start.8
  188.3 4.4 %collective-permute-done.8 = f32[2,2,4,8,384]{4,3,1,0,2:T(8,128)S(1)} collective-permute-done((f32[2,2,4,8,384]{4,3,1,0,2:T(8,128)S(1)}, f32[2,2,4,8,384]{4,3,1,0,2:T(8,128)S(1)}, u32[]{:S(2)}, u32[]{:S(2)}) %collective-permute-start.8) | collective-permute-done | bytes 196640 | tf_op jit(solution)/shard_map/ppermute | solution.py:130
  193.7 14.0 %all_to_all.45 = bf16[16,32,288]{2,1,0:T(8,128)(2,1)} all-to-all(bf16[16,32,288]{2,1,0:T(8,128)(2,1)S(1)} %bitcast.185), channel_id=1, replica_groups=mesh['lon'=16,'lat'=16,'segment'=2] {'lon'}, dimensions={0} | all-to-all | bytes 589824 | tf_op jit(solution)/shard_map/all_to_all | solution.py:106
  207.7 5.0 %shard_map.121 = bf16[512,96]{1,0:T(8,128)(2,1)} custom-call(bf16[512,288]{1,0:T(8,128)(2,1)} %bitcast.180, f32[3,512,512]{2,1,0:T(8,128)} %bitcast.169), custom_call_target="tpu_custom_call" | custom-call | tf_op jit(solution)/shard_map/pallas_call | solution.py:73
  212.7 12.9 %all_to_all.46 = bf16[16,32,96]{2,1,0:T(8,128)(2,1)S(1)} all-to-all(bf16[16,32,96]{2,1,0:T(8,128)(2,1)} %bitcast.186), channel_id=1, replica_groups=mesh['lon'=16,'lat'=16,'segment'=2] {'lon'}, dimensions={0} | all-to-all | bytes 196608 | tf_op jit(solution)/shard_map/all_to_all | solution.py:109
  226.4 1.9 collective-permute-start.10
  228.3 13.4 %collective-permute-start.9 = (bf16[2,2,4,8,384]{4,3,1,0,2:T(8,128)(2,1)S(1)}, bf16[2,2,4,8,384]{4,3,1,0,2:T(8,128)(2,1)S(1)}, u32[]{:S(2)}, u32[]{:S(2)}) collective-permute-start(bf16[2,2,4,8,384]{4,3,1,0,2:T(8,128)(2,1)S(1)} %multiply_convert_fusion.1), channel_id=1, source_target_pairs={{0,2},{2,4},{4,6},{6,8},{8,10},{10,12},{12,14},{14,16},{16,18},{18... | collective-permute-start | bytes 294920 | tf_op jit(solution)/shard_map/ppermute | solution.py:24
  (130 shorter events, 29.9 us)
Async XLA Ops:
  0.0 69.1 %copy-start = (bf16[1,384,1536]{2,1,0:T(8,128)(2,1)S(1)}, bf16[1,384,1536]{2,1,0:T(8,128)(2,1)}, u32[]{:S(2)}) copy-start(bf16[1,384,1536]{2,1,0:T(8,128)(2,1)} %param.19) | copy-start | bytes 3538948
  0.0 11.9 %copy-start.4 = (bf16[1,384,1152]{2,1,0:T(8,128)(2,1)S(1)}, bf16[1,384,1152]{2,1,0:T(8,128)(2,1)}, u32[]{:S(2)}) copy-start(bf16[1,384,1152]{2,1,0:T(8,128)(2,1)} %param.17) | copy-start | bytes 2654212
  13.3 11.4 %copy-start.5 = (f32[1,12,8,64]{3,2,1,0:T(8,128)S(1)}, f32[1,12,8,64]{3,2,1,0:T(8,128)}, u32[]{:S(2)}) copy-start(f32[1,12,8,64]{3,2,1,0:T(8,128)} %param.23) | copy-start | bytes 73732
  14.2 22.4 %all-to-all-start = ((bf16[16,32,288]{2,1,0:T(8,128)(2,1)}), bf16[16,32,288]{2,1,0:T(8,128)(2,1)S(1)}, u32[]{:S(2)}, u32[]{:S(2)}) async-start(bf16[16,32,288]{2,1,0:T(8,128)(2,1)} %bitcast.7), calls=%async_computation | async-start | bytes 786432 | tf_op jit(solution)/shard_map/all_to_all | solution.py:106
  36.7 0.7 copy-start.3
  37.4 20.5 %copy-start.1 = (bf16[1,384,384]{2,1,0:T(8,128)(2,1)S(1)}, bf16[1,384,384]{2,1,0:T(8,128)(2,1)}, u32[]{:S(2)}) copy-start(bf16[1,384,384]{2,1,0:T(8,128)(2,1)} %param.18) | copy-start | bytes 884740
  37.4 20.8 %copy-start.2 = (f32[2,2,4,8,384]{4,3,2,1,0:T(8,128)S(1)}, f32[2,2,4,8,384]{4,3,2,1,0:T(8,128)}, u32[]{:S(2)}) copy-start(f32[2,2,4,8,384]{4,3,2,1,0:T(8,128)} %param.12) | copy-start | bytes 589828
  42.5 24.5 %copy-start.6 = (f32[1,5,384]{2,0,1:T(1,128)S(1)}, f32[1,5,384]{2,0,1:T(1,128)}, u32[]{:S(2)}) copy-start(f32[1,5,384]{2,0,1:T(1,128)} %param.22) | copy-start | bytes 23044
  58.7 8.6 %collective-permute-start.1 = (bf16[2,2,4,8,384]{4,3,1,0,2:T(8,128)(2,1)S(1)}, bf16[2,2,4,8,384]{4,3,1,0,2:T(8,128)(2,1)S(1)}, u32[]{:S(2)}, u32[]{:S(2)}) collective-permute-start(bf16[2,2,4,8,384]{4,3,1,0,2:T(8,128)(2,1)S(1)} %multiply_convert_fusion.10), channel_id=1, source_target_pairs={{2,0},{4,2},{6,4},{8,6},{10,8},{12,10},{14,12},{16,14},{18,16},{20... | collective-permute-start | bytes 294920 | tf_op jit(solution)/shard_map/ppermute | solution.py:25
  63.1 5.5 %collective-permute-start = (bf16[2,2,4,8,384]{4,3,1,0,2:T(8,128)(2,1)S(1)}, bf16[2,2,4,8,384]{4,3,1,0,2:T(8,128)(2,1)S(1)}, u32[]{:S(2)}, u32[]{:S(2)}) collective-permute-start(bf16[2,2,4,8,384]{4,3,1,0,2:T(8,128)(2,1)S(1)} %multiply_convert_fusion.10), channel_id=1, source_target_pairs={{0,2},{2,4},{4,6},{6,8},{8,10},{10,12},{12,14},{14,16},{16,18},{18... | collective-permute-start | bytes 294920 | tf_op jit(solution)/shard_map/ppermute | solution.py:24
  69.1 1.3 copy-start.7
  70.8 6.8 %collective-permute-start.2 = (f32[2,2,4,8,384]{4,3,1,0,2:T(8,128)S(1)}, f32[2,2,4,8,384]{4,3,1,0,2:T(8,128)S(1)}, u32[]{:S(2)}, u32[]{:S(2)}) collective-permute-start(f32[2,2,4,8,384]{4,3,1,0,2:T(8,128)S(1)} %fusion.20), channel_id=1, source_target_pairs={{0,1},{1,0},{2,3},{3,2},{4,5},{5,4},{6,7},{7,6},{8,9},{9,8},{10,11... | collective-permute-start | bytes 589832 | tf_op jit(solution)/shard_map/ppermute | solution.py:130
  115.1 9.9 %collective-permute-start.4 = (bf16[2,2,4,8,384]{4,3,1,0,2:T(8,128)(2,1)S(1)}, bf16[2,2,4,8,384]{4,3,1,0,2:T(8,128)(2,1)S(1)}, u32[]{:S(2)}, u32[]{:S(2)}) collective-permute-start(bf16[2,2,4,8,384]{4,3,1,0,2:T(8,128)(2,1)S(1)} %multiply_convert_fusion.7), channel_id=1, source_target_pairs={{2,0},{4,2},{6,4},{8,6},{10,8},{12,10},{14,12},{16,14},{18,16},{20... | collective-permute-start | bytes 294920 | tf_op jit(solution)/shard_map/ppermute | solution.py:25
  119.0 7.3 %collective-permute-start.3 = (bf16[2,2,4,8,384]{4,3,1,0,2:T(8,128)(2,1)S(1)}, bf16[2,2,4,8,384]{4,3,1,0,2:T(8,128)(2,1)S(1)}, u32[]{:S(2)}, u32[]{:S(2)}) collective-permute-start(bf16[2,2,4,8,384]{4,3,1,0,2:T(8,128)(2,1)S(1)} %multiply_convert_fusion.7), channel_id=1, source_target_pairs={{0,2},{2,4},{4,6},{6,8},{8,10},{10,12},{12,14},{14,16},{16,18},{18... | collective-permute-start | bytes 294920 | tf_op jit(solution)/shard_map/ppermute | solution.py:24
  126.8 1.3 copy-start.8
  128.4 6.4 %collective-permute-start.5 = (f32[2,2,4,8,384]{4,3,1,0,2:T(8,128)S(1)}, f32[2,2,4,8,384]{4,3,1,0,2:T(8,128)S(1)}, u32[]{:S(2)}, u32[]{:S(2)}) collective-permute-start(f32[2,2,4,8,384]{4,3,1,0,2:T(8,128)S(1)} %fusion.23), channel_id=1, source_target_pairs={{0,1},{1,0},{2,3},{3,2},{4,5},{5,4},{6,7},{7,6},{8,9},{9,8},{10,11... | collective-permute-start | bytes 589832 | tf_op jit(solution)/shard_map/ppermute | solution.py:130
  170.6 12.2 %collective-permute-start.7 = (bf16[2,2,4,8,384]{4,3,1,0,2:T(8,128)(2,1)S(1)}, bf16[2,2,4,8,384]{4,3,1,0,2:T(8,128)(2,1)S(1)}, u32[]{:S(2)}, u32[]{:S(2)}) collective-permute-start(bf16[2,2,4,8,384]{4,3,1,0,2:T(8,128)(2,1)S(1)} %multiply_convert_fusion.4), channel_id=1, source_target_pairs={{2,0},{4,2},{6,4},{8,6},{10,8},{12,10},{14,12},{16,14},{18,16},{20... | collective-permute-start | bytes 294920 | tf_op jit(solution)/shard_map/ppermute | solution.py:25
  173.7 10.4 %collective-permute-start.6 = (bf16[2,2,4,8,384]{4,3,1,0,2:T(8,128)(2,1)S(1)}, bf16[2,2,4,8,384]{4,3,1,0,2:T(8,128)(2,1)S(1)}, u32[]{:S(2)}, u32[]{:S(2)}) collective-permute-start(bf16[2,2,4,8,384]{4,3,1,0,2:T(8,128)(2,1)S(1)} %multiply_convert_fusion.4), channel_id=1, source_target_pairs={{0,2},{2,4},{4,6},{6,8},{8,10},{10,12},{12,14},{14,16},{16,18},{18... | collective-permute-start | bytes 294920 | tf_op jit(solution)/shard_map/ppermute | solution.py:24
  184.6 1.3 copy-start.9
  186.2 6.4 %collective-permute-start.8 = (f32[2,2,4,8,384]{4,3,1,0,2:T(8,128)S(1)}, f32[2,2,4,8,384]{4,3,1,0,2:T(8,128)S(1)}, u32[]{:S(2)}, u32[]{:S(2)}) collective-permute-start(f32[2,2,4,8,384]{4,3,1,0,2:T(8,128)S(1)} %fusion.26), channel_id=1, source_target_pairs={{0,1},{1,0},{2,3},{3,2},{4,5},{5,4},{6,7},{7,6},{8,9},{9,8},{10,11... | collective-permute-start | bytes 589832 | tf_op jit(solution)/shard_map/ppermute | solution.py:130
  226.4 15.7 %collective-permute-start.10 = (bf16[2,2,4,8,384]{4,3,1,0,2:T(8,128)(2,1)S(1)}, bf16[2,2,4,8,384]{4,3,1,0,2:T(8,128)(2,1)S(1)}, u32[]{:S(2)}, u32[]{:S(2)}) collective-permute-start(bf16[2,2,4,8,384]{4,3,1,0,2:T(8,128)(2,1)S(1)} %multiply_convert_fusion.1), channel_id=1, source_target_pairs={{2,0},{4,2},{6,4},{8,6},{10,8},{12,10},{14,12},{16,14},{18,16},{20... | collective-permute-start | bytes 294920 | tf_op jit(solution)/shard_map/ppermute | solution.py:25
  228.3 15.0 %collective-permute-start.9 = (bf16[2,2,4,8,384]{4,3,1,0,2:T(8,128)(2,1)S(1)}, bf16[2,2,4,8,384]{4,3,1,0,2:T(8,128)(2,1)S(1)}, u32[]{:S(2)}, u32[]{:S(2)}) collective-permute-start(bf16[2,2,4,8,384]{4,3,1,0,2:T(8,128)(2,1)S(1)} %multiply_convert_fusion.1), channel_id=1, source_target_pairs={{0,2},{2,4},{4,6},{6,8},{8,10},{10,12},{12,14},{14,16},{16,18},{18... | collective-permute-start | bytes 294920 | tf_op jit(solution)/shard_map/ppermute | solution.py:24
  243.9 1.3 copy-start.10

commit v5 on v1

--- a/solution.py
+++ b/solution.py
@@ -1,6 +1,7 @@
 import functools
 
 import jax
+import numpy as np
 import jax.numpy as jnp
 from jax import lax
 from jax.experimental import pallas as pl
@@ -74,6 +75,44 @@
     )(x, bias_full)
 
 
+def tail_kernel(h2_ref, pad_ref, taps_ref, gain_ref, wup_ref, wdown_ref, o_ref, h3_ref):
+    members, rows_lat, tokens, features = h2_ref.shape
+    taps = taps_ref[...]
+    for m in range(members):
+        for r in range(rows_lat):
+            window_sum = jnp.zeros((tokens, features), jnp.float32)
+            for k in range(taps.shape[0]):
+                window_sum = window_sum + taps[k : k + 1] * pad_ref[m, r + k].astype(jnp.float32)
+            start = (m * rows_lat + r) * tokens
+            h3_ref[start : start + tokens, :] = h2_ref[m, r] + window_sum
+    hidden3 = h3_ref[...]
+    mean_val = jnp.mean(hidden3, axis=-1, keepdims=True)
+    centered = hidden3 - mean_val
+    variance = jnp.mean(centered * centered, axis=-1, keepdims=True)
+    normed3 = (centered * lax.rsqrt(variance + epsilon) * gain_ref[...]).astype(jnp.bfloat16)
+    up = jnp.dot(normed3, wup_ref[...], preferred_element_type=jnp.float32)
+    cdf = 0.5 * (1.0 + jnp.tanh(np.sqrt(2 / np.pi).astype(np.float32) * (up + 0.044715 * (up * up * up))))
+    activated = (up * cdf).astype(jnp.bfloat16)
+    o_ref[...] = hidden3 + jnp.dot(activated, wdown_ref[...], preferred_element_type=jnp.float32)
+
+
+def block_tail(hidden2, padded, taps, gain_row, wup, wdown):
+    members, rows_lat = hidden2.shape[0], hidden2.shape[1]
+    features = hidden2.shape[-1]
+    h2 = hidden2.reshape(members, rows_lat, -1, features)
+    pad = padded.reshape(members, padded.shape[1], -1, features)
+    count = members * rows_lat * h2.shape[2]
+    vmem = pl.BlockSpec(memory_space=pltpu.VMEM)
+    out = pl.pallas_call(
+        tail_kernel,
+        out_shape=jax.ShapeDtypeStruct((count, features), jnp.float32),
+        in_specs=[vmem] * 6,
+        out_specs=vmem,
+        scratch_shapes=[pltpu.VMEM((count, features), jnp.float32)],
+    )(h2, pad, taps, gain_row.reshape(1, features), wup, wdown)
+    return out.reshape(hidden2.shape)
+
+
 def block(field, lead_index, mask_ids, params, bias_full):
     mask_tab, lead_tab, wqkv, wout, wup, wdown, gains, taps = params
     members, rows_lat, lon_local, levels, features = field.shape
@@ -102,18 +141,7 @@
     hidden2 = hidden + projected_out.reshape(hidden.shape)
     normed2 = layer_norm(hidden2, gains[1]).astype(jnp.bfloat16)
     padded = lat_halo(normed2, 2)
-    window_sum = jnp.zeros_like(hidden2)
-    for offset_row in range(5):
-        window_sum = window_sum + taps[offset_row] * padded[:, offset_row : offset_row + rows_lat].astype(
-            jnp.float32
-        )
-    hidden3 = hidden2 + window_sum
-    normed3 = layer_norm(hidden3, gains[2]).astype(jnp.bfloat16)
-    activated = jax.nn.gelu(
-        jnp.dot(normed3.reshape(-1, features), wup, preferred_element_type=jnp.float32),
-        approximate=True,
-    ).astype(jnp.bfloat16)
-    return hidden3 + jnp.dot(activated, wdown, preferred_element_type=jnp.float32).reshape(hidden.shape)
+    return block_tail(hidden2, padded, taps, gains[2], wup, wdown)
 
 
 def from_partner(array):

time: 248 us -> 261 us (1.052)
  Pallas kernels: 19 us -> 32.6 us
  local copies, waits for them, and re-layouts: 11.9 us -> 16.2 us
  matrix products: 12.2 us -> 8.93 us
  waiting for transfers between devices: 25.1 us -> 22.2 us
    pallas_call x0 -> x4, Pallas kernels: none -> 13.7 us  [block_tail(): pl.pallas_call(tail_kernel, out_shape=jax.ShapeDtypeStruct((count, featur...]
    dot_general x8 -> x0, matrix products: 3.26 us -> none  [the longest x4 1.83 us: block(): jnp.dot(normed3.reshape(-1, features), wup, preferred_element_type=jnp.fl...]
    reshape x0 -> x4, other arithmetic: none -> 2.99 us  [block_tail(): pad = padded.reshape(members, padded.shape[1], -1, features)]
    reshape x0 -> x3, local copies, waits for them, and re-layouts: none -> 2.82 us  [block_tail(): return out.reshape(hidden2.shape)]
    add x0 -> x4, local copies, waits for them, and re-layouts: none -> 2.76 us  [block(): hidden2 = hidden + projected_out.reshape(hidden.shape)]
  transfers between devices with their start and end apart: 12 -> 12, of which waited for: 12 -> 8; matrix products, arithmetic and copies ran while one was open for 3% -> 4% of each run, Pallas kernels for 0% -> 0%
where the time goes in v5:
time: 261 us; the launch traced here: 259 us
  blocking collectives  104 us (40%)
  starting transfers between devices  59.6 us (23%)
  Pallas kernels  32.6 us (12%)
  waiting for transfers between devices  22.2 us (9%)
  local copies, waits for them, and re-layouts  16.2 us (6%)
  other arithmetic  11.7 us (4%)
  matrix products  8.93 us (3%)
  between operations  4.6 us (2%)
    all_to_all x4, blocking collectives, block(): returned = lax.all_to_all(back, 'lon', 0, 0, tiled=True)  55.2 us
    all_to_all x3, blocking collectives, block(): incoming = lax.all_to_all(outgoing, 'lon', 0, 0, tiled=True)  48.4 us
    ppermute x4, starting transfers between devices, lat_halo(): before = lax.ppermute(array[:, length - width:], 'lat', up)  29 us
    pallas_call x4, Pallas kernels, attend(): pl.pallas_call(functools.partial(attention_kernel, heads=heads, head_dim=...  19 us
    ppermute x4, starting transfers between devices, lat_halo(): after = lax.ppermute(array[:, :width], 'lat', down)  13.8 us
    pallas_call x4, Pallas kernels, block_tail(): pl.pallas_call(tail_kernel, out_shape=jax.ShapeDtypeStruct((count, featur...  13.7 us
    ppermute x3, waiting for transfers between devices, from_partner(): lax.ppermute(array, 'segment', [(i, i ^ 1) for i in range(lax.axis_size('...  13.4 us
    all_to_all x1, starting transfers between devices, block(): incoming = lax.all_to_all(outgoing, 'lon', 0, 0, tiled=True)  10.2 us
  transfers between devices with their start and end apart: 12, of which 8 were waited for; matrix products, arithmetic and copies ran while one was open for 4% of the time, Pallas kernels for 0%

profile of v5, /device:TPU:1, one launch (start us, length us, event | category | flops | bytes accessed | tf_op | source)
XLA Modules:
  0.0 259.3 jit_solution(1450054954137981038)
XLA Ops:
  17.0 10.2 %all-to-all-start = ((bf16[16,32,288]{2,1,0:T(8,128)(2,1)}), bf16[16,32,288]{2,1,0:T(8,128)(2,1)S(1)}, u32[]{:S(2)}, u32[]{:S(2)}) async-start(bf16[16,32,288]{2,1,0:T(8,128)(2,1)} %bitcast.6), calls=%async_computation | async-start | bytes 786432 | tf_op jit(solution)/shard_map/all_to_all | solution.py:135
  30.4 3.3 %convolution_add_fusion = f32[24,32768]{1,0:T(8,128)} fusion(f32[24,32768]{1,0:T(8,128)S(1)} %convolution_add_fusion.1, s32[32768]{0:T(1024)S(1)} %add_select_fusion, f32[1,12,8,64]{3,2,1,0:T(8,128)S(1)} %copy-done.3, s32[]{:T(128)S(6)} %select_n.49), kind=kOutput, calls=%fused_computation.1 | convolution fusion | flops 103557632 | bytes 6434820 | tf_op jit(solution)/shard_map/dot_general | solution.py:44
  33.7 5.7 %all-to-all-done = bf16[16,32,288]{2,1,0:T(8,128)(2,1)S(1)} async-done(((bf16[16,32,288]{2,1,0:T(8,128)(2,1)}), bf16[16,32,288]{2,1,0:T(8,128)(2,1)S(1)}, u32[]{:S(2)}, u32[]{:S(2)}) %all-to-all-start) | async-done | bytes 294944 | tf_op jit(solution)/shard_map/all_to_all | solution.py:135
  40.1 4.7 %shard_map.118 = bf16[512,96]{1,0:T(8,128)(2,1)} custom-call(bf16[512,288]{1,0:T(8,128)(2,1)} %bitcast.153, f32[3,512,512]{2,1,0:T(8,128)} %bitcast.136), custom_call_target="tpu_custom_call" | custom-call | tf_op jit(solution)/shard_map/pallas_call | solution.py:70
  44.9 15.4 %all_to_all.40 = bf16[16,32,96]{2,1,0:T(8,128)(2,1)S(1)} all-to-all(bf16[16,32,96]{2,1,0:T(8,128)(2,1)} %bitcast.170), channel_id=1, replica_groups=mesh['lon'=16,'lat'=16,'segment'=2] {'lon'}, dimensions={0} | all-to-all | bytes 196608 | tf_op jit(solution)/shard_map/all_to_all | solution.py:138
  61.0 4.3 %collective-permute-start.1 = (bf16[2,2,4,8,384]{4,3,1,0,2:T(8,128)(2,1)S(1)}, bf16[2,2,4,8,384]{4,3,1,0,2:T(8,128)(2,1)S(1)}, u32[]{:S(2)}, u32[]{:S(2)}) collective-permute-start(bf16[2,2,4,8,384]{4,3,1,0,2:T(8,128)(2,1)S(1)} %multiply_convert_fusion.6), channel_id=1, source_target_pairs={{2,0},{4,2},{6,4},{8,6},{10,8},{12,10},{14,12},{16,14},{18,16},{20... | collective-permute-start | bytes 294920 | tf_op jit(solution)/shard_map/ppermute | solution.py:26
  65.3 3.9 %collective-permute-start = (bf16[2,2,4,8,384]{4,3,1,0,2:T(8,128)(2,1)S(1)}, bf16[2,2,4,8,384]{4,3,1,0,2:T(8,128)(2,1)S(1)}, u32[]{:S(2)}, u32[]{:S(2)}) collective-permute-start(bf16[2,2,4,8,384]{4,3,1,0,2:T(8,128)(2,1)S(1)} %multiply_convert_fusion.6), channel_id=1, source_target_pairs={{0,2},{2,4},{4,6},{6,8},{8,10},{10,12},{12,14},{14,16},{16,18},{18... | collective-permute-start | bytes 294920 | tf_op jit(solution)/shard_map/ppermute | solution.py:25
  71.6 3.4 %shard_map.119 = f32[128,384]{1,0:T(8,128)} custom-call(f32[2,2,32,384]{3,2,1,0:T(8,128)} %bitcast.161, bf16[2,6,32,384]{3,2,1,0:T(8,128)(2,1)} %copy_bitcast_fusion.3.pad_ref, f32[5,384]{1,0:T(8,128)} %bitcast.182, f32[1,384]{1,0:T(1,128)} %get-tuple-element.18.gain_ref, bf16[384,1536]{1,0:T(8,128)(2,1)} %bitcast.144, bf16[1536,384]{1,0:T(8,128)(2,1)} %bitcast.148), custom_call_target="tpu_custom_call" | custom-call | tf_op jit(solution)/shard_map/pallas_call | solution.py:106
  75.9 2.2 collective-permute-start.2
  78.2 5.0 %collective-permute-done.2 = f32[2,2,4,8,384]{4,3,1,0,2:T(8,128)S(1)} collective-permute-done((f32[2,2,4,8,384]{4,3,1,0,2:T(8,128)S(1)}, f32[2,2,4,8,384]{4,3,1,0,2:T(8,128)S(1)}, u32[]{:S(2)}, u32[]{:S(2)}) %collective-permute-start.2) | collective-permute-done | bytes 196640 | tf_op jit(solution)/shard_map/ppermute | solution.py:148
  84.2 17.8 %all_to_all.41 = bf16[16,32,288]{2,1,0:T(8,128)(2,1)} all-to-all(bf16[16,32,288]{2,1,0:T(8,128)(2,1)S(1)} %bitcast.157), channel_id=1, replica_groups=mesh['lon'=16,'lat'=16,'segment'=2] {'lon'}, dimensions={0} | all-to-all | bytes 589824 | tf_op jit(solution)/shard_map/all_to_all | solution.py:135
  102.0 4.7 %shard_map.120 = bf16[512,96]{1,0:T(8,128)(2,1)} custom-call(bf16[512,288]{1,0:T(8,128)(2,1)} %bitcast.155, f32[3,512,512]{2,1,0:T(8,128)} %bitcast.137), custom_call_target="tpu_custom_call" | custom-call | tf_op jit(solution)/shard_map/pallas_call | solution.py:70
  106.8 13.4 %all_to_all.42 = bf16[16,32,96]{2,1,0:T(8,128)(2,1)S(1)} all-to-all(bf16[16,32,96]{2,1,0:T(8,128)(2,1)} %bitcast.172), channel_id=1, replica_groups=mesh['lon'=16,'lat'=16,'segment'=2] {'lon'}, dimensions={0} | all-to-all | bytes 196608 | tf_op jit(solution)/shard_map/all_to_all | solution.py:138
  120.8 3.9 %collective-permute-start.4 = (bf16[2,2,4,8,384]{4,3,1,0,2:T(8,128)(2,1)S(1)}, bf16[2,2,4,8,384]{4,3,1,0,2:T(8,128)(2,1)S(1)}, u32[]{:S(2)}, u32[]{:S(2)}) collective-permute-start(bf16[2,2,4,8,384]{4,3,1,0,2:T(8,128)(2,1)S(1)} %multiply_convert_fusion.4), channel_id=1, source_target_pairs={{2,0},{4,2},{6,4},{8,6},{10,8},{12,10},{14,12},{16,14},{18,16},{20... | collective-permute-start | bytes 294920 | tf_op jit(solution)/shard_map/ppermute | solution.py:26
  124.7 4.8 %collective-permute-start.3 = (bf16[2,2,4,8,384]{4,3,1,0,2:T(8,128)(2,1)S(1)}, bf16[2,2,4,8,384]{4,3,1,0,2:T(8,128)(2,1)S(1)}, u32[]{:S(2)}, u32[]{:S(2)}) collective-permute-start(bf16[2,2,4,8,384]{4,3,1,0,2:T(8,128)(2,1)S(1)} %multiply_convert_fusion.4), channel_id=1, source_target_pairs={{0,2},{2,4},{4,6},{6,8},{8,10},{10,12},{12,14},{14,16},{16,18},{18... | collective-permute-start | bytes 294920 | tf_op jit(solution)/shard_map/ppermute | solution.py:25
  131.9 3.4 %shard_map.121 = f32[128,384]{1,0:T(8,128)} custom-call(f32[2,2,32,384]{3,2,1,0:T(8,128)} %bitcast.162, bf16[2,6,32,384]{3,2,1,0:T(8,128)(2,1)} %copy_bitcast_fusion.2.pad_ref, f32[5,384]{1,0:T(8,128)} %bitcast.183, f32[1,384]{1,0:T(1,128)} %get-tuple-element.18.gain_ref, bf16[384,1536]{1,0:T(8,128)(2,1)} %bitcast.145, bf16[1536,384]{1,0:T(8,128)(2,1)} %bitcast.149), custom_call_target="tpu_custom_call" | custom-call | tf_op jit(solution)/shard_map/pallas_call | solution.py:106
  136.3 2.2 collective-permute-start.5
  138.5 4.2 %collective-permute-done.5 = f32[2,2,4,8,384]{4,3,1,0,2:T(8,128)S(1)} collective-permute-done((f32[2,2,4,8,384]{4,3,1,0,2:T(8,128)S(1)}, f32[2,2,4,8,384]{4,3,1,0,2:T(8,128)S(1)}, u32[]{:S(2)}, u32[]{:S(2)}) %collective-permute-start.5) | collective-permute-done | bytes 196640 | tf_op jit(solution)/shard_map/ppermute | solution.py:148
  143.8 16.2 %all_to_all.43 = bf16[16,32,288]{2,1,0:T(8,128)(2,1)} all-to-all(bf16[16,32,288]{2,1,0:T(8,128)(2,1)S(1)} %bitcast.158), channel_id=1, replica_groups=mesh['lon'=16,'lat'=16,'segment'=2] {'lon'}, dimensions={0} | all-to-all | bytes 589824 | tf_op jit(solution)/shard_map/all_to_all | solution.py:135
  160.0 4.7 %shard_map.122 = bf16[512,96]{1,0:T(8,128)(2,1)} custom-call(bf16[512,288]{1,0:T(8,128)(2,1)} %bitcast.156, f32[3,512,512]{2,1,0:T(8,128)} %bitcast.138), custom_call_target="tpu_custom_call" | custom-call | tf_op jit(solution)/shard_map/pallas_call | solution.py:70
  164.7 13.5 %all_to_all.44 = bf16[16,32,96]{2,1,0:T(8,128)(2,1)S(1)} all-to-all(bf16[16,32,96]{2,1,0:T(8,128)(2,1)} %bitcast.174), channel_id=1, replica_groups=mesh['lon'=16,'lat'=16,'segment'=2] {'lon'}, dimensions={0} | all-to-all | bytes 196608 | tf_op jit(solution)/shard_map/all_to_all | solution.py:138
  178.9 3.7 %collective-permute-start.7 = (bf16[2,2,4,8,384]{4,3,1,0,2:T(8,128)(2,1)S(1)}, bf16[2,2,4,8,384]{4,3,1,0,2:T(8,128)(2,1)S(1)}, u32[]{:S(2)}, u32[]{:S(2)}) collective-permute-start(bf16[2,2,4,8,384]{4,3,1,0,2:T(8,128)(2,1)S(1)} %multiply_convert_fusion.2), channel_id=1, source_target_pairs={{2,0},{4,2},{6,4},{8,6},{10,8},{12,10},{14,12},{16,14},{18,16},{20... | collective-permute-start | bytes 294920 | tf_op jit(solution)/shard_map/ppermute | solution.py:26
  182.6 7.3 %collective-permute-start.6 = (bf16[2,2,4,8,384]{4,3,1,0,2:T(8,128)(2,1)S(1)}, bf16[2,2,4,8,384]{4,3,1,0,2:T(8,128)(2,1)S(1)}, u32[]{:S(2)}, u32[]{:S(2)}) collective-permute-start(bf16[2,2,4,8,384]{4,3,1,0,2:T(8,128)(2,1)S(1)} %multiply_convert_fusion.2), channel_id=1, source_target_pairs={{0,2},{2,4},{4,6},{6,8},{8,10},{10,12},{12,14},{14,16},{16,18},{18... | collective-permute-start | bytes 294920 | tf_op jit(solution)/shard_map/ppermute | solution.py:25
  192.3 3.4 %shard_map.123 = f32[128,384]{1,0:T(8,128)} custom-call(f32[2,2,32,384]{3,2,1,0:T(8,128)} %bitcast.163, bf16[2,6,32,384]{3,2,1,0:T(8,128)(2,1)} %copy_bitcast_fusion.1.pad_ref, f32[5,384]{1,0:T(8,128)} %bitcast.184, f32[1,384]{1,0:T(1,128)} %get-tuple-element.18.gain_ref, bf16[384,1536]{1,0:T(8,128)(2,1)} %bitcast.146, bf16[1536,384]{1,0:T(8,128)(2,1)} %bitcast.150), custom_call_target="tpu_custom_call" | custom-call | tf_op jit(solution)/shard_map/pallas_call | solution.py:106
  196.7 2.2 collective-permute-start.8
  198.8 4.2 %collective-permute-done.8 = f32[2,2,4,8,384]{4,3,1,0,2:T(8,128)S(1)} collective-permute-done((f32[2,2,4,8,384]{4,3,1,0,2:T(8,128)S(1)}, f32[2,2,4,8,384]{4,3,1,0,2:T(8,128)S(1)}, u32[]{:S(2)}, u32[]{:S(2)}) %collective-permute-start.8) | collective-permute-done | bytes 196640 | tf_op jit(solution)/shard_map/ppermute | solution.py:148
  204.2 14.3 %all_to_all.45 = bf16[16,32,288]{2,1,0:T(8,128)(2,1)} all-to-all(bf16[16,32,288]{2,1,0:T(8,128)(2,1)S(1)} %bitcast.159), channel_id=1, replica_groups=mesh['lon'=16,'lat'=16,'segment'=2] {'lon'}, dimensions={0} | all-to-all | bytes 589824 | tf_op jit(solution)/shard_map/all_to_all | solution.py:135
  218.5 4.7 %shard_map.124 = bf16[512,96]{1,0:T(8,128)(2,1)} custom-call(bf16[512,288]{1,0:T(8,128)(2,1)} %bitcast.154, f32[3,512,512]{2,1,0:T(8,128)} %bitcast.139), custom_call_target="tpu_custom_call" | custom-call | tf_op jit(solution)/shard_map/pallas_call | solution.py:70
  223.3 13.0 %all_to_all.46 = bf16[16,32,96]{2,1,0:T(8,128)(2,1)S(1)} all-to-all(bf16[16,32,96]{2,1,0:T(8,128)(2,1)} %bitcast.169), channel_id=1, replica_groups=mesh['lon'=16,'lat'=16,'segment'=2] {'lon'}, dimensions={0} | all-to-all | bytes 196608 | tf_op jit(solution)/shard_map/all_to_all | solution.py:138
  237.0 1.9 collective-permute-start.10
  238.9 13.0 %collective-permute-start.9 = (bf16[2,2,4,8,384]{4,3,1,0,2:T(8,128)(2,1)S(1)}, bf16[2,2,4,8,384]{4,3,1,0,2:T(8,128)(2,1)S(1)}, u32[]{:S(2)}, u32[]{:S(2)}) collective-permute-start(bf16[2,2,4,8,384]{4,3,1,0,2:T(8,128)(2,1)S(1)} %multiply_convert_fusion), channel_id=1, source_target_pairs={{0,2},{2,4},{4,6},{6,8},{8,10},{10,12},{12,14},{14,16},{16,18},{18... | collective-permute-start | bytes 294920 | tf_op jit(solution)/shard_map/ppermute | solution.py:25
  254.3 3.4 %shard_map.125 = f32[128,384]{1,0:T(8,128)} custom-call(f32[2,2,32,384]{3,2,1,0:T(8,128)} %bitcast.160, bf16[2,6,32,384]{3,2,1,0:T(8,128)(2,1)} %copy_bitcast_fusion.pad_ref, f32[5,384]{1,0:T(8,128)} %bitcast.185, f32[1,384]{1,0:T(1,128)} %get-tuple-element.18.gain_ref, bf16[384,1536]{1,0:T(8,128)(2,1)} %bitcast.147, bf16[1536,384]{1,0:T(8,128)(2,1)} %bitcast.151), custom_call_target="tpu_custom_call" | custom-call | tf_op jit(solution)/shard_map/pallas_call | solution.py:106
  (108 shorter events, 36.6 us)
Async XLA Ops:
  0.0 60.3 %copy-start = (bf16[1,384,384]{2,1,0:T(8,128)(2,1)S(1)}, bf16[1,384,384]{2,1,0:T(8,128)(2,1)}, u32[]{:S(2)}) copy-start(bf16[1,384,384]{2,1,0:T(8,128)(2,1)} %param.20) | copy-start | bytes 884740
  13.7 13.7 %copy-start.3 = (f32[1,12,8,64]{3,2,1,0:T(8,128)S(1)}, f32[1,12,8,64]{3,2,1,0:T(8,128)}, u32[]{:S(2)}) copy-start(f32[1,12,8,64]{3,2,1,0:T(8,128)} %param.25) | copy-start | bytes 73732
  17.0 22.4 %all-to-all-start = ((bf16[16,32,288]{2,1,0:T(8,128)(2,1)}), bf16[16,32,288]{2,1,0:T(8,128)(2,1)S(1)}, u32[]{:S(2)}, u32[]{:S(2)}) async-start(bf16[16,32,288]{2,1,0:T(8,128)(2,1)} %bitcast.6), calls=%async_computation | async-start | bytes 786432 | tf_op jit(solution)/shard_map/all_to_all | solution.py:135
  33.7 26.8 %copy-start.1 = (f32[2,2,4,8,384]{4,3,2,1,0:T(8,128)S(1)}, f32[2,2,4,8,384]{4,3,2,1,0:T(8,128)}, u32[]{:S(2)}) copy-start(f32[2,2,4,8,384]{4,3,2,1,0:T(8,128)} %param.14) | copy-start | bytes 589828
  33.7 35.5 %copy-start.4 = (f32[1,5,384]{2,0,1:T(1,128)S(1)}, f32[1,5,384]{2,0,1:T(1,128)}, u32[]{:S(2)}) copy-start(f32[1,5,384]{2,0,1:T(1,128)} %param.24) | copy-start | bytes 23044
  39.4 0.7 copy-start.2
  61.0 9.5 %collective-permute-start.1 = (bf16[2,2,4,8,384]{4,3,1,0,2:T(8,128)(2,1)S(1)}, bf16[2,2,4,8,384]{4,3,1,0,2:T(8,128)(2,1)S(1)}, u32[]{:S(2)}, u32[]{:S(2)}) collective-permute-start(bf16[2,2,4,8,384]{4,3,1,0,2:T(8,128)(2,1)S(1)} %multiply_convert_fusion.6), channel_id=1, source_target_pairs={{2,0},{4,2},{6,4},{8,6},{10,8},{12,10},{14,12},{16,14},{18,16},{20... | collective-permute-start | bytes 294920 | tf_op jit(solution)/shard_map/ppermute | solution.py:26
  65.3 5.5 %collective-permute-start = (bf16[2,2,4,8,384]{4,3,1,0,2:T(8,128)(2,1)S(1)}, bf16[2,2,4,8,384]{4,3,1,0,2:T(8,128)(2,1)S(1)}, u32[]{:S(2)}, u32[]{:S(2)}) collective-permute-start(bf16[2,2,4,8,384]{4,3,1,0,2:T(8,128)(2,1)S(1)} %multiply_convert_fusion.6), channel_id=1, source_target_pairs={{0,2},{2,4},{4,6},{6,8},{8,10},{10,12},{12,14},{14,16},{16,18},{18... | collective-permute-start | bytes 294920 | tf_op jit(solution)/shard_map/ppermute | solution.py:25
  75.9 7.2 %collective-permute-start.2 = (f32[2,2,4,8,384]{4,3,1,0,2:T(8,128)S(1)}, f32[2,2,4,8,384]{4,3,1,0,2:T(8,128)S(1)}, u32[]{:S(2)}, u32[]{:S(2)}) collective-permute-start(f32[2,2,4,8,384]{4,3,1,0,2:T(8,128)S(1)} %copy.57), channel_id=1, source_target_pairs={{0,1},{1,0},{2,3},{3,2},{4,5},{5,4},{6,7},{7,6},{8,9},{9,8},{10,11... | collective-permute-start | bytes 589832 | tf_op jit(solution)/shard_map/ppermute | solution.py:148
  120.8 9.4 %collective-permute-start.4 = (bf16[2,2,4,8,384]{4,3,1,0,2:T(8,128)(2,1)S(1)}, bf16[2,2,4,8,384]{4,3,1,0,2:T(8,128)(2,1)S(1)}, u32[]{:S(2)}, u32[]{:S(2)}) collective-permute-start(bf16[2,2,4,8,384]{4,3,1,0,2:T(8,128)(2,1)S(1)} %multiply_convert_fusion.4), channel_id=1, source_target_pairs={{2,0},{4,2},{6,4},{8,6},{10,8},{12,10},{14,12},{16,14},{18,16},{20... | collective-permute-start | bytes 294920 | tf_op jit(solution)/shard_map/ppermute | solution.py:26
  124.7 6.4 %collective-permute-start.3 = (bf16[2,2,4,8,384]{4,3,1,0,2:T(8,128)(2,1)S(1)}, bf16[2,2,4,8,384]{4,3,1,0,2:T(8,128)(2,1)S(1)}, u32[]{:S(2)}, u32[]{:S(2)}) collective-permute-start(bf16[2,2,4,8,384]{4,3,1,0,2:T(8,128)(2,1)S(1)} %multiply_convert_fusion.4), channel_id=1, source_target_pairs={{0,2},{2,4},{4,6},{6,8},{8,10},{10,12},{12,14},{14,16},{16,18},{18... | collective-permute-start | bytes 294920 | tf_op jit(solution)/shard_map/ppermute | solution.py:25
  136.3 6.4 %collective-permute-start.5 = (f32[2,2,4,8,384]{4,3,1,0,2:T(8,128)S(1)}, f32[2,2,4,8,384]{4,3,1,0,2:T(8,128)S(1)}, u32[]{:S(2)}, u32[]{:S(2)}) collective-permute-start(f32[2,2,4,8,384]{4,3,1,0,2:T(8,128)S(1)} %copy.63), channel_id=1, source_target_pairs={{0,1},{1,0},{2,3},{3,2},{4,5},{5,4},{6,7},{7,6},{8,9},{9,8},{10,11... | collective-permute-start | bytes 589832 | tf_op jit(solution)/shard_map/ppermute | solution.py:148
  178.9 11.7 %collective-permute-start.7 = (bf16[2,2,4,8,384]{4,3,1,0,2:T(8,128)(2,1)S(1)}, bf16[2,2,4,8,384]{4,3,1,0,2:T(8,128)(2,1)S(1)}, u32[]{:S(2)}, u32[]{:S(2)}) collective-permute-start(bf16[2,2,4,8,384]{4,3,1,0,2:T(8,128)(2,1)S(1)} %multiply_convert_fusion.2), channel_id=1, source_target_pairs={{2,0},{4,2},{6,4},{8,6},{10,8},{12,10},{14,12},{16,14},{18,16},{20... | collective-permute-start | bytes 294920 | tf_op jit(solution)/shard_map/ppermute | solution.py:26
  182.6 8.9 %collective-permute-start.6 = (bf16[2,2,4,8,384]{4,3,1,0,2:T(8,128)(2,1)S(1)}, bf16[2,2,4,8,384]{4,3,1,0,2:T(8,128)(2,1)S(1)}, u32[]{:S(2)}, u32[]{:S(2)}) collective-permute-start(bf16[2,2,4,8,384]{4,3,1,0,2:T(8,128)(2,1)S(1)} %multiply_convert_fusion.2), channel_id=1, source_target_pairs={{0,2},{2,4},{4,6},{6,8},{8,10},{10,12},{12,14},{14,16},{16,18},{18... | collective-permute-start | bytes 294920 | tf_op jit(solution)/shard_map/ppermute | solution.py:25
  196.7 6.4 %collective-permute-start.8 = (f32[2,2,4,8,384]{4,3,1,0,2:T(8,128)S(1)}, f32[2,2,4,8,384]{4,3,1,0,2:T(8,128)S(1)}, u32[]{:S(2)}, u32[]{:S(2)}) collective-permute-start(f32[2,2,4,8,384]{4,3,1,0,2:T(8,128)S(1)} %copy.69), channel_id=1, source_target_pairs={{0,1},{1,0},{2,3},{3,2},{4,5},{5,4},{6,7},{7,6},{8,9},{9,8},{10,11... | collective-permute-start | bytes 589832 | tf_op jit(solution)/shard_map/ppermute | solution.py:148
  237.0 15.6 %collective-permute-start.10 = (bf16[2,2,4,8,384]{4,3,1,0,2:T(8,128)(2,1)S(1)}, bf16[2,2,4,8,384]{4,3,1,0,2:T(8,128)(2,1)S(1)}, u32[]{:S(2)}, u32[]{:S(2)}) collective-permute-start(bf16[2,2,4,8,384]{4,3,1,0,2:T(8,128)(2,1)S(1)} %multiply_convert_fusion), channel_id=1, source_target_pairs={{2,0},{4,2},{6,4},{8,6},{10,8},{12,10},{14,12},{16,14},{18,16},{20... | collective-permute-start | bytes 294920 | tf_op jit(solution)/shard_map/ppermute | solution.py:26
  238.9 14.6 %collective-permute-start.9 = (bf16[2,2,4,8,384]{4,3,1,0,2:T(8,128)(2,1)S(1)}, bf16[2,2,4,8,384]{4,3,1,0,2:T(8,128)(2,1)S(1)}, u32[]{:S(2)}, u32[]{:S(2)}) collective-permute-start(bf16[2,2,4,8,384]{4,3,1,0,2:T(8,128)(2,1)S(1)} %multiply_convert_fusion), channel_id=1, source_target_pairs={{0,2},{2,4},{4,6},{6,8},{8,10},{10,12},{12,14},{14,16},{16,18},{18... | collective-permute-start | bytes 294920 | tf_op jit(solution)/shard_map/ppermute | solution.py:25

commit v6 on v1

--- a/solution.py
+++ b/solution.py
@@ -84,7 +84,9 @@
     tokens_local = lon_local * levels
     combos = members * rows_lat
 
-    mask_embed = jnp.take(mask_tab, mask_ids, axis=0)
+    kinds = mask_tab.shape[0]
+    mask_onehot = (mask_ids[..., None] == jnp.arange(kinds, dtype=jnp.int32)).astype(jnp.float32)
+    mask_embed = jnp.dot(mask_onehot, mask_tab, precision=lax.Precision.HIGHEST)
     lead_row = lax.dynamic_index_in_dim(lead_tab, lead_index, axis=0, keepdims=False)
     hidden = field + mask_embed[None, :, :, None, :] + lead_row
     normed = layer_norm(hidden, gains[0]).astype(jnp.bfloat16)

time: 248 us -> 246 us (level)
  no operation moved by 1% of the time
where the time goes in v6:
time: 246 us; the launch traced here: 245 us
  blocking collectives  102 us (41%)
  starting transfers between devices  61.6 us (25%)
  waiting for transfers between devices  25.2 us (10%)
  Pallas kernels  19 us (8%)
  matrix products  13.1 us (5%)
  local copies, waits for them, and re-layouts  10.5 us (4%)
  other arithmetic  8.92 us (4%)
  between operations  4.81 us (2%)
    all_to_all x4, blocking collectives, block(): returned = lax.all_to_all(back, 'lon', 0, 0, tiled=True)  55.3 us
    all_to_all x3, blocking collectives, block(): incoming = lax.all_to_all(outgoing, 'lon', 0, 0, tiled=True)  46.6 us
    ppermute x4, starting transfers between devices, lat_halo(): before = lax.ppermute(array[:, length - width:], 'lat', up)  31.7 us
    pallas_call x4, Pallas kernels, attend(): pl.pallas_call(functools.partial(attention_kernel, heads=heads, head_dim=...  19 us
    ppermute x4, starting transfers between devices, lat_halo(): after = lax.ppermute(array[:, :width], 'lat', down)  13.2 us
    ppermute x3, waiting for transfers between devices, from_partner(): lax.ppermute(array, 'segment', [(i, i ^ 1) for i in range(lax.axis_size('...  13.1 us
    all_to_all x1, starting transfers between devices, block(): incoming = lax.all_to_all(outgoing, 'lon', 0, 0, tiled=True)  10.2 us
    ppermute x3, starting transfers between devices, from_partner(): lax.ppermute(array, 'segment', [(i, i ^ 1) for i in range(lax.axis_size('...  6.5 us
  transfers between devices with their start and end apart: 12, of which 12 were waited for; matrix products, arithmetic and copies ran while one was open for 3% of the time, Pallas kernels for 0%

profile of v6, /device:TPU:1, one launch (start us, length us, event | category | flops | bytes accessed | tf_op | source)
XLA Modules:
  0.0 245.0 jit_solution(3458187961558896193)
XLA Ops:
  0.0 1.5 fusion.116
  14.2 10.2 %all-to-all-start = ((bf16[16,32,288]{2,1,0:T(8,128)(2,1)}), bf16[16,32,288]{2,1,0:T(8,128)(2,1)S(1)}, u32[]{:S(2)}, u32[]{:S(2)}) async-start(bf16[16,32,288]{2,1,0:T(8,128)(2,1)} %bitcast.7), calls=%async_computation | async-start | bytes 786432 | tf_op jit(solution)/shard_map/all_to_all | solution.py:98
  24.7 1.3 fusion
  26.1 1.6 convolution_add_fusion.1
  27.7 3.3 %convolution_add_fusion = f32[24,32768]{1,0:T(8,128)} fusion(f32[24,32768]{1,0:T(8,128)S(1)} %convolution_add_fusion.1, s32[32768]{0:T(1024)S(1)} %add_select_fusion, f32[1,12,8,64]{3,2,1,0:T(8,128)S(1)} %copy-done.5, s32[]{:T(128)S(6)} %select_n.42), kind=kOutput, calls=%fused_computation | convolution fusion | flops 103557632 | bytes 6434820 | tf_op jit(solution)/shard_map/dot_general | solution.py:43
  31.0 5.7 %all-to-all-done = bf16[16,32,288]{2,1,0:T(8,128)(2,1)S(1)} async-done(((bf16[16,32,288]{2,1,0:T(8,128)(2,1)}), bf16[16,32,288]{2,1,0:T(8,128)(2,1)S(1)}, u32[]{:S(2)}, u32[]{:S(2)}) %all-to-all-start) | async-done | bytes 294944 | tf_op jit(solution)/shard_map/all_to_all | solution.py:98
  37.4 4.8 %shard_map.118 = bf16[512,96]{1,0:T(8,128)(2,1)} custom-call(bf16[512,288]{1,0:T(8,128)(2,1)} %bitcast.179, f32[3,512,512]{2,1,0:T(8,128)} %bitcast.166), custom_call_target="tpu_custom_call" | custom-call | tf_op jit(solution)/shard_map/pallas_call | solution.py:69
  42.2 15.4 %all_to_all.40 = bf16[16,32,96]{2,1,0:T(8,128)(2,1)S(1)} all-to-all(bf16[16,32,96]{2,1,0:T(8,128)(2,1)} %bitcast.187), channel_id=1, replica_groups=mesh['lon'=16,'lat'=16,'segment'=2] {'lon'}, dimensions={0} | all-to-all | bytes 196608 | tf_op jit(solution)/shard_map/all_to_all | solution.py:101
  58.4 4.4 %collective-permute-start.1 = (bf16[2,2,4,8,384]{4,3,1,0,2:T(8,128)(2,1)S(1)}, bf16[2,2,4,8,384]{4,3,1,0,2:T(8,128)(2,1)S(1)}, u32[]{:S(2)}, u32[]{:S(2)}) collective-permute-start(bf16[2,2,4,8,384]{4,3,1,0,2:T(8,128)(2,1)S(1)} %multiply_convert_fusion.10), channel_id=1, source_target_pairs={{2,0},{4,2},{6,4},{8,6},{10,8},{12,10},{14,12},{16,14},{18,16},{20... | collective-permute-start | bytes 294920 | tf_op jit(solution)/shard_map/ppermute | solution.py:25
  62.8 3.9 %collective-permute-start = (bf16[2,2,4,8,384]{4,3,1,0,2:T(8,128)(2,1)S(1)}, bf16[2,2,4,8,384]{4,3,1,0,2:T(8,128)(2,1)S(1)}, u32[]{:S(2)}, u32[]{:S(2)}) collective-permute-start(bf16[2,2,4,8,384]{4,3,1,0,2:T(8,128)(2,1)S(1)} %multiply_convert_fusion.10), channel_id=1, source_target_pairs={{0,2},{2,4},{4,6},{6,8},{8,10},{10,12},{12,14},{14,16},{16,18},{18... | collective-permute-start | bytes 294920 | tf_op jit(solution)/shard_map/ppermute | solution.py:24
  67.0 1.3 collective-permute-done
  70.5 2.2 collective-permute-start.2
  72.7 4.6 %collective-permute-done.2 = f32[2,2,4,8,384]{4,3,1,0,2:T(8,128)S(1)} collective-permute-done((f32[2,2,4,8,384]{4,3,1,0,2:T(8,128)S(1)}, f32[2,2,4,8,384]{4,3,1,0,2:T(8,128)S(1)}, u32[]{:S(2)}, u32[]{:S(2)}) %collective-permute-start.2) | collective-permute-done | bytes 196640 | tf_op jit(solution)/shard_map/ppermute | solution.py:122
  78.4 17.3 %all_to_all.41 = bf16[16,32,288]{2,1,0:T(8,128)(2,1)} all-to-all(bf16[16,32,288]{2,1,0:T(8,128)(2,1)S(1)} %bitcast.183), channel_id=1, replica_groups=mesh['lon'=16,'lat'=16,'segment'=2] {'lon'}, dimensions={0} | all-to-all | bytes 589824 | tf_op jit(solution)/shard_map/all_to_all | solution.py:98
  95.6 4.7 %shard_map.119 = bf16[512,96]{1,0:T(8,128)(2,1)} custom-call(bf16[512,288]{1,0:T(8,128)(2,1)} %bitcast.181, f32[3,512,512]{2,1,0:T(8,128)} %bitcast.167), custom_call_target="tpu_custom_call" | custom-call | tf_op jit(solution)/shard_map/pallas_call | solution.py:69
  100.4 13.4 %all_to_all.42 = bf16[16,32,96]{2,1,0:T(8,128)(2,1)S(1)} all-to-all(bf16[16,32,96]{2,1,0:T(8,128)(2,1)} %bitcast.189), channel_id=1, replica_groups=mesh['lon'=16,'lat'=16,'segment'=2] {'lon'}, dimensions={0} | all-to-all | bytes 196608 | tf_op jit(solution)/shard_map/all_to_all | solution.py:101
  114.5 3.9 %collective-permute-start.4 = (bf16[2,2,4,8,384]{4,3,1,0,2:T(8,128)(2,1)S(1)}, bf16[2,2,4,8,384]{4,3,1,0,2:T(8,128)(2,1)S(1)}, u32[]{:S(2)}, u32[]{:S(2)}) collective-permute-start(bf16[2,2,4,8,384]{4,3,1,0,2:T(8,128)(2,1)S(1)} %multiply_convert_fusion.7), channel_id=1, source_target_pairs={{2,0},{4,2},{6,4},{8,6},{10,8},{12,10},{14,12},{16,14},{18,16},{20... | collective-permute-start | bytes 294920 | tf_op jit(solution)/shard_map/ppermute | solution.py:25
  118.4 5.6 %collective-permute-start.3 = (bf16[2,2,4,8,384]{4,3,1,0,2:T(8,128)(2,1)S(1)}, bf16[2,2,4,8,384]{4,3,1,0,2:T(8,128)(2,1)S(1)}, u32[]{:S(2)}, u32[]{:S(2)}) collective-permute-start(bf16[2,2,4,8,384]{4,3,1,0,2:T(8,128)(2,1)S(1)} %multiply_convert_fusion.7), channel_id=1, source_target_pairs={{0,2},{2,4},{4,6},{6,8},{8,10},{10,12},{12,14},{14,16},{16,18},{18... | collective-permute-start | bytes 294920 | tf_op jit(solution)/shard_map/ppermute | solution.py:24
  127.8 2.2 collective-permute-start.5
  130.0 4.2 %collective-permute-done.5 = f32[2,2,4,8,384]{4,3,1,0,2:T(8,128)S(1)} collective-permute-done((f32[2,2,4,8,384]{4,3,1,0,2:T(8,128)S(1)}, f32[2,2,4,8,384]{4,3,1,0,2:T(8,128)S(1)}, u32[]{:S(2)}, u32[]{:S(2)}) %collective-permute-start.5) | collective-permute-done | bytes 196640 | tf_op jit(solution)/shard_map/ppermute | solution.py:122
  135.3 15.4 %all_to_all.43 = bf16[16,32,288]{2,1,0:T(8,128)(2,1)} all-to-all(bf16[16,32,288]{2,1,0:T(8,128)(2,1)S(1)} %bitcast.184), channel_id=1, replica_groups=mesh['lon'=16,'lat'=16,'segment'=2] {'lon'}, dimensions={0} | all-to-all | bytes 589824 | tf_op jit(solution)/shard_map/all_to_all | solution.py:98
  150.7 4.7 %shard_map.120 = bf16[512,96]{1,0:T(8,128)(2,1)} custom-call(bf16[512,288]{1,0:T(8,128)(2,1)} %bitcast.182, f32[3,512,512]{2,1,0:T(8,128)} %bitcast.168), custom_call_target="tpu_custom_call" | custom-call | tf_op jit(solution)/shard_map/pallas_call | solution.py:69
  155.4 13.6 %all_to_all.44 = bf16[16,32,96]{2,1,0:T(8,128)(2,1)S(1)} all-to-all(bf16[16,32,96]{2,1,0:T(8,128)(2,1)} %bitcast.191), channel_id=1, replica_groups=mesh['lon'=16,'lat'=16,'segment'=2] {'lon'}, dimensions={0} | all-to-all | bytes 196608 | tf_op jit(solution)/shard_map/all_to_all | solution.py:101
  169.7 3.1 %collective-permute-start.7 = (bf16[2,2,4,8,384]{4,3,1,0,2:T(8,128)(2,1)S(1)}, bf16[2,2,4,8,384]{4,3,1,0,2:T(8,128)(2,1)S(1)}, u32[]{:S(2)}, u32[]{:S(2)}) collective-permute-start(bf16[2,2,4,8,384]{4,3,1,0,2:T(8,128)(2,1)S(1)} %multiply_convert_fusion.4), channel_id=1, source_target_pairs={{2,0},{4,2},{6,4},{8,6},{10,8},{12,10},{14,12},{16,14},{18,16},{20... | collective-permute-start | bytes 294920 | tf_op jit(solution)/shard_map/ppermute | solution.py:25
  172.8 8.7 %collective-permute-start.6 = (bf16[2,2,4,8,384]{4,3,1,0,2:T(8,128)(2,1)S(1)}, bf16[2,2,4,8,384]{4,3,1,0,2:T(8,128)(2,1)S(1)}, u32[]{:S(2)}, u32[]{:S(2)}) collective-permute-start(bf16[2,2,4,8,384]{4,3,1,0,2:T(8,128)(2,1)S(1)} %multiply_convert_fusion.4), channel_id=1, source_target_pairs={{0,2},{2,4},{4,6},{6,8},{8,10},{10,12},{12,14},{14,16},{16,18},{18... | collective-permute-start | bytes 294920 | tf_op jit(solution)/shard_map/ppermute | solution.py:24
  185.3 2.1 collective-permute-start.8
  187.4 4.3 %collective-permute-done.8 = f32[2,2,4,8,384]{4,3,1,0,2:T(8,128)S(1)} collective-permute-done((f32[2,2,4,8,384]{4,3,1,0,2:T(8,128)S(1)}, f32[2,2,4,8,384]{4,3,1,0,2:T(8,128)S(1)}, u32[]{:S(2)}, u32[]{:S(2)}) %collective-permute-start.8) | collective-permute-done | bytes 196640 | tf_op jit(solution)/shard_map/ppermute | solution.py:122
  192.8 14.0 %all_to_all.45 = bf16[16,32,288]{2,1,0:T(8,128)(2,1)} all-to-all(bf16[16,32,288]{2,1,0:T(8,128)(2,1)S(1)} %bitcast.185), channel_id=1, replica_groups=mesh['lon'=16,'lat'=16,'segment'=2] {'lon'}, dimensions={0} | all-to-all | bytes 589824 | tf_op jit(solution)/shard_map/all_to_all | solution.py:98
  206.8 4.7 %shard_map.121 = bf16[512,96]{1,0:T(8,128)(2,1)} custom-call(bf16[512,288]{1,0:T(8,128)(2,1)} %bitcast.180, f32[3,512,512]{2,1,0:T(8,128)} %bitcast.169), custom_call_target="tpu_custom_call" | custom-call | tf_op jit(solution)/shard_map/pallas_call | solution.py:69
  211.5 12.9 %all_to_all.46 = bf16[16,32,96]{2,1,0:T(8,128)(2,1)S(1)} all-to-all(bf16[16,32,96]{2,1,0:T(8,128)(2,1)} %bitcast.186), channel_id=1, replica_groups=mesh['lon'=16,'lat'=16,'segment'=2] {'lon'}, dimensions={0} | all-to-all | bytes 196608 | tf_op jit(solution)/shard_map/all_to_all | solution.py:101
  225.2 1.9 collective-permute-start.10
  227.1 13.4 %collective-permute-start.9 = (bf16[2,2,4,8,384]{4,3,1,0,2:T(8,128)(2,1)S(1)}, bf16[2,2,4,8,384]{4,3,1,0,2:T(8,128)(2,1)S(1)}, u32[]{:S(2)}, u32[]{:S(2)}) collective-permute-start(bf16[2,2,4,8,384]{4,3,1,0,2:T(8,128)(2,1)S(1)} %multiply_convert_fusion.1), channel_id=1, source_target_pairs={{0,2},{2,4},{4,6},{6,8},{8,10},{10,12},{12,14},{14,16},{16,18},{18... | collective-permute-start | bytes 294920 | tf_op jit(solution)/shard_map/ppermute | solution.py:24
  (130 shorter events, 29.9 us)
Async XLA Ops:
  0.0 68.8 %copy-start = (bf16[1,384,1536]{2,1,0:T(8,128)(2,1)S(1)}, bf16[1,384,1536]{2,1,0:T(8,128)(2,1)}, u32[]{:S(2)}) copy-start(bf16[1,384,1536]{2,1,0:T(8,128)(2,1)} %param.19) | copy-start | bytes 3538948
  0.0 11.9 %copy-start.4 = (bf16[1,384,1152]{2,1,0:T(8,128)(2,1)S(1)}, bf16[1,384,1152]{2,1,0:T(8,128)(2,1)}, u32[]{:S(2)}) copy-start(bf16[1,384,1152]{2,1,0:T(8,128)(2,1)} %param.17) | copy-start | bytes 2654212
  13.3 11.4 %copy-start.5 = (f32[1,12,8,64]{3,2,1,0:T(8,128)S(1)}, f32[1,12,8,64]{3,2,1,0:T(8,128)}, u32[]{:S(2)}) copy-start(f32[1,12,8,64]{3,2,1,0:T(8,128)} %param.23) | copy-start | bytes 73732
  14.2 22.4 %all-to-all-start = ((bf16[16,32,288]{2,1,0:T(8,128)(2,1)}), bf16[16,32,288]{2,1,0:T(8,128)(2,1)S(1)}, u32[]{:S(2)}, u32[]{:S(2)}) async-start(bf16[16,32,288]{2,1,0:T(8,128)(2,1)} %bitcast.7), calls=%async_computation | async-start | bytes 786432 | tf_op jit(solution)/shard_map/all_to_all | solution.py:98
  36.7 0.7 copy-start.3
  37.4 20.2 %copy-start.1 = (bf16[1,384,384]{2,1,0:T(8,128)(2,1)S(1)}, bf16[1,384,384]{2,1,0:T(8,128)(2,1)}, u32[]{:S(2)}) copy-start(bf16[1,384,384]{2,1,0:T(8,128)(2,1)} %param.18) | copy-start | bytes 884740
  37.4 20.5 %copy-start.2 = (f32[2,2,4,8,384]{4,3,2,1,0:T(8,128)S(1)}, f32[2,2,4,8,384]{4,3,2,1,0:T(8,128)}, u32[]{:S(2)}) copy-start(f32[2,2,4,8,384]{4,3,2,1,0:T(8,128)} %param.12) | copy-start | bytes 589828
  42.2 24.5 %copy-start.6 = (f32[1,5,384]{2,0,1:T(1,128)S(1)}, f32[1,5,384]{2,0,1:T(1,128)}, u32[]{:S(2)}) copy-start(f32[1,5,384]{2,0,1:T(1,128)} %param.22) | copy-start | bytes 23044
  58.4 8.6 %collective-permute-start.1 = (bf16[2,2,4,8,384]{4,3,1,0,2:T(8,128)(2,1)S(1)}, bf16[2,2,4,8,384]{4,3,1,0,2:T(8,128)(2,1)S(1)}, u32[]{:S(2)}, u32[]{:S(2)}) collective-permute-start(bf16[2,2,4,8,384]{4,3,1,0,2:T(8,128)(2,1)S(1)} %multiply_convert_fusion.10), channel_id=1, source_target_pairs={{2,0},{4,2},{6,4},{8,6},{10,8},{12,10},{14,12},{16,14},{18,16},{20... | collective-permute-start | bytes 294920 | tf_op jit(solution)/shard_map/ppermute | solution.py:25
  62.8 5.5 %collective-permute-start = (bf16[2,2,4,8,384]{4,3,1,0,2:T(8,128)(2,1)S(1)}, bf16[2,2,4,8,384]{4,3,1,0,2:T(8,128)(2,1)S(1)}, u32[]{:S(2)}, u32[]{:S(2)}) collective-permute-start(bf16[2,2,4,8,384]{4,3,1,0,2:T(8,128)(2,1)S(1)} %multiply_convert_fusion.10), channel_id=1, source_target_pairs={{0,2},{2,4},{4,6},{6,8},{8,10},{10,12},{12,14},{14,16},{16,18},{18... | collective-permute-start | bytes 294920 | tf_op jit(solution)/shard_map/ppermute | solution.py:24
  68.8 1.3 copy-start.7
  70.5 6.8 %collective-permute-start.2 = (f32[2,2,4,8,384]{4,3,1,0,2:T(8,128)S(1)}, f32[2,2,4,8,384]{4,3,1,0,2:T(8,128)S(1)}, u32[]{:S(2)}, u32[]{:S(2)}) collective-permute-start(f32[2,2,4,8,384]{4,3,1,0,2:T(8,128)S(1)} %fusion.20), channel_id=1, source_target_pairs={{0,1},{1,0},{2,3},{3,2},{4,5},{5,4},{6,7},{7,6},{8,9},{9,8},{10,11... | collective-permute-start | bytes 589832 | tf_op jit(solution)/shard_map/ppermute | solution.py:122
  114.5 9.9 %collective-permute-start.4 = (bf16[2,2,4,8,384]{4,3,1,0,2:T(8,128)(2,1)S(1)}, bf16[2,2,4,8,384]{4,3,1,0,2:T(8,128)(2,1)S(1)}, u32[]{:S(2)}, u32[]{:S(2)}) collective-permute-start(bf16[2,2,4,8,384]{4,3,1,0,2:T(8,128)(2,1)S(1)} %multiply_convert_fusion.7), channel_id=1, source_target_pairs={{2,0},{4,2},{6,4},{8,6},{10,8},{12,10},{14,12},{16,14},{18,16},{20... | collective-permute-start | bytes 294920 | tf_op jit(solution)/shard_map/ppermute | solution.py:25
  118.4 7.3 %collective-permute-start.3 = (bf16[2,2,4,8,384]{4,3,1,0,2:T(8,128)(2,1)S(1)}, bf16[2,2,4,8,384]{4,3,1,0,2:T(8,128)(2,1)S(1)}, u32[]{:S(2)}, u32[]{:S(2)}) collective-permute-start(bf16[2,2,4,8,384]{4,3,1,0,2:T(8,128)(2,1)S(1)} %multiply_convert_fusion.7), channel_id=1, source_target_pairs={{0,2},{2,4},{4,6},{6,8},{8,10},{10,12},{12,14},{14,16},{16,18},{18... | collective-permute-start | bytes 294920 | tf_op jit(solution)/shard_map/ppermute | solution.py:24
  126.2 1.3 copy-start.8
  127.8 6.4 %collective-permute-start.5 = (f32[2,2,4,8,384]{4,3,1,0,2:T(8,128)S(1)}, f32[2,2,4,8,384]{4,3,1,0,2:T(8,128)S(1)}, u32[]{:S(2)}, u32[]{:S(2)}) collective-permute-start(f32[2,2,4,8,384]{4,3,1,0,2:T(8,128)S(1)} %fusion.23), channel_id=1, source_target_pairs={{0,1},{1,0},{2,3},{3,2},{4,5},{5,4},{6,7},{7,6},{8,9},{9,8},{10,11... | collective-permute-start | bytes 589832 | tf_op jit(solution)/shard_map/ppermute | solution.py:122
  169.7 12.2 %collective-permute-start.7 = (bf16[2,2,4,8,384]{4,3,1,0,2:T(8,128)(2,1)S(1)}, bf16[2,2,4,8,384]{4,3,1,0,2:T(8,128)(2,1)S(1)}, u32[]{:S(2)}, u32[]{:S(2)}) collective-permute-start(bf16[2,2,4,8,384]{4,3,1,0,2:T(8,128)(2,1)S(1)} %multiply_convert_fusion.4), channel_id=1, source_target_pairs={{2,0},{4,2},{6,4},{8,6},{10,8},{12,10},{14,12},{16,14},{18,16},{20... | collective-permute-start | bytes 294920 | tf_op jit(solution)/shard_map/ppermute | solution.py:25
  172.8 10.4 %collective-permute-start.6 = (bf16[2,2,4,8,384]{4,3,1,0,2:T(8,128)(2,1)S(1)}, bf16[2,2,4,8,384]{4,3,1,0,2:T(8,128)(2,1)S(1)}, u32[]{:S(2)}, u32[]{:S(2)}) collective-permute-start(bf16[2,2,4,8,384]{4,3,1,0,2:T(8,128)(2,1)S(1)} %multiply_convert_fusion.4), channel_id=1, source_target_pairs={{0,2},{2,4},{4,6},{6,8},{8,10},{10,12},{12,14},{14,16},{16,18},{18... | collective-permute-start | bytes 294920 | tf_op jit(solution)/shard_map/ppermute | solution.py:24
  183.7 1.3 copy-start.9
  185.3 6.4 %collective-permute-start.8 = (f32[2,2,4,8,384]{4,3,1,0,2:T(8,128)S(1)}, f32[2,2,4,8,384]{4,3,1,0,2:T(8,128)S(1)}, u32[]{:S(2)}, u32[]{:S(2)}) collective-permute-start(f32[2,2,4,8,384]{4,3,1,0,2:T(8,128)S(1)} %fusion.26), channel_id=1, source_target_pairs={{0,1},{1,0},{2,3},{3,2},{4,5},{5,4},{6,7},{7,6},{8,9},{9,8},{10,11... | collective-permute-start | bytes 589832 | tf_op jit(solution)/shard_map/ppermute | solution.py:122
  225.2 15.7 %collective-permute-start.10 = (bf16[2,2,4,8,384]{4,3,1,0,2:T(8,128)(2,1)S(1)}, bf16[2,2,4,8,384]{4,3,1,0,2:T(8,128)(2,1)S(1)}, u32[]{:S(2)}, u32[]{:S(2)}) collective-permute-start(bf16[2,2,4,8,384]{4,3,1,0,2:T(8,128)(2,1)S(1)} %multiply_convert_fusion.1), channel_id=1, source_target_pairs={{2,0},{4,2},{6,4},{8,6},{10,8},{12,10},{14,12},{16,14},{18,16},{20... | collective-permute-start | bytes 294920 | tf_op jit(solution)/shard_map/ppermute | solution.py:25
  227.1 15.0 %collective-permute-start.9 = (bf16[2,2,4,8,384]{4,3,1,0,2:T(8,128)(2,1)S(1)}, bf16[2,2,4,8,384]{4,3,1,0,2:T(8,128)(2,1)S(1)}, u32[]{:S(2)}, u32[]{:S(2)}) collective-permute-start(bf16[2,2,4,8,384]{4,3,1,0,2:T(8,128)(2,1)S(1)} %multiply_convert_fusion.1), channel_id=1, source_target_pairs={{0,2},{2,4},{4,6},{6,8},{8,10},{10,12},{12,14},{14,16},{16,18},{18... | collective-permute-start | bytes 294920 | tf_op jit(solution)/shard_map/ppermute | solution.py:24
  242.7 1.3 copy-start.10

commit v7 on v6

--- a/solution.py
+++ b/solution.py
@@ -26,30 +26,21 @@
     return jnp.concatenate([before, array, after], axis=1)
 
 
-def head_bias(bias_segment, groups, lon_total, levels):
+def head_bias(bias_segment, groups, levels):
     heads_here = bias_segment.shape[0] // groups
     group = lax.axis_index("lon") // (lax.axis_size("lon") // groups)
     picked = lax.dynamic_slice_in_dim(bias_segment, group * heads_here, heads_here, axis=0)
-    lhs = picked.reshape(heads_here * levels, lon_total)
-    high = lhs.astype(jnp.bfloat16)
-    rest = lhs - high.astype(jnp.float32)
-    middle = rest.astype(jnp.bfloat16)
-    low = (rest - middle.astype(jnp.float32)).astype(jnp.bfloat16)
-    lon = jnp.arange(lon_total, dtype=jnp.int32)
-    key_lon = jnp.repeat(lon, levels)
-    offsets = jnp.mod(key_lon[None, :] - lon[:, None], lon_total)
-    onehot = (lon[:, None, None] == offsets[None]).astype(jnp.bfloat16).reshape(lon_total, -1)
-    parts = [
-        jnp.dot(part, onehot, preferred_element_type=jnp.float32) for part in (high, middle, low)
-    ]
-    table = (parts[0] + parts[1]) + parts[2]
-    table = table.reshape(heads_here, levels, lon_total, lon_total * levels)
-    table = jnp.transpose(table, (0, 2, 1, 3))
-    return table.reshape(heads_here, lon_total * levels, lon_total * levels)
+    return jnp.repeat(picked, levels, axis=2)
 
 
-def attention_kernel(x_ref, bias_ref, o_ref, *, heads, head_dim):
+def attention_kernel(x_ref, base_ref, o_ref, bias_ref, *, heads, head_dim, levels):
     width = heads * head_dim
+    lon_total = x_ref.shape[0] // levels
+    for h in range(heads):
+        base = base_ref[h]
+        for i in range(lon_total):
+            rotated = base if i == 0 else pltpu.roll(base, i * levels, 1)
+            bias_ref[h, i * levels : (i + 1) * levels, :] = rotated
     for h in range(heads):
         cols = slice(h * head_dim, (h + 1) * head_dim)
         q = x_ref[:, cols]
@@ -64,14 +55,15 @@
         o_ref[:, cols] = (summed / total).astype(o_ref.dtype)
 
 
-def attend(x, bias_full, head_dim):
-    heads = bias_full.shape[0]
+def attend(x, bias_base, head_dim):
+    heads, levels, keys = bias_base.shape
     return pl.pallas_call(
-        functools.partial(attention_kernel, heads=heads, head_dim=head_dim),
+        functools.partial(attention_kernel, heads=heads, head_dim=head_dim, levels=levels),
         out_shape=jax.ShapeDtypeStruct((x.shape[0], heads * head_dim), jnp.bfloat16),
         in_specs=[pl.BlockSpec(memory_space=pltpu.VMEM)] * 2,
         out_specs=pl.BlockSpec(memory_space=pltpu.VMEM),
-    )(x, bias_full)
+        scratch_shapes=[pltpu.VMEM((heads, x.shape[0], keys), jnp.float32)],
+    )(x, bias_base)
 
 
 def block(field, lead_index, mask_ids, params, bias_full):
@@ -151,7 +143,7 @@
     wqkv = wqkv.reshape(groups, features, 3 * heads_here * head_dim)
     wout = wout.reshape(groups, heads_here * head_dim, features)
     params = (mask_tab, lead_tab, wqkv, wout, wup, wdown, gains, taps)
-    bias_full = head_bias(score_bias[0], groups, lon_local * lon_devices, initial_state.shape[3])
+    bias_full = head_bias(score_bias[0], groups, initial_state.shape[3])
     segment_first = lax.axis_index("segment") == 0
     current = initial_state
     first = None

time: 246 us -> 242 us (0.984)
  matrix products: 13.1 us -> 6.75 us
  waiting for transfers between devices: 25.2 us -> 29.6 us
  Pallas kernels: 19 us -> 15.6 us
    dot_general x3 -> x0, matrix products: 6.29 us -> none  [head_bias(): jnp.dot(part, onehot, preferred_element_type=jnp.float32)]
    all_to_all x1, waiting for transfers between devices: 5.67 us -> 10.3 us  [block(): incoming = lax.all_to_all(outgoing, 'lon', 0, 0, tiled=True)]
    pallas_call x4, Pallas kernels: 19 us -> 15.6 us  [attend(): pl.pallas_call(functools.partial(attention_kernel, heads=heads, head_dim=...]
  transfers between devices with their start and end apart: 12 -> 12, of which waited for: 12 -> 12; matrix products, arithmetic and copies ran while one was open for 3% -> 1% of each run, Pallas kernels for 0% -> 0%
where the time goes in v7:
time: 242 us; the launch traced here: 241 us
  blocking collectives  102 us (42%)
  starting transfers between devices  61.7 us (25%)
  waiting for transfers between devices  29.6 us (12%)
  Pallas kernels  15.6 us (6%)
  local copies, waits for them, and re-layouts  11.6 us (5%)
  other arithmetic  8.85 us (4%)
  matrix products  6.75 us (3%)
  between operations  4.77 us (2%)
    all_to_all x4, blocking collectives, block(): returned = lax.all_to_all(back, 'lon', 0, 0, tiled=True)  55.2 us
    all_to_all x3, blocking collectives, block(): incoming = lax.all_to_all(outgoing, 'lon', 0, 0, tiled=True)  46.4 us
    ppermute x4, starting transfers between devices, lat_halo(): before = lax.ppermute(array[:, length - width:], 'lat', up)  31.5 us
    pallas_call x4, Pallas kernels, attend(): pl.pallas_call(functools.partial(attention_kernel, heads=heads, head_dim=...  15.6 us
    ppermute x4, starting transfers between devices, lat_halo(): after = lax.ppermute(array[:, :width], 'lat', down)  13.2 us
    ppermute x3, waiting for transfers between devices, from_partner(): lax.ppermute(array, 'segment', [(i, i ^ 1) for i in range(lax.axis_size('...  13 us
    all_to_all x1, waiting for transfers between devices, block(): incoming = lax.all_to_all(outgoing, 'lon', 0, 0, tiled=True)  10.3 us
    all_to_all x1, starting transfers between devices, block(): incoming = lax.all_to_all(outgoing, 'lon', 0, 0, tiled=True)  10.3 us
  transfers between devices with their start and end apart: 12, of which 12 were waited for; matrix products, arithmetic and copies ran while one was open for 1% of the time, Pallas kernels for 0%

profile of v7, /device:TPU:1, one launch (start us, length us, event | category | flops | bytes accessed | tf_op | source)
XLA Modules:
  0.0 240.5 jit_solution(9241660637110446400)
XLA Ops:
  0.0 1.5 fusion.106
  14.2 10.3 %all-to-all-start = ((bf16[16,32,288]{2,1,0:T(8,128)(2,1)}), bf16[16,32,288]{2,1,0:T(8,128)(2,1)}, u32[]{:S(2)}, u32[]{:S(2)}) async-start(bf16[16,32,288]{2,1,0:T(8,128)(2,1)} %bitcast.7), calls=%async_computation | async-start | bytes 786432 | tf_op jit(solution)/shard_map/all_to_all | solution.py:90
  26.5 10.3 %all-to-all-done = bf16[16,32,288]{2,1,0:T(8,128)(2,1)} async-done(((bf16[16,32,288]{2,1,0:T(8,128)(2,1)}), bf16[16,32,288]{2,1,0:T(8,128)(2,1)}, u32[]{:S(2)}, u32[]{:S(2)}) %all-to-all-start) | async-done | bytes 294944 | tf_op jit(solution)/shard_map/all_to_all | solution.py:90
  36.8 3.9 %shard_map.118 = bf16[512,96]{1,0:T(8,128)(2,1)} custom-call(bf16[512,288]{1,0:T(8,128)(2,1)} %bitcast.8.x_ref, f32[3,8,512]{2,1,0:T(8,128)} %reshape.272.base_ref), custom_call_target="tpu_custom_call" | custom-call | tf_op jit(solution)/shard_map/pallas_call | solution.py:60
  40.7 15.3 %all_to_all.40 = bf16[16,32,96]{2,1,0:T(8,128)(2,1)S(1)} all-to-all(bf16[16,32,96]{2,1,0:T(8,128)(2,1)} %bitcast.163), channel_id=1, replica_groups=mesh['lon'=16,'lat'=16,'segment'=2] {'lon'}, dimensions={0} | all-to-all | bytes 196608 | tf_op jit(solution)/shard_map/all_to_all | solution.py:93
  56.7 4.4 %collective-permute-start.1 = (bf16[2,2,4,8,384]{4,3,1,0,2:T(8,128)(2,1)S(1)}, bf16[2,2,4,8,384]{4,3,1,0,2:T(8,128)(2,1)S(1)}, u32[]{:S(2)}, u32[]{:S(2)}) collective-permute-start(bf16[2,2,4,8,384]{4,3,1,0,2:T(8,128)(2,1)S(1)} %multiply_convert_fusion.10), channel_id=1, source_target_pairs={{2,0},{4,2},{6,4},{8,6},{10,8},{12,10},{14,12},{16,14},{18,16},{20... | collective-permute-start | bytes 294920 | tf_op jit(solution)/shard_map/ppermute | solution.py:25
  61.1 3.9 %collective-permute-start = (bf16[2,2,4,8,384]{4,3,1,0,2:T(8,128)(2,1)S(1)}, bf16[2,2,4,8,384]{4,3,1,0,2:T(8,128)(2,1)S(1)}, u32[]{:S(2)}, u32[]{:S(2)}) collective-permute-start(bf16[2,2,4,8,384]{4,3,1,0,2:T(8,128)(2,1)S(1)} %multiply_convert_fusion.10), channel_id=1, source_target_pairs={{0,2},{2,4},{4,6},{6,8},{8,10},{10,12},{12,14},{14,16},{16,18},{18... | collective-permute-start | bytes 294920 | tf_op jit(solution)/shard_map/ppermute | solution.py:24
  65.4 1.3 collective-permute-done
  68.8 2.2 collective-permute-start.2
  71.0 4.6 %collective-permute-done.2 = f32[2,2,4,8,384]{4,3,1,0,2:T(8,128)S(1)} collective-permute-done((f32[2,2,4,8,384]{4,3,1,0,2:T(8,128)S(1)}, f32[2,2,4,8,384]{4,3,1,0,2:T(8,128)S(1)}, u32[]{:S(2)}, u32[]{:S(2)}) %collective-permute-start.2) | collective-permute-done | bytes 196640 | tf_op jit(solution)/shard_map/ppermute | solution.py:114
  76.7 17.3 %all_to_all.41 = bf16[16,32,288]{2,1,0:T(8,128)(2,1)} all-to-all(bf16[16,32,288]{2,1,0:T(8,128)(2,1)S(1)} %bitcast.155), channel_id=1, replica_groups=mesh['lon'=16,'lat'=16,'segment'=2] {'lon'}, dimensions={0} | all-to-all | bytes 589824 | tf_op jit(solution)/shard_map/all_to_all | solution.py:90
  94.0 3.9 %shard_map.119 = bf16[512,96]{1,0:T(8,128)(2,1)} custom-call(bf16[512,288]{1,0:T(8,128)(2,1)} %bitcast.153, f32[3,8,512]{2,1,0:T(8,128)} %reshape.272.base_ref), custom_call_target="tpu_custom_call" | custom-call | tf_op jit(solution)/shard_map/pallas_call | solution.py:60
  97.9 13.4 %all_to_all.42 = bf16[16,32,96]{2,1,0:T(8,128)(2,1)S(1)} all-to-all(bf16[16,32,96]{2,1,0:T(8,128)(2,1)} %bitcast.164), channel_id=1, replica_groups=mesh['lon'=16,'lat'=16,'segment'=2] {'lon'}, dimensions={0} | all-to-all | bytes 196608 | tf_op jit(solution)/shard_map/all_to_all | solution.py:93
  112.0 3.9 %collective-permute-start.4 = (bf16[2,2,4,8,384]{4,3,1,0,2:T(8,128)(2,1)S(1)}, bf16[2,2,4,8,384]{4,3,1,0,2:T(8,128)(2,1)S(1)}, u32[]{:S(2)}, u32[]{:S(2)}) collective-permute-start(bf16[2,2,4,8,384]{4,3,1,0,2:T(8,128)(2,1)S(1)} %multiply_convert_fusion.7), channel_id=1, source_target_pairs={{2,0},{4,2},{6,4},{8,6},{10,8},{12,10},{14,12},{16,14},{18,16},{20... | collective-permute-start | bytes 294920 | tf_op jit(solution)/shard_map/ppermute | solution.py:25
  115.9 5.8 %collective-permute-start.3 = (bf16[2,2,4,8,384]{4,3,1,0,2:T(8,128)(2,1)S(1)}, bf16[2,2,4,8,384]{4,3,1,0,2:T(8,128)(2,1)S(1)}, u32[]{:S(2)}, u32[]{:S(2)}) collective-permute-start(bf16[2,2,4,8,384]{4,3,1,0,2:T(8,128)(2,1)S(1)} %multiply_convert_fusion.7), channel_id=1, source_target_pairs={{0,2},{2,4},{4,6},{6,8},{8,10},{10,12},{12,14},{14,16},{16,18},{18... | collective-permute-start | bytes 294920 | tf_op jit(solution)/shard_map/ppermute | solution.py:24
  122.1 1.3 collective-permute-done.3
  125.5 2.1 collective-permute-start.5
  127.6 4.3 %collective-permute-done.5 = f32[2,2,4,8,384]{4,3,1,0,2:T(8,128)S(1)} collective-permute-done((f32[2,2,4,8,384]{4,3,1,0,2:T(8,128)S(1)}, f32[2,2,4,8,384]{4,3,1,0,2:T(8,128)S(1)}, u32[]{:S(2)}, u32[]{:S(2)}) %collective-permute-start.5) | collective-permute-done | bytes 196640 | tf_op jit(solution)/shard_map/ppermute | solution.py:114
  133.0 15.2 %all_to_all.43 = bf16[16,32,288]{2,1,0:T(8,128)(2,1)} all-to-all(bf16[16,32,288]{2,1,0:T(8,128)(2,1)S(1)} %bitcast.156), channel_id=1, replica_groups=mesh['lon'=16,'lat'=16,'segment'=2] {'lon'}, dimensions={0} | all-to-all | bytes 589824 | tf_op jit(solution)/shard_map/all_to_all | solution.py:90
  148.2 3.9 %shard_map.120 = bf16[512,96]{1,0:T(8,128)(2,1)} custom-call(bf16[512,288]{1,0:T(8,128)(2,1)} %bitcast.154, f32[3,8,512]{2,1,0:T(8,128)} %reshape.272.base_ref), custom_call_target="tpu_custom_call" | custom-call | tf_op jit(solution)/shard_map/pallas_call | solution.py:60
  152.1 13.5 %all_to_all.44 = bf16[16,32,96]{2,1,0:T(8,128)(2,1)S(1)} all-to-all(bf16[16,32,96]{2,1,0:T(8,128)(2,1)} %bitcast.165), channel_id=1, replica_groups=mesh['lon'=16,'lat'=16,'segment'=2] {'lon'}, dimensions={0} | all-to-all | bytes 196608 | tf_op jit(solution)/shard_map/all_to_all | solution.py:93
  166.4 3.1 %collective-permute-start.7 = (bf16[2,2,4,8,384]{4,3,1,0,2:T(8,128)(2,1)S(1)}, bf16[2,2,4,8,384]{4,3,1,0,2:T(8,128)(2,1)S(1)}, u32[]{:S(2)}, u32[]{:S(2)}) collective-permute-start(bf16[2,2,4,8,384]{4,3,1,0,2:T(8,128)(2,1)S(1)} %multiply_convert_fusion.4), channel_id=1, source_target_pairs={{2,0},{4,2},{6,4},{8,6},{10,8},{12,10},{14,12},{16,14},{18,16},{20... | collective-permute-start | bytes 294920 | tf_op jit(solution)/shard_map/ppermute | solution.py:25
  169.5 8.4 %collective-permute-start.6 = (bf16[2,2,4,8,384]{4,3,1,0,2:T(8,128)(2,1)S(1)}, bf16[2,2,4,8,384]{4,3,1,0,2:T(8,128)(2,1)S(1)}, u32[]{:S(2)}, u32[]{:S(2)}) collective-permute-start(bf16[2,2,4,8,384]{4,3,1,0,2:T(8,128)(2,1)S(1)} %multiply_convert_fusion.4), channel_id=1, source_target_pairs={{0,2},{2,4},{4,6},{6,8},{8,10},{10,12},{12,14},{14,16},{16,18},{18... | collective-permute-start | bytes 294920 | tf_op jit(solution)/shard_map/ppermute | solution.py:24
  178.2 1.3 collective-permute-done.6
  181.7 2.4 collective-permute-start.8
  184.0 4.0 %collective-permute-done.8 = f32[2,2,4,8,384]{4,3,1,0,2:T(8,128)S(1)} collective-permute-done((f32[2,2,4,8,384]{4,3,1,0,2:T(8,128)S(1)}, f32[2,2,4,8,384]{4,3,1,0,2:T(8,128)S(1)}, u32[]{:S(2)}, u32[]{:S(2)}) %collective-permute-start.8) | collective-permute-done | bytes 196640 | tf_op jit(solution)/shard_map/ppermute | solution.py:114
  189.2 13.9 %all_to_all.45 = bf16[16,32,288]{2,1,0:T(8,128)(2,1)} all-to-all(bf16[16,32,288]{2,1,0:T(8,128)(2,1)S(1)} %bitcast.157), channel_id=1, replica_groups=mesh['lon'=16,'lat'=16,'segment'=2] {'lon'}, dimensions={0} | all-to-all | bytes 589824 | tf_op jit(solution)/shard_map/all_to_all | solution.py:90
  203.1 3.9 %shard_map.121 = bf16[512,96]{1,0:T(8,128)(2,1)} custom-call(bf16[512,288]{1,0:T(8,128)(2,1)} %bitcast.152, f32[3,8,512]{2,1,0:T(8,128)} %reshape.272.base_ref), custom_call_target="tpu_custom_call" | custom-call | tf_op jit(solution)/shard_map/pallas_call | solution.py:60
  207.0 13.0 %all_to_all.46 = bf16[16,32,96]{2,1,0:T(8,128)(2,1)S(1)} all-to-all(bf16[16,32,96]{2,1,0:T(8,128)(2,1)} %bitcast.162), channel_id=1, replica_groups=mesh['lon'=16,'lat'=16,'segment'=2] {'lon'}, dimensions={0} | all-to-all | bytes 196608 | tf_op jit(solution)/shard_map/all_to_all | solution.py:93
  220.7 1.9 collective-permute-start.10
  222.6 13.4 %collective-permute-start.9 = (bf16[2,2,4,8,384]{4,3,1,0,2:T(8,128)(2,1)S(1)}, bf16[2,2,4,8,384]{4,3,1,0,2:T(8,128)(2,1)S(1)}, u32[]{:S(2)}, u32[]{:S(2)}) collective-permute-start(bf16[2,2,4,8,384]{4,3,1,0,2:T(8,128)(2,1)S(1)} %multiply_convert_fusion.1), channel_id=1, source_target_pairs={{0,2},{2,4},{4,6},{6,8},{8,10},{10,12},{12,14},{14,16},{16,18},{18... | collective-permute-start | bytes 294920 | tf_op jit(solution)/shard_map/ppermute | solution.py:24
  236.4 1.3 collective-permute-done.9
  (121 shorter events, 27.1 us)
Async XLA Ops:
  0.0 67.2 %copy-start = (bf16[1,384,1536]{2,1,0:T(8,128)(2,1)S(1)}, bf16[1,384,1536]{2,1,0:T(8,128)(2,1)}, u32[]{:S(2)}) copy-start(bf16[1,384,1536]{2,1,0:T(8,128)(2,1)} %param.19) | copy-start | bytes 3538948
  0.0 11.9 %copy-start.3 = (bf16[1,384,1152]{2,1,0:T(8,128)(2,1)S(1)}, bf16[1,384,1152]{2,1,0:T(8,128)(2,1)}, u32[]{:S(2)}) copy-start(bf16[1,384,1152]{2,1,0:T(8,128)(2,1)} %param.17) | copy-start | bytes 2654212
  14.2 22.5 %all-to-all-start = ((bf16[16,32,288]{2,1,0:T(8,128)(2,1)}), bf16[16,32,288]{2,1,0:T(8,128)(2,1)}, u32[]{:S(2)}, u32[]{:S(2)}) async-start(bf16[16,32,288]{2,1,0:T(8,128)(2,1)} %bitcast.7), calls=%async_computation | async-start | bytes 786432 | tf_op jit(solution)/shard_map/all_to_all | solution.py:90
  25.2 30.8 %copy-start.1 = (bf16[1,384,384]{2,1,0:T(8,128)(2,1)S(1)}, bf16[1,384,384]{2,1,0:T(8,128)(2,1)}, u32[]{:S(2)}) copy-start(bf16[1,384,384]{2,1,0:T(8,128)(2,1)} %param.18) | copy-start | bytes 884740
  25.5 30.8 %copy-start.2 = (f32[2,2,4,8,384]{4,3,2,1,0:T(8,128)S(1)}, f32[2,2,4,8,384]{4,3,2,1,0:T(8,128)}, u32[]{:S(2)}) copy-start(f32[2,2,4,8,384]{4,3,2,1,0:T(8,128)} %param.12) | copy-start | bytes 589828
  36.8 28.2 %copy-start.4 = (f32[1,5,384]{2,0,1:T(1,128)S(1)}, f32[1,5,384]{2,0,1:T(1,128)}, u32[]{:S(2)}) copy-start(f32[1,5,384]{2,0,1:T(1,128)} %param.22) | copy-start | bytes 23044
  56.7 8.6 %collective-permute-start.1 = (bf16[2,2,4,8,384]{4,3,1,0,2:T(8,128)(2,1)S(1)}, bf16[2,2,4,8,384]{4,3,1,0,2:T(8,128)(2,1)S(1)}, u32[]{:S(2)}, u32[]{:S(2)}) collective-permute-start(bf16[2,2,4,8,384]{4,3,1,0,2:T(8,128)(2,1)S(1)} %multiply_convert_fusion.10), channel_id=1, source_target_pairs={{2,0},{4,2},{6,4},{8,6},{10,8},{12,10},{14,12},{16,14},{18,16},{20... | collective-permute-start | bytes 294920 | tf_op jit(solution)/shard_map/ppermute | solution.py:25
  61.1 5.5 %collective-permute-start = (bf16[2,2,4,8,384]{4,3,1,0,2:T(8,128)(2,1)S(1)}, bf16[2,2,4,8,384]{4,3,1,0,2:T(8,128)(2,1)S(1)}, u32[]{:S(2)}, u32[]{:S(2)}) collective-permute-start(bf16[2,2,4,8,384]{4,3,1,0,2:T(8,128)(2,1)S(1)} %multiply_convert_fusion.10), channel_id=1, source_target_pairs={{0,2},{2,4},{4,6},{6,8},{8,10},{10,12},{12,14},{14,16},{16,18},{18... | collective-permute-start | bytes 294920 | tf_op jit(solution)/shard_map/ppermute | solution.py:24
  67.2 1.3 copy-start.5
  68.8 6.8 %collective-permute-start.2 = (f32[2,2,4,8,384]{4,3,1,0,2:T(8,128)S(1)}, f32[2,2,4,8,384]{4,3,1,0,2:T(8,128)S(1)}, u32[]{:S(2)}, u32[]{:S(2)}) collective-permute-start(f32[2,2,4,8,384]{4,3,1,0,2:T(8,128)S(1)} %fusion.16), channel_id=1, source_target_pairs={{0,1},{1,0},{2,3},{3,2},{4,5},{5,4},{6,7},{7,6},{8,9},{9,8},{10,11... | collective-permute-start | bytes 589832 | tf_op jit(solution)/shard_map/ppermute | solution.py:114
  112.0 10.1 %collective-permute-start.4 = (bf16[2,2,4,8,384]{4,3,1,0,2:T(8,128)(2,1)S(1)}, bf16[2,2,4,8,384]{4,3,1,0,2:T(8,128)(2,1)S(1)}, u32[]{:S(2)}, u32[]{:S(2)}) collective-permute-start(bf16[2,2,4,8,384]{4,3,1,0,2:T(8,128)(2,1)S(1)} %multiply_convert_fusion.7), channel_id=1, source_target_pairs={{2,0},{4,2},{6,4},{8,6},{10,8},{12,10},{14,12},{16,14},{18,16},{20... | collective-permute-start | bytes 294920 | tf_op jit(solution)/shard_map/ppermute | solution.py:25
  115.9 7.4 %collective-permute-start.3 = (bf16[2,2,4,8,384]{4,3,1,0,2:T(8,128)(2,1)S(1)}, bf16[2,2,4,8,384]{4,3,1,0,2:T(8,128)(2,1)S(1)}, u32[]{:S(2)}, u32[]{:S(2)}) collective-permute-start(bf16[2,2,4,8,384]{4,3,1,0,2:T(8,128)(2,1)S(1)} %multiply_convert_fusion.7), channel_id=1, source_target_pairs={{0,2},{2,4},{4,6},{6,8},{8,10},{10,12},{12,14},{14,16},{16,18},{18... | collective-permute-start | bytes 294920 | tf_op jit(solution)/shard_map/ppermute | solution.py:24
  123.8 1.3 copy-start.6
  125.5 6.4 %collective-permute-start.5 = (f32[2,2,4,8,384]{4,3,1,0,2:T(8,128)S(1)}, f32[2,2,4,8,384]{4,3,1,0,2:T(8,128)S(1)}, u32[]{:S(2)}, u32[]{:S(2)}) collective-permute-start(f32[2,2,4,8,384]{4,3,1,0,2:T(8,128)S(1)} %fusion.19), channel_id=1, source_target_pairs={{0,1},{1,0},{2,3},{3,2},{4,5},{5,4},{6,7},{7,6},{8,9},{9,8},{10,11... | collective-permute-start | bytes 589832 | tf_op jit(solution)/shard_map/ppermute | solution.py:114
  166.4 11.8 %collective-permute-start.7 = (bf16[2,2,4,8,384]{4,3,1,0,2:T(8,128)(2,1)S(1)}, bf16[2,2,4,8,384]{4,3,1,0,2:T(8,128)(2,1)S(1)}, u32[]{:S(2)}, u32[]{:S(2)}) collective-permute-start(bf16[2,2,4,8,384]{4,3,1,0,2:T(8,128)(2,1)S(1)} %multiply_convert_fusion.4), channel_id=1, source_target_pairs={{2,0},{4,2},{6,4},{8,6},{10,8},{12,10},{14,12},{16,14},{18,16},{20... | collective-permute-start | bytes 294920 | tf_op jit(solution)/shard_map/ppermute | solution.py:25
  169.5 10.0 %collective-permute-start.6 = (bf16[2,2,4,8,384]{4,3,1,0,2:T(8,128)(2,1)S(1)}, bf16[2,2,4,8,384]{4,3,1,0,2:T(8,128)(2,1)S(1)}, u32[]{:S(2)}, u32[]{:S(2)}) collective-permute-start(bf16[2,2,4,8,384]{4,3,1,0,2:T(8,128)(2,1)S(1)} %multiply_convert_fusion.4), channel_id=1, source_target_pairs={{0,2},{2,4},{4,6},{6,8},{8,10},{10,12},{12,14},{14,16},{16,18},{18... | collective-permute-start | bytes 294920 | tf_op jit(solution)/shard_map/ppermute | solution.py:24
  180.0 1.3 copy-start.7
  181.7 6.4 %collective-permute-start.8 = (f32[2,2,4,8,384]{4,3,1,0,2:T(8,128)S(1)}, f32[2,2,4,8,384]{4,3,1,0,2:T(8,128)S(1)}, u32[]{:S(2)}, u32[]{:S(2)}) collective-permute-start(f32[2,2,4,8,384]{4,3,1,0,2:T(8,128)S(1)} %fusion.22), channel_id=1, source_target_pairs={{0,1},{1,0},{2,3},{3,2},{4,5},{5,4},{6,7},{7,6},{8,9},{9,8},{10,11... | collective-permute-start | bytes 589832 | tf_op jit(solution)/shard_map/ppermute | solution.py:114
  220.7 15.7 %collective-permute-start.10 = (bf16[2,2,4,8,384]{4,3,1,0,2:T(8,128)(2,1)S(1)}, bf16[2,2,4,8,384]{4,3,1,0,2:T(8,128)(2,1)S(1)}, u32[]{:S(2)}, u32[]{:S(2)}) collective-permute-start(bf16[2,2,4,8,384]{4,3,1,0,2:T(8,128)(2,1)S(1)} %multiply_convert_fusion.1), channel_id=1, source_target_pairs={{2,0},{4,2},{6,4},{8,6},{10,8},{12,10},{14,12},{16,14},{18,16},{20... | collective-permute-start | bytes 294920 | tf_op jit(solution)/shard_map/ppermute | solution.py:25
  222.6 15.0 %collective-permute-start.9 = (bf16[2,2,4,8,384]{4,3,1,0,2:T(8,128)(2,1)S(1)}, bf16[2,2,4,8,384]{4,3,1,0,2:T(8,128)(2,1)S(1)}, u32[]{:S(2)}, u32[]{:S(2)}) collective-permute-start(bf16[2,2,4,8,384]{4,3,1,0,2:T(8,128)(2,1)S(1)} %multiply_convert_fusion.1), channel_id=1, source_target_pairs={{0,2},{2,4},{4,6},{6,8},{8,10},{10,12},{12,14},{14,16},{16,18},{18... | collective-permute-start | bytes 294920 | tf_op jit(solution)/shard_map/ppermute | solution.py:24
  238.2 1.3 copy-start.8

commit v8 on v7

--- a/solution.py
+++ b/solution.py
@@ -69,7 +69,8 @@
 def block(field, lead_index, mask_ids, params, bias_full):
     mask_tab, lead_tab, wqkv, wout, wup, wdown, gains, taps = params
     members, rows_lat, lon_local, levels, features = field.shape
-    groups, _, group_width = wqkv.shape
+    groups = wout.shape[0]
+    group_width = wqkv.shape[1] // groups
     heads_here = bias_full.shape[0]
     head_dim = group_width // (3 * heads_here)
     lon_devices = lax.axis_size("lon")
@@ -82,11 +83,11 @@
     lead_row = lax.dynamic_index_in_dim(lead_tab, lead_index, axis=0, keepdims=False)
     hidden = field + mask_embed[None, :, :, None, :] + lead_row
     normed = layer_norm(hidden, gains[0]).astype(jnp.bfloat16)
-    spread = jnp.broadcast_to(normed.reshape(1, -1, features), (groups, combos * tokens_local, features))
-    projected = jnp.einsum(
-        "gnc,gcf->gnf", spread, wqkv, preferred_element_type=jnp.float32
+    projected = jnp.dot(
+        normed.reshape(-1, features), wqkv, preferred_element_type=jnp.float32
     ).astype(jnp.bfloat16)
-    outgoing = projected.reshape(lon_devices, tokens_local, group_width)
+    projected = projected.reshape(combos * tokens_local, 3, groups, group_width // 3)
+    outgoing = jnp.transpose(projected, (2, 0, 1, 3)).reshape(lon_devices, tokens_local, group_width)
     incoming = lax.all_to_all(outgoing, "lon", 0, 0, tiled=True)
     attended = attend(incoming.reshape(lon_devices * tokens_local, group_width), bias_full, head_dim)
     back = attended.reshape(lon_devices, tokens_local, heads_here * head_dim)
@@ -139,8 +140,6 @@
     features = wqkv.shape[0]
     head_dim = features // head_count
     heads_here = head_count // groups
-    wqkv = jnp.transpose(wqkv.reshape(features, 3, groups, heads_here * head_dim), (2, 0, 1, 3))
-    wqkv = wqkv.reshape(groups, features, 3 * heads_here * head_dim)
     wout = wout.reshape(groups, heads_here * head_dim, features)
     params = (mask_tab, lead_tab, wqkv, wout, wup, wdown, gains, taps)
     bias_full = head_bias(score_bias[0], groups, initial_state.shape[3])

time: 242 us -> 243 us (level)
  no operation moved by 1% of the time
where the time goes in v8:
time: 243 us; the launch traced here: 241 us
  blocking collectives  102 us (42%)
  starting transfers between devices  61.7 us (25%)
  waiting for transfers between devices  29.5 us (12%)
  Pallas kernels  15.6 us (6%)
  local copies, waits for them, and re-layouts  12.5 us (5%)
  other arithmetic  8.13 us (3%)
  matrix products  7.32 us (3%)
  between operations  4.61 us (2%)
    all_to_all x4, blocking collectives, block(): returned = lax.all_to_all(back, 'lon', 0, 0, tiled=True)  55.3 us
    all_to_all x3, blocking collectives, block(): incoming = lax.all_to_all(outgoing, 'lon', 0, 0, tiled=True)  46.5 us
    ppermute x4, starting transfers between devices, lat_halo(): before = lax.ppermute(array[:, length - width:], 'lat', up)  31.4 us
    pallas_call x4, Pallas kernels, attend(): pl.pallas_call(functools.partial(attention_kernel, heads=heads, head_dim=...  15.6 us
    ppermute x4, starting transfers between devices, lat_halo(): after = lax.ppermute(array[:, :width], 'lat', down)  13.2 us
    ppermute x3, waiting for transfers between devices, from_partner(): lax.ppermute(array, 'segment', [(i, i ^ 1) for i in range(lax.axis_size('...  12.8 us
    all_to_all x1, waiting for transfers between devices, block(): incoming = lax.all_to_all(outgoing, 'lon', 0, 0, tiled=True)  10.3 us
    all_to_all x1, starting transfers between devices, block(): incoming = lax.all_to_all(outgoing, 'lon', 0, 0, tiled=True)  10.3 us
  transfers between devices with their start and end apart: 12, of which 12 were waited for; matrix products, arithmetic and copies ran while one was open for 1% of the time, Pallas kernels for 0%

profile of v8, /device:TPU:1, one launch (start us, length us, event | category | flops | bytes accessed | tf_op | source)
XLA Modules:
  0.0 241.1 jit_solution(1393766010064101632)
XLA Ops:
  0.0 1.5 fusion.109
  13.2 10.3 %all-to-all-start = ((bf16[16,32,288]{2,1,0:T(8,128)(2,1)}), bf16[16,32,288]{2,1,0:T(8,128)(2,1)}, u32[]{:S(2)}, u32[]{:S(2)}) async-start(bf16[16,32,288]{2,1,0:T(8,128)(2,1)} %reshape.284), calls=%async_computation | async-start | bytes 786432 | tf_op jit(solution)/shard_map/all_to_all | solution.py:91
  25.5 10.3 %all-to-all-done = bf16[16,32,288]{2,1,0:T(8,128)(2,1)} async-done(((bf16[16,32,288]{2,1,0:T(8,128)(2,1)}), bf16[16,32,288]{2,1,0:T(8,128)(2,1)}, u32[]{:S(2)}, u32[]{:S(2)}) %all-to-all-start) | async-done | bytes 294944 | tf_op jit(solution)/shard_map/all_to_all | solution.py:91
  35.8 3.9 %shard_map.118 = bf16[512,96]{1,0:T(8,128)(2,1)} custom-call(bf16[512,288]{1,0:T(8,128)(2,1)} %bitcast.7.x_ref, f32[3,8,512]{2,1,0:T(8,128)} %reshape.286.base_ref), custom_call_target="tpu_custom_call" | custom-call | tf_op jit(solution)/shard_map/pallas_call | solution.py:60
  39.7 15.4 %all_to_all.40 = bf16[16,32,96]{2,1,0:T(8,128)(2,1)S(1)} all-to-all(bf16[16,32,96]{2,1,0:T(8,128)(2,1)} %bitcast.172), channel_id=1, replica_groups=mesh['lon'=16,'lat'=16,'segment'=2] {'lon'}, dimensions={0} | all-to-all | bytes 196608 | tf_op jit(solution)/shard_map/all_to_all | solution.py:94
  55.8 4.3 %collective-permute-start.1 = (bf16[2,2,4,8,384]{4,3,2,1,0:T(8,128)(2,1)S(1)}, bf16[2,2,4,8,384]{4,3,2,1,0:T(8,128)(2,1)S(1)}, u32[]{:S(2)}, u32[]{:S(2)}) collective-permute-start(bf16[2,2,4,8,384]{4,3,2,1,0:T(8,128)(2,1)S(1)} %multiply_convert_fusion.10), channel_id=1, source_target_pairs={{2,0},{4,2},{6,4},{8,6},{10,8},{12,10},{14,12},{16,14},{18,16},{20... | collective-permute-start | bytes 294920 | tf_op jit(solution)/shard_map/ppermute | solution.py:25
  60.1 3.9 %collective-permute-start = (bf16[2,2,4,8,384]{4,3,2,1,0:T(8,128)(2,1)S(1)}, bf16[2,2,4,8,384]{4,3,2,1,0:T(8,128)(2,1)S(1)}, u32[]{:S(2)}, u32[]{:S(2)}) collective-permute-start(bf16[2,2,4,8,384]{4,3,2,1,0:T(8,128)(2,1)S(1)} %multiply_convert_fusion.10), channel_id=1, source_target_pairs={{0,2},{2,4},{4,6},{6,8},{8,10},{10,12},{12,14},{14,16},{16,18},{18... | collective-permute-start | bytes 294920 | tf_op jit(solution)/shard_map/ppermute | solution.py:24
  64.3 1.3 collective-permute-done
  67.7 2.2 collective-permute-start.2
  70.0 4.6 %collective-permute-done.2 = f32[2,2,4,8,384]{4,3,2,1,0:T(8,128)S(1)} collective-permute-done((f32[2,2,4,8,384]{4,3,2,1,0:T(8,128)S(1)}, f32[2,2,4,8,384]{4,3,2,1,0:T(8,128)S(1)}, u32[]{:S(2)}, u32[]{:S(2)}) %collective-permute-start.2) | collective-permute-done | bytes 196640 | tf_op jit(solution)/shard_map/ppermute | solution.py:115
  76.2 17.3 %all_to_all.41 = bf16[16,32,288]{2,1,0:T(8,128)(2,1)} all-to-all(bf16[16,32,288]{2,1,0:T(8,128)(2,1)S(1)} %reshape.292), channel_id=1, replica_groups=mesh['lon'=16,'lat'=16,'segment'=2] {'lon'}, dimensions={0} | all-to-all | bytes 589824 | tf_op jit(solution)/shard_map/all_to_all | solution.py:91
  93.5 3.9 %shard_map.119 = bf16[512,96]{1,0:T(8,128)(2,1)} custom-call(bf16[512,288]{1,0:T(8,128)(2,1)} %bitcast.161, f32[3,8,512]{2,1,0:T(8,128)} %reshape.286.base_ref), custom_call_target="tpu_custom_call" | custom-call | tf_op jit(solution)/shard_map/pallas_call | solution.py:60
  97.4 13.4 %all_to_all.42 = bf16[16,32,96]{2,1,0:T(8,128)(2,1)S(1)} all-to-all(bf16[16,32,96]{2,1,0:T(8,128)(2,1)} %bitcast.173), channel_id=1, replica_groups=mesh['lon'=16,'lat'=16,'segment'=2] {'lon'}, dimensions={0} | all-to-all | bytes 196608 | tf_op jit(solution)/shard_map/all_to_all | solution.py:94
  111.5 3.9 %collective-permute-start.4 = (bf16[2,2,4,8,384]{4,3,2,1,0:T(8,128)(2,1)S(1)}, bf16[2,2,4,8,384]{4,3,2,1,0:T(8,128)(2,1)S(1)}, u32[]{:S(2)}, u32[]{:S(2)}) collective-permute-start(bf16[2,2,4,8,384]{4,3,2,1,0:T(8,128)(2,1)S(1)} %multiply_convert_fusion.7), channel_id=1, source_target_pairs={{2,0},{4,2},{6,4},{8,6},{10,8},{12,10},{14,12},{16,14},{18,16},{20... | collective-permute-start | bytes 294920 | tf_op jit(solution)/shard_map/ppermute | solution.py:25
  115.4 5.7 %collective-permute-start.3 = (bf16[2,2,4,8,384]{4,3,2,1,0:T(8,128)(2,1)S(1)}, bf16[2,2,4,8,384]{4,3,2,1,0:T(8,128)(2,1)S(1)}, u32[]{:S(2)}, u32[]{:S(2)}) collective-permute-start(bf16[2,2,4,8,384]{4,3,2,1,0:T(8,128)(2,1)S(1)} %multiply_convert_fusion.7), channel_id=1, source_target_pairs={{0,2},{2,4},{4,6},{6,8},{8,10},{10,12},{12,14},{14,16},{16,18},{18... | collective-permute-start | bytes 294920 | tf_op jit(solution)/shard_map/ppermute | solution.py:24
  121.5 1.3 collective-permute-done.3
  125.0 2.2 collective-permute-start.5
  127.2 4.2 %collective-permute-done.5 = f32[2,2,4,8,384]{4,3,2,1,0:T(8,128)S(1)} collective-permute-done((f32[2,2,4,8,384]{4,3,2,1,0:T(8,128)S(1)}, f32[2,2,4,8,384]{4,3,2,1,0:T(8,128)S(1)}, u32[]{:S(2)}, u32[]{:S(2)}) %collective-permute-start.5) | collective-permute-done | bytes 196640 | tf_op jit(solution)/shard_map/ppermute | solution.py:115
  133.0 15.3 %all_to_all.43 = bf16[16,32,288]{2,1,0:T(8,128)(2,1)} all-to-all(bf16[16,32,288]{2,1,0:T(8,128)(2,1)S(1)} %reshape.299), channel_id=1, replica_groups=mesh['lon'=16,'lat'=16,'segment'=2] {'lon'}, dimensions={0} | all-to-all | bytes 589824 | tf_op jit(solution)/shard_map/all_to_all | solution.py:91
  148.3 3.9 %shard_map.120 = bf16[512,96]{1,0:T(8,128)(2,1)} custom-call(bf16[512,288]{1,0:T(8,128)(2,1)} %bitcast.162, f32[3,8,512]{2,1,0:T(8,128)} %reshape.286.base_ref), custom_call_target="tpu_custom_call" | custom-call | tf_op jit(solution)/shard_map/pallas_call | solution.py:60
  152.2 13.5 %all_to_all.44 = bf16[16,32,96]{2,1,0:T(8,128)(2,1)S(1)} all-to-all(bf16[16,32,96]{2,1,0:T(8,128)(2,1)} %bitcast.174), channel_id=1, replica_groups=mesh['lon'=16,'lat'=16,'segment'=2] {'lon'}, dimensions={0} | all-to-all | bytes 196608 | tf_op jit(solution)/shard_map/all_to_all | solution.py:94
  166.5 3.1 %collective-permute-start.7 = (bf16[2,2,4,8,384]{4,3,2,1,0:T(8,128)(2,1)S(1)}, bf16[2,2,4,8,384]{4,3,2,1,0:T(8,128)(2,1)S(1)}, u32[]{:S(2)}, u32[]{:S(2)}) collective-permute-start(bf16[2,2,4,8,384]{4,3,2,1,0:T(8,128)(2,1)S(1)} %multiply_convert_fusion.4), channel_id=1, source_target_pairs={{2,0},{4,2},{6,4},{8,6},{10,8},{12,10},{14,12},{16,14},{18,16},{20... | collective-permute-start | bytes 294920 | tf_op jit(solution)/shard_map/ppermute | solution.py:25
  169.5 8.4 %collective-permute-start.6 = (bf16[2,2,4,8,384]{4,3,2,1,0:T(8,128)(2,1)S(1)}, bf16[2,2,4,8,384]{4,3,2,1,0:T(8,128)(2,1)S(1)}, u32[]{:S(2)}, u32[]{:S(2)}) collective-permute-start(bf16[2,2,4,8,384]{4,3,2,1,0:T(8,128)(2,1)S(1)} %multiply_convert_fusion.4), channel_id=1, source_target_pairs={{0,2},{2,4},{4,6},{6,8},{8,10},{10,12},{12,14},{14,16},{16,18},{18... | collective-permute-start | bytes 294920 | tf_op jit(solution)/shard_map/ppermute | solution.py:24
  178.3 1.3 collective-permute-done.6
  181.7 2.4 collective-permute-start.8
  184.1 4.1 %collective-permute-done.8 = f32[2,2,4,8,384]{4,3,2,1,0:T(8,128)S(1)} collective-permute-done((f32[2,2,4,8,384]{4,3,2,1,0:T(8,128)S(1)}, f32[2,2,4,8,384]{4,3,2,1,0:T(8,128)S(1)}, u32[]{:S(2)}, u32[]{:S(2)}) %collective-permute-start.8) | collective-permute-done | bytes 196640 | tf_op jit(solution)/shard_map/ppermute | solution.py:115
  189.8 13.9 %all_to_all.45 = bf16[16,32,288]{2,1,0:T(8,128)(2,1)} all-to-all(bf16[16,32,288]{2,1,0:T(8,128)(2,1)S(1)} %reshape.306), channel_id=1, replica_groups=mesh['lon'=16,'lat'=16,'segment'=2] {'lon'}, dimensions={0} | all-to-all | bytes 589824 | tf_op jit(solution)/shard_map/all_to_all | solution.py:91
  203.7 3.9 %shard_map.121 = bf16[512,96]{1,0:T(8,128)(2,1)} custom-call(bf16[512,288]{1,0:T(8,128)(2,1)} %bitcast.160, f32[3,8,512]{2,1,0:T(8,128)} %reshape.286.base_ref), custom_call_target="tpu_custom_call" | custom-call | tf_op jit(solution)/shard_map/pallas_call | solution.py:60
  207.6 13.0 %all_to_all.46 = bf16[16,32,96]{2,1,0:T(8,128)(2,1)S(1)} all-to-all(bf16[16,32,96]{2,1,0:T(8,128)(2,1)} %bitcast.171), channel_id=1, replica_groups=mesh['lon'=16,'lat'=16,'segment'=2] {'lon'}, dimensions={0} | all-to-all | bytes 196608 | tf_op jit(solution)/shard_map/all_to_all | solution.py:94
  221.3 1.9 collective-permute-start.10
  223.2 13.4 %collective-permute-start.9 = (bf16[2,2,4,8,384]{4,3,2,1,0:T(8,128)(2,1)S(1)}, bf16[2,2,4,8,384]{4,3,2,1,0:T(8,128)(2,1)S(1)}, u32[]{:S(2)}, u32[]{:S(2)}) collective-permute-start(bf16[2,2,4,8,384]{4,3,2,1,0:T(8,128)(2,1)S(1)} %multiply_convert_fusion.1), channel_id=1, source_target_pairs={{0,2},{2,4},{4,6},{6,8},{8,10},{10,12},{12,14},{14,16},{16,18},{18... | collective-permute-start | bytes 294920 | tf_op jit(solution)/shard_map/ppermute | solution.py:24
  237.0 1.3 collective-permute-done.9
  (117 shorter events, 27.8 us)
Async XLA Ops:
  0.0 66.1 %copy-start = (bf16[1,384,1536]{2,1,0:T(8,128)(2,1)S(1)}, bf16[1,384,1536]{2,1,0:T(8,128)(2,1)}, u32[]{:S(2)}) copy-start(bf16[1,384,1536]{2,1,0:T(8,128)(2,1)} %param.19) | copy-start | bytes 3538948
  0.0 11.2 %copy-start.1 = (bf16[1,384,1152]{2,1,0:T(8,128)(2,1)S(1)}, bf16[1,384,1152]{2,1,0:T(8,128)(2,1)}, u32[]{:S(2)}) copy-start(bf16[1,384,1152]{2,1,0:T(8,128)(2,1)} %param.17) | copy-start | bytes 2654212
  13.2 22.6 %all-to-all-start = ((bf16[16,32,288]{2,1,0:T(8,128)(2,1)}), bf16[16,32,288]{2,1,0:T(8,128)(2,1)}, u32[]{:S(2)}, u32[]{:S(2)}) async-start(bf16[16,32,288]{2,1,0:T(8,128)(2,1)} %reshape.284), calls=%async_computation | async-start | bytes 786432 | tf_op jit(solution)/shard_map/all_to_all | solution.py:91
  24.2 30.9 %copy-start.2 = (bf16[1,384,384]{2,1,0:T(8,128)(2,1)S(1)}, bf16[1,384,384]{2,1,0:T(8,128)(2,1)}, u32[]{:S(2)}) copy-start(bf16[1,384,384]{2,1,0:T(8,128)(2,1)} %param.18) | copy-start | bytes 884740
  24.5 30.9 %copy-start.3 = (f32[2,2,4,8,384]{4,3,2,1,0:T(8,128)S(1)}, f32[2,2,4,8,384]{4,3,2,1,0:T(8,128)}, u32[]{:S(2)}) copy-start(f32[2,2,4,8,384]{4,3,2,1,0:T(8,128)} %param.12) | copy-start | bytes 589828
  35.8 28.2 %copy-start.8 = (f32[1,5,384]{2,0,1:T(1,128)S(1)}, f32[1,5,384]{2,0,1:T(1,128)}, u32[]{:S(2)}) copy-start(f32[1,5,384]{2,0,1:T(1,128)} %param.22) | copy-start | bytes 23044
  55.8 8.5 %collective-permute-start.1 = (bf16[2,2,4,8,384]{4,3,2,1,0:T(8,128)(2,1)S(1)}, bf16[2,2,4,8,384]{4,3,2,1,0:T(8,128)(2,1)S(1)}, u32[]{:S(2)}, u32[]{:S(2)}) collective-permute-start(bf16[2,2,4,8,384]{4,3,2,1,0:T(8,128)(2,1)S(1)} %multiply_convert_fusion.10), channel_id=1, source_target_pairs={{2,0},{4,2},{6,4},{8,6},{10,8},{12,10},{14,12},{16,14},{18,16},{20... | collective-permute-start | bytes 294920 | tf_op jit(solution)/shard_map/ppermute | solution.py:25
  60.1 5.5 %collective-permute-start = (bf16[2,2,4,8,384]{4,3,2,1,0:T(8,128)(2,1)S(1)}, bf16[2,2,4,8,384]{4,3,2,1,0:T(8,128)(2,1)S(1)}, u32[]{:S(2)}, u32[]{:S(2)}) collective-permute-start(bf16[2,2,4,8,384]{4,3,2,1,0:T(8,128)(2,1)S(1)} %multiply_convert_fusion.10), channel_id=1, source_target_pairs={{0,2},{2,4},{4,6},{6,8},{8,10},{10,12},{12,14},{14,16},{16,18},{18... | collective-permute-start | bytes 294920 | tf_op jit(solution)/shard_map/ppermute | solution.py:24
  66.1 1.3 copy-start.4
  67.7 6.8 %collective-permute-start.2 = (f32[2,2,4,8,384]{4,3,2,1,0:T(8,128)S(1)}, f32[2,2,4,8,384]{4,3,2,1,0:T(8,128)S(1)}, u32[]{:S(2)}, u32[]{:S(2)}) collective-permute-start(f32[2,2,4,8,384]{4,3,2,1,0:T(8,128)S(1)} %fusion.16), channel_id=1, source_target_pairs={{0,1},{1,0},{2,3},{3,2},{4,5},{5,4},{6,7},{7,6},{8,9},{9,8},{10,11... | collective-permute-start | bytes 589832 | tf_op jit(solution)/shard_map/ppermute | solution.py:115
  111.5 10.0 %collective-permute-start.4 = (bf16[2,2,4,8,384]{4,3,2,1,0:T(8,128)(2,1)S(1)}, bf16[2,2,4,8,384]{4,3,2,1,0:T(8,128)(2,1)S(1)}, u32[]{:S(2)}, u32[]{:S(2)}) collective-permute-start(bf16[2,2,4,8,384]{4,3,2,1,0:T(8,128)(2,1)S(1)} %multiply_convert_fusion.7), channel_id=1, source_target_pairs={{2,0},{4,2},{6,4},{8,6},{10,8},{12,10},{14,12},{16,14},{18,16},{20... | collective-permute-start | bytes 294920 | tf_op jit(solution)/shard_map/ppermute | solution.py:25
  115.4 7.4 %collective-permute-start.3 = (bf16[2,2,4,8,384]{4,3,2,1,0:T(8,128)(2,1)S(1)}, bf16[2,2,4,8,384]{4,3,2,1,0:T(8,128)(2,1)S(1)}, u32[]{:S(2)}, u32[]{:S(2)}) collective-permute-start(bf16[2,2,4,8,384]{4,3,2,1,0:T(8,128)(2,1)S(1)} %multiply_convert_fusion.7), channel_id=1, source_target_pairs={{0,2},{2,4},{4,6},{6,8},{8,10},{10,12},{12,14},{14,16},{16,18},{18... | collective-permute-start | bytes 294920 | tf_op jit(solution)/shard_map/ppermute | solution.py:24
  123.3 1.3 copy-start.5
  125.0 6.4 %collective-permute-start.5 = (f32[2,2,4,8,384]{4,3,2,1,0:T(8,128)S(1)}, f32[2,2,4,8,384]{4,3,2,1,0:T(8,128)S(1)}, u32[]{:S(2)}, u32[]{:S(2)}) collective-permute-start(f32[2,2,4,8,384]{4,3,2,1,0:T(8,128)S(1)} %fusion.19), channel_id=1, source_target_pairs={{0,1},{1,0},{2,3},{3,2},{4,5},{5,4},{6,7},{7,6},{8,9},{9,8},{10,11... | collective-permute-start | bytes 589832 | tf_op jit(solution)/shard_map/ppermute | solution.py:115
  166.5 11.8 %collective-permute-start.7 = (bf16[2,2,4,8,384]{4,3,2,1,0:T(8,128)(2,1)S(1)}, bf16[2,2,4,8,384]{4,3,2,1,0:T(8,128)(2,1)S(1)}, u32[]{:S(2)}, u32[]{:S(2)}) collective-permute-start(bf16[2,2,4,8,384]{4,3,2,1,0:T(8,128)(2,1)S(1)} %multiply_convert_fusion.4), channel_id=1, source_target_pairs={{2,0},{4,2},{6,4},{8,6},{10,8},{12,10},{14,12},{16,14},{18,16},{20... | collective-permute-start | bytes 294920 | tf_op jit(solution)/shard_map/ppermute | solution.py:25
  169.5 10.0 %collective-permute-start.6 = (bf16[2,2,4,8,384]{4,3,2,1,0:T(8,128)(2,1)S(1)}, bf16[2,2,4,8,384]{4,3,2,1,0:T(8,128)(2,1)S(1)}, u32[]{:S(2)}, u32[]{:S(2)}) collective-permute-start(bf16[2,2,4,8,384]{4,3,2,1,0:T(8,128)(2,1)S(1)} %multiply_convert_fusion.4), channel_id=1, source_target_pairs={{0,2},{2,4},{4,6},{6,8},{8,10},{10,12},{12,14},{14,16},{16,18},{18... | collective-permute-start | bytes 294920 | tf_op jit(solution)/shard_map/ppermute | solution.py:24
  180.1 1.3 copy-start.6
  181.7 6.4 %collective-permute-start.8 = (f32[2,2,4,8,384]{4,3,2,1,0:T(8,128)S(1)}, f32[2,2,4,8,384]{4,3,2,1,0:T(8,128)S(1)}, u32[]{:S(2)}, u32[]{:S(2)}) collective-permute-start(f32[2,2,4,8,384]{4,3,2,1,0:T(8,128)S(1)} %fusion.22), channel_id=1, source_target_pairs={{0,1},{1,0},{2,3},{3,2},{4,5},{5,4},{6,7},{7,6},{8,9},{9,8},{10,11... | collective-permute-start | bytes 589832 | tf_op jit(solution)/shard_map/ppermute | solution.py:115
  221.3 15.7 %collective-permute-start.10 = (bf16[2,2,4,8,384]{4,3,2,1,0:T(8,128)(2,1)S(1)}, bf16[2,2,4,8,384]{4,3,2,1,0:T(8,128)(2,1)S(1)}, u32[]{:S(2)}, u32[]{:S(2)}) collective-permute-start(bf16[2,2,4,8,384]{4,3,2,1,0:T(8,128)(2,1)S(1)} %multiply_convert_fusion.1), channel_id=1, source_target_pairs={{2,0},{4,2},{6,4},{8,6},{10,8},{12,10},{14,12},{16,14},{18,16},{20... | collective-permute-start | bytes 294920 | tf_op jit(solution)/shard_map/ppermute | solution.py:25
  223.2 15.0 %collective-permute-start.9 = (bf16[2,2,4,8,384]{4,3,2,1,0:T(8,128)(2,1)S(1)}, bf16[2,2,4,8,384]{4,3,2,1,0:T(8,128)(2,1)S(1)}, u32[]{:S(2)}, u32[]{:S(2)}) collective-permute-start(bf16[2,2,4,8,384]{4,3,2,1,0:T(8,128)(2,1)S(1)} %multiply_convert_fusion.1), channel_id=1, source_target_pairs={{0,2},{2,4},{4,6},{6,8},{8,10},{10,12},{12,14},{14,16},{16,18},{18... | collective-permute-start | bytes 294920 | tf_op jit(solution)/shard_map/ppermute | solution.py:24
  238.8 1.3 copy-start.7

commit v9 on v7

--- a/solution.py
+++ b/solution.py
@@ -151,7 +151,7 @@
         result = block(current, lead_steps[tick_num // 2], mask_ids, params, bias_full)
         if tick_num == 3:
             break
-        current = from_partner(result)
+        current = from_partner(result.astype(jnp.bfloat16)).astype(result.dtype)
         if tick_num == 1:
             first = current
     output = jnp.where(segment_first, first, result)

time: 242 us -> 240 us (level)
  starting transfers between devices: 61.7 us -> 51.1 us
  blocking collectives: 102 us -> 106 us
  waiting for transfers between devices: 29.6 us -> 33.2 us
    ppermute x4, waiting for transfers between devices: 1.38 us -> 12.3 us  [lat_halo(): after = lax.ppermute(array[:, :width], 'lat', down)]
    ppermute x4, starting transfers between devices: 31.5 us -> 24.5 us  [lat_halo(): before = lax.ppermute(array[:, length - width:], 'lat', up)]
    all_to_all x3, blocking collectives: 46.4 us -> 50.3 us  [block(): incoming = lax.all_to_all(outgoing, 'lon', 0, 0, tiled=True)]
    ppermute x4, waiting for transfers between devices: 5.04 us -> 1.27 us  [lat_halo(): before = lax.ppermute(array[:, length - width:], 'lat', up)]
    ppermute x3, waiting for transfers between devices: 13 us -> 9.37 us  [from_partner(): lax.ppermute(array, 'segment', [(i, i ^ 1) for i in range(lax.axis_size('...]
    ppermute x4, starting transfers between devices: 13.2 us -> 9.66 us  [lat_halo(): after = lax.ppermute(array[:, :width], 'lat', down)]
  transfers between devices with their start and end apart: 12 -> 12, of which waited for: 12 -> 9; matrix products, arithmetic and copies ran while one was open for 1% -> 1% of each run, Pallas kernels for 0% -> 0%
where the time goes in v9:
time: 240 us; the launch traced here: 238 us
  blocking collectives  106 us (44%)
  starting transfers between devices  51.1 us (21%)
  waiting for transfers between devices  33.2 us (14%)
  Pallas kernels  15.6 us (6%)
  local copies, waits for them, and re-layouts  11.6 us (5%)
  other arithmetic  9.03 us (4%)
  matrix products  6.76 us (3%)
  between operations  4.74 us (2%)
    all_to_all x4, blocking collectives, block(): returned = lax.all_to_all(back, 'lon', 0, 0, tiled=True)  55.3 us
    all_to_all x3, blocking collectives, block(): incoming = lax.all_to_all(outgoing, 'lon', 0, 0, tiled=True)  50.3 us
    ppermute x4, starting transfers between devices, lat_halo(): before = lax.ppermute(array[:, length - width:], 'lat', up)  24.5 us
    pallas_call x4, Pallas kernels, attend(): pl.pallas_call(functools.partial(attention_kernel, heads=heads, head_dim=...  15.6 us
    ppermute x4, waiting for transfers between devices, lat_halo(): after = lax.ppermute(array[:, :width], 'lat', down)  12.3 us
    all_to_all x1, waiting for transfers between devices, block(): incoming = lax.all_to_all(outgoing, 'lon', 0, 0, tiled=True)  10.3 us
    all_to_all x1, starting transfers between devices, block(): incoming = lax.all_to_all(outgoing, 'lon', 0, 0, tiled=True)  10.3 us
    ppermute x4, starting transfers between devices, lat_halo(): after = lax.ppermute(array[:, :width], 'lat', down)  9.66 us
  transfers between devices with their start and end apart: 12, of which 9 were waited for; matrix products, arithmetic and copies ran while one was open for 1% of the time, Pallas kernels for 0%

profile of v9, /device:TPU:1, one launch (start us, length us, event | category | flops | bytes accessed | tf_op | source)
XLA Modules:
  0.0 237.6 jit_solution(13672215521276578035)
XLA Ops:
  0.0 1.5 fusion.125
  14.2 10.3 %all-to-all-start = ((bf16[16,32,288]{2,1,0:T(8,128)(2,1)}), bf16[16,32,288]{2,1,0:T(8,128)(2,1)}, u32[]{:S(2)}, u32[]{:S(2)}) async-start(bf16[16,32,288]{2,1,0:T(8,128)(2,1)} %bitcast.7), calls=%async_computation | async-start | bytes 786432 | tf_op jit(solution)/shard_map/all_to_all | solution.py:90
  26.5 10.3 %all-to-all-done = bf16[16,32,288]{2,1,0:T(8,128)(2,1)} async-done(((bf16[16,32,288]{2,1,0:T(8,128)(2,1)}), bf16[16,32,288]{2,1,0:T(8,128)(2,1)}, u32[]{:S(2)}, u32[]{:S(2)}) %all-to-all-start) | async-done | bytes 294944 | tf_op jit(solution)/shard_map/all_to_all | solution.py:90
  36.8 3.9 %shard_map.118 = bf16[512,96]{1,0:T(8,128)(2,1)} custom-call(bf16[512,288]{1,0:T(8,128)(2,1)} %bitcast.8.x_ref, f32[3,8,512]{2,1,0:T(8,128)} %reshape.272.base_ref), custom_call_target="tpu_custom_call" | custom-call | tf_op jit(solution)/shard_map/pallas_call | solution.py:60
  40.7 15.4 %all_to_all.40 = bf16[16,32,96]{2,1,0:T(8,128)(2,1)S(1)} all-to-all(bf16[16,32,96]{2,1,0:T(8,128)(2,1)} %bitcast.193), channel_id=1, replica_groups=mesh['lon'=16,'lat'=16,'segment'=2] {'lon'}, dimensions={0} | all-to-all | bytes 196608 | tf_op jit(solution)/shard_map/all_to_all | solution.py:93
  56.8 6.3 %collective-permute-start = (bf16[2,2,4,8,384]{4,3,1,0,2:T(8,128)(2,1)S(1)}, bf16[2,2,4,8,384]{4,3,1,0,2:T(8,128)(2,1)S(1)}, u32[]{:S(2)}, u32[]{:S(2)}) collective-permute-start(bf16[2,2,4,8,384]{4,3,1,0,2:T(8,128)(2,1)S(1)} %multiply_convert_fusion.9), channel_id=1, source_target_pairs={{0,2},{2,4},{4,6},{6,8},{8,10},{10,12},{12,14},{14,16},{16,18},{18... | collective-permute-start | bytes 294920 | tf_op jit(solution)/shard_map/ppermute | solution.py:24
  63.1 1.9 collective-permute-start.1
  65.1 4.0 %collective-permute-done.1 = bf16[2,2,4,8,384]{4,3,1,0,2:T(8,128)(2,1)S(1)} collective-permute-done((bf16[2,2,4,8,384]{4,3,1,0,2:T(8,128)(2,1)S(1)}, bf16[2,2,4,8,384]{4,3,1,0,2:T(8,128)(2,1)S(1)}, u32[]{:S(2)}, u32[]{:S(2)}) %collective-permute-start.1) | collective-permute-done | bytes 98336 | tf_op jit(solution)/shard_map/ppermute | solution.py:25
  71.2 2.2 collective-permute-start.2
  73.4 3.1 %collective-permute-done.2 = bf16[2,2,4,8,384]{4,3,1,0,2:T(8,128)(2,1)S(1)} collective-permute-done((bf16[2,2,4,8,384]{4,3,1,0,2:T(8,128)(2,1)S(1)}, bf16[2,2,4,8,384]{4,3,1,0,2:T(8,128)(2,1)S(1)}, u32[]{:S(2)}, u32[]{:S(2)}) %collective-permute-start.2) | collective-permute-done | bytes 98336 | tf_op jit(solution)/shard_map/ppermute | solution.py:114
  77.6 16.7 %all_to_all.41 = bf16[16,32,288]{2,1,0:T(8,128)(2,1)} all-to-all(bf16[16,32,288]{2,1,0:T(8,128)(2,1)S(1)} %bitcast.185), channel_id=1, replica_groups=mesh['lon'=16,'lat'=16,'segment'=2] {'lon'}, dimensions={0} | all-to-all | bytes 589824 | tf_op jit(solution)/shard_map/all_to_all | solution.py:90
  94.3 3.9 %shard_map.119 = bf16[512,96]{1,0:T(8,128)(2,1)} custom-call(bf16[512,288]{1,0:T(8,128)(2,1)} %bitcast.183, f32[3,8,512]{2,1,0:T(8,128)} %reshape.272.base_ref), custom_call_target="tpu_custom_call" | custom-call | tf_op jit(solution)/shard_map/pallas_call | solution.py:60
  98.2 13.3 %all_to_all.42 = bf16[16,32,96]{2,1,0:T(8,128)(2,1)S(1)} all-to-all(bf16[16,32,96]{2,1,0:T(8,128)(2,1)} %bitcast.194), channel_id=1, replica_groups=mesh['lon'=16,'lat'=16,'segment'=2] {'lon'}, dimensions={0} | all-to-all | bytes 196608 | tf_op jit(solution)/shard_map/all_to_all | solution.py:93
  112.3 6.7 %collective-permute-start.3 = (bf16[2,2,4,8,384]{4,3,1,0,2:T(8,128)(2,1)S(1)}, bf16[2,2,4,8,384]{4,3,1,0,2:T(8,128)(2,1)S(1)}, u32[]{:S(2)}, u32[]{:S(2)}) collective-permute-start(bf16[2,2,4,8,384]{4,3,1,0,2:T(8,128)(2,1)S(1)} %multiply_convert_fusion.6), channel_id=1, source_target_pairs={{0,2},{2,4},{4,6},{6,8},{8,10},{10,12},{12,14},{14,16},{16,18},{18... | collective-permute-start | bytes 294920 | tf_op jit(solution)/shard_map/ppermute | solution.py:24
  119.0 1.9 collective-permute-start.4
  121.0 4.0 %collective-permute-done.4 = bf16[2,2,4,8,384]{4,3,1,0,2:T(8,128)(2,1)S(1)} collective-permute-done((bf16[2,2,4,8,384]{4,3,1,0,2:T(8,128)(2,1)S(1)}, bf16[2,2,4,8,384]{4,3,1,0,2:T(8,128)(2,1)S(1)}, u32[]{:S(2)}, u32[]{:S(2)}) %collective-permute-start.4) | collective-permute-done | bytes 98336 | tf_op jit(solution)/shard_map/ppermute | solution.py:25
  127.2 2.2 collective-permute-start.5
  129.4 3.1 %collective-permute-done.5 = bf16[2,2,4,8,384]{4,3,1,0,2:T(8,128)(2,1)S(1)} collective-permute-done((bf16[2,2,4,8,384]{4,3,1,0,2:T(8,128)(2,1)S(1)}, bf16[2,2,4,8,384]{4,3,1,0,2:T(8,128)(2,1)S(1)}, u32[]{:S(2)}, u32[]{:S(2)}) %collective-permute-start.5) | collective-permute-done | bytes 98336 | tf_op jit(solution)/shard_map/ppermute | solution.py:114
  133.6 16.8 %all_to_all.43 = bf16[16,32,288]{2,1,0:T(8,128)(2,1)} all-to-all(bf16[16,32,288]{2,1,0:T(8,128)(2,1)S(1)} %bitcast.186), channel_id=1, replica_groups=mesh['lon'=16,'lat'=16,'segment'=2] {'lon'}, dimensions={0} | all-to-all | bytes 589824 | tf_op jit(solution)/shard_map/all_to_all | solution.py:90
  150.5 3.9 %shard_map.120 = bf16[512,96]{1,0:T(8,128)(2,1)} custom-call(bf16[512,288]{1,0:T(8,128)(2,1)} %bitcast.184, f32[3,8,512]{2,1,0:T(8,128)} %reshape.272.base_ref), custom_call_target="tpu_custom_call" | custom-call | tf_op jit(solution)/shard_map/pallas_call | solution.py:60
  154.4 13.3 %all_to_all.44 = bf16[16,32,96]{2,1,0:T(8,128)(2,1)S(1)} all-to-all(bf16[16,32,96]{2,1,0:T(8,128)(2,1)} %bitcast.195), channel_id=1, replica_groups=mesh['lon'=16,'lat'=16,'segment'=2] {'lon'}, dimensions={0} | all-to-all | bytes 196608 | tf_op jit(solution)/shard_map/all_to_all | solution.py:93
  168.5 6.7 %collective-permute-start.6 = (bf16[2,2,4,8,384]{4,3,1,0,2:T(8,128)(2,1)S(1)}, bf16[2,2,4,8,384]{4,3,1,0,2:T(8,128)(2,1)S(1)}, u32[]{:S(2)}, u32[]{:S(2)}) collective-permute-start(bf16[2,2,4,8,384]{4,3,1,0,2:T(8,128)(2,1)S(1)} %multiply_convert_fusion.4), channel_id=1, source_target_pairs={{0,2},{2,4},{4,6},{6,8},{8,10},{10,12},{12,14},{14,16},{16,18},{18... | collective-permute-start | bytes 294920 | tf_op jit(solution)/shard_map/ppermute | solution.py:24
  175.2 1.9 collective-permute-start.7
  177.1 4.0 %collective-permute-done.7 = bf16[2,2,4,8,384]{4,3,1,0,2:T(8,128)(2,1)S(1)} collective-permute-done((bf16[2,2,4,8,384]{4,3,1,0,2:T(8,128)(2,1)S(1)}, bf16[2,2,4,8,384]{4,3,1,0,2:T(8,128)(2,1)S(1)}, u32[]{:S(2)}, u32[]{:S(2)}) %collective-permute-start.7) | collective-permute-done | bytes 98336 | tf_op jit(solution)/shard_map/ppermute | solution.py:25
  183.3 2.2 collective-permute-start.8
  185.6 3.1 %collective-permute-done.8 = bf16[2,2,4,8,384]{4,3,1,0,2:T(8,128)(2,1)S(1)} collective-permute-done((bf16[2,2,4,8,384]{4,3,1,0,2:T(8,128)(2,1)S(1)}, bf16[2,2,4,8,384]{4,3,1,0,2:T(8,128)(2,1)S(1)}, u32[]{:S(2)}, u32[]{:S(2)}) %collective-permute-start.8) | collective-permute-done | bytes 98336 | tf_op jit(solution)/shard_map/ppermute | solution.py:114
  189.8 16.8 %all_to_all.45 = bf16[16,32,288]{2,1,0:T(8,128)(2,1)} all-to-all(bf16[16,32,288]{2,1,0:T(8,128)(2,1)S(1)} %bitcast.187), channel_id=1, replica_groups=mesh['lon'=16,'lat'=16,'segment'=2] {'lon'}, dimensions={0} | all-to-all | bytes 589824 | tf_op jit(solution)/shard_map/all_to_all | solution.py:90
  206.6 3.9 %shard_map.121 = bf16[512,96]{1,0:T(8,128)(2,1)} custom-call(bf16[512,288]{1,0:T(8,128)(2,1)} %bitcast.182, f32[3,8,512]{2,1,0:T(8,128)} %reshape.272.base_ref), custom_call_target="tpu_custom_call" | custom-call | tf_op jit(solution)/shard_map/pallas_call | solution.py:60
  210.5 13.3 %all_to_all.46 = bf16[16,32,96]{2,1,0:T(8,128)(2,1)S(1)} all-to-all(bf16[16,32,96]{2,1,0:T(8,128)(2,1)} %bitcast.192), channel_id=1, replica_groups=mesh['lon'=16,'lat'=16,'segment'=2] {'lon'}, dimensions={0} | all-to-all | bytes 196608 | tf_op jit(solution)/shard_map/all_to_all | solution.py:93
  224.5 3.9 %collective-permute-start.10 = (bf16[2,2,4,8,384]{4,3,1,0,2:T(8,128)(2,1)S(1)}, bf16[2,2,4,8,384]{4,3,1,0,2:T(8,128)(2,1)S(1)}, u32[]{:S(2)}, u32[]{:S(2)}) collective-permute-start(bf16[2,2,4,8,384]{4,3,1,0,2:T(8,128)(2,1)S(1)} %multiply_convert_fusion.1), channel_id=1, source_target_pairs={{2,0},{4,2},{6,4},{8,6},{10,8},{12,10},{14,12},{16,14},{18,16},{20... | collective-permute-start | bytes 294920 | tf_op jit(solution)/shard_map/ppermute | solution.py:25
  228.4 4.7 %collective-permute-start.9 = (bf16[2,2,4,8,384]{4,3,1,0,2:T(8,128)(2,1)S(1)}, bf16[2,2,4,8,384]{4,3,1,0,2:T(8,128)(2,1)S(1)}, u32[]{:S(2)}, u32[]{:S(2)}) collective-permute-start(bf16[2,2,4,8,384]{4,3,1,0,2:T(8,128)(2,1)S(1)} %multiply_convert_fusion.1), channel_id=1, source_target_pairs={{0,2},{2,4},{4,6},{6,8},{8,10},{10,12},{12,14},{14,16},{16,18},{18... | collective-permute-start | bytes 294920 | tf_op jit(solution)/shard_map/ppermute | solution.py:24
  233.5 1.3 collective-permute-done.9
  (121 shorter events, 26.3 us)
Async XLA Ops:
  0.0 69.5 %copy-start = (bf16[1,384,1536]{2,1,0:T(8,128)(2,1)S(1)}, bf16[1,384,1536]{2,1,0:T(8,128)(2,1)}, u32[]{:S(2)}) copy-start(bf16[1,384,1536]{2,1,0:T(8,128)(2,1)} %param.19) | copy-start | bytes 3538948
  0.0 11.9 %copy-start.3 = (bf16[1,384,1152]{2,1,0:T(8,128)(2,1)S(1)}, bf16[1,384,1152]{2,1,0:T(8,128)(2,1)}, u32[]{:S(2)}) copy-start(bf16[1,384,1152]{2,1,0:T(8,128)(2,1)} %param.17) | copy-start | bytes 2654212
  14.2 22.5 %all-to-all-start = ((bf16[16,32,288]{2,1,0:T(8,128)(2,1)}), bf16[16,32,288]{2,1,0:T(8,128)(2,1)}, u32[]{:S(2)}, u32[]{:S(2)}) async-start(bf16[16,32,288]{2,1,0:T(8,128)(2,1)} %bitcast.7), calls=%async_computation | async-start | bytes 786432 | tf_op jit(solution)/shard_map/all_to_all | solution.py:90
  25.2 30.8 %copy-start.1 = (bf16[1,384,384]{2,1,0:T(8,128)(2,1)S(1)}, bf16[1,384,384]{2,1,0:T(8,128)(2,1)}, u32[]{:S(2)}) copy-start(bf16[1,384,384]{2,1,0:T(8,128)(2,1)} %param.18) | copy-start | bytes 884740
  25.5 30.8 %copy-start.2 = (f32[2,2,4,8,384]{4,3,2,1,0:T(8,128)S(1)}, f32[2,2,4,8,384]{4,3,2,1,0:T(8,128)}, u32[]{:S(2)}) copy-start(f32[2,2,4,8,384]{4,3,2,1,0:T(8,128)} %param.12) | copy-start | bytes 589828
  36.8 28.2 %copy-start.4 = (f32[1,5,384]{2,0,1:T(1,128)S(1)}, f32[1,5,384]{2,0,1:T(1,128)}, u32[]{:S(2)}) copy-start(f32[1,5,384]{2,0,1:T(1,128)} %param.22) | copy-start | bytes 23044
  56.8 8.3 %collective-permute-start = (bf16[2,2,4,8,384]{4,3,1,0,2:T(8,128)(2,1)S(1)}, bf16[2,2,4,8,384]{4,3,1,0,2:T(8,128)(2,1)S(1)}, u32[]{:S(2)}, u32[]{:S(2)}) collective-permute-start(bf16[2,2,4,8,384]{4,3,1,0,2:T(8,128)(2,1)S(1)} %multiply_convert_fusion.9), channel_id=1, source_target_pairs={{0,2},{2,4},{4,6},{6,8},{8,10},{10,12},{12,14},{14,16},{16,18},{18... | collective-permute-start | bytes 294920 | tf_op jit(solution)/shard_map/ppermute | solution.py:24
  63.1 5.9 %collective-permute-start.1 = (bf16[2,2,4,8,384]{4,3,1,0,2:T(8,128)(2,1)S(1)}, bf16[2,2,4,8,384]{4,3,1,0,2:T(8,128)(2,1)S(1)}, u32[]{:S(2)}, u32[]{:S(2)}) collective-permute-start(bf16[2,2,4,8,384]{4,3,1,0,2:T(8,128)(2,1)S(1)} %multiply_convert_fusion.9), channel_id=1, source_target_pairs={{2,0},{4,2},{6,4},{8,6},{10,8},{12,10},{14,12},{16,14},{18,16},{20... | collective-permute-start | bytes 294920 | tf_op jit(solution)/shard_map/ppermute | solution.py:25
  69.6 1.3 copy-start.5
  71.2 5.4 %collective-permute-start.2 = (bf16[2,2,4,8,384]{4,3,1,0,2:T(8,128)(2,1)S(1)}, bf16[2,2,4,8,384]{4,3,1,0,2:T(8,128)(2,1)S(1)}, u32[]{:S(2)}, u32[]{:S(2)}) collective-permute-start(bf16[2,2,4,8,384]{4,3,1,0,2:T(8,128)(2,1)S(1)} %fusion.40), channel_id=1, source_target_pairs={{0,1},{1,0},{2,3},{3,2},{4,5},{5,4},{6,7},{7,6},{8,9},{9,8},{10,11... | collective-permute-start | bytes 294920 | tf_op jit(solution)/shard_map/ppermute | solution.py:114
  112.3 8.7 %collective-permute-start.3 = (bf16[2,2,4,8,384]{4,3,1,0,2:T(8,128)(2,1)S(1)}, bf16[2,2,4,8,384]{4,3,1,0,2:T(8,128)(2,1)S(1)}, u32[]{:S(2)}, u32[]{:S(2)}) collective-permute-start(bf16[2,2,4,8,384]{4,3,1,0,2:T(8,128)(2,1)S(1)} %multiply_convert_fusion.6), channel_id=1, source_target_pairs={{0,2},{2,4},{4,6},{6,8},{8,10},{10,12},{12,14},{14,16},{16,18},{18... | collective-permute-start | bytes 294920 | tf_op jit(solution)/shard_map/ppermute | solution.py:24
  119.0 5.9 %collective-permute-start.4 = (bf16[2,2,4,8,384]{4,3,1,0,2:T(8,128)(2,1)S(1)}, bf16[2,2,4,8,384]{4,3,1,0,2:T(8,128)(2,1)S(1)}, u32[]{:S(2)}, u32[]{:S(2)}) collective-permute-start(bf16[2,2,4,8,384]{4,3,1,0,2:T(8,128)(2,1)S(1)} %multiply_convert_fusion.6), channel_id=1, source_target_pairs={{2,0},{4,2},{6,4},{8,6},{10,8},{12,10},{14,12},{16,14},{18,16},{20... | collective-permute-start | bytes 294920 | tf_op jit(solution)/shard_map/ppermute | solution.py:25
  125.5 1.3 copy-start.6
  127.2 5.4 %collective-permute-start.5 = (bf16[2,2,4,8,384]{4,3,1,0,2:T(8,128)(2,1)S(1)}, bf16[2,2,4,8,384]{4,3,1,0,2:T(8,128)(2,1)S(1)}, u32[]{:S(2)}, u32[]{:S(2)}) collective-permute-start(bf16[2,2,4,8,384]{4,3,1,0,2:T(8,128)(2,1)S(1)} %fusion.37), channel_id=1, source_target_pairs={{0,1},{1,0},{2,3},{3,2},{4,5},{5,4},{6,7},{7,6},{8,9},{9,8},{10,11... | collective-permute-start | bytes 294920 | tf_op jit(solution)/shard_map/ppermute | solution.py:114
  168.5 8.7 %collective-permute-start.6 = (bf16[2,2,4,8,384]{4,3,1,0,2:T(8,128)(2,1)S(1)}, bf16[2,2,4,8,384]{4,3,1,0,2:T(8,128)(2,1)S(1)}, u32[]{:S(2)}, u32[]{:S(2)}) collective-permute-start(bf16[2,2,4,8,384]{4,3,1,0,2:T(8,128)(2,1)S(1)} %multiply_convert_fusion.4), channel_id=1, source_target_pairs={{0,2},{2,4},{4,6},{6,8},{8,10},{10,12},{12,14},{14,16},{16,18},{18... | collective-permute-start | bytes 294920 | tf_op jit(solution)/shard_map/ppermute | solution.py:24
  175.2 5.9 %collective-permute-start.7 = (bf16[2,2,4,8,384]{4,3,1,0,2:T(8,128)(2,1)S(1)}, bf16[2,2,4,8,384]{4,3,1,0,2:T(8,128)(2,1)S(1)}, u32[]{:S(2)}, u32[]{:S(2)}) collective-permute-start(bf16[2,2,4,8,384]{4,3,1,0,2:T(8,128)(2,1)S(1)} %multiply_convert_fusion.4), channel_id=1, source_target_pairs={{2,0},{4,2},{6,4},{8,6},{10,8},{12,10},{14,12},{16,14},{18,16},{20... | collective-permute-start | bytes 294920 | tf_op jit(solution)/shard_map/ppermute | solution.py:25
  181.7 1.3 copy-start.7
  183.3 5.4 %collective-permute-start.8 = (bf16[2,2,4,8,384]{4,3,1,0,2:T(8,128)(2,1)S(1)}, bf16[2,2,4,8,384]{4,3,1,0,2:T(8,128)(2,1)S(1)}, u32[]{:S(2)}, u32[]{:S(2)}) collective-permute-start(bf16[2,2,4,8,384]{4,3,1,0,2:T(8,128)(2,1)S(1)} %fusion.34), channel_id=1, source_target_pairs={{0,1},{1,0},{2,3},{3,2},{4,5},{5,4},{6,7},{7,6},{8,9},{9,8},{10,11... | collective-permute-start | bytes 294920 | tf_op jit(solution)/shard_map/ppermute | solution.py:114
  224.5 9.0 %collective-permute-start.10 = (bf16[2,2,4,8,384]{4,3,1,0,2:T(8,128)(2,1)S(1)}, bf16[2,2,4,8,384]{4,3,1,0,2:T(8,128)(2,1)S(1)}, u32[]{:S(2)}, u32[]{:S(2)}) collective-permute-start(bf16[2,2,4,8,384]{4,3,1,0,2:T(8,128)(2,1)S(1)} %multiply_convert_fusion.1), channel_id=1, source_target_pairs={{2,0},{4,2},{6,4},{8,6},{10,8},{12,10},{14,12},{16,14},{18,16},{20... | collective-permute-start | bytes 294920 | tf_op jit(solution)/shard_map/ppermute | solution.py:25
  228.4 6.4 %collective-permute-start.9 = (bf16[2,2,4,8,384]{4,3,1,0,2:T(8,128)(2,1)S(1)}, bf16[2,2,4,8,384]{4,3,1,0,2:T(8,128)(2,1)S(1)}, u32[]{:S(2)}, u32[]{:S(2)}) collective-permute-start(bf16[2,2,4,8,384]{4,3,1,0,2:T(8,128)(2,1)S(1)} %multiply_convert_fusion.1), channel_id=1, source_target_pairs={{0,2},{2,4},{4,6},{6,8},{8,10},{10,12},{12,14},{14,16},{16,18},{18... | collective-permute-start | bytes 294920 | tf_op jit(solution)/shard_map/ppermute | solution.py:24
  235.3 1.3 copy-start.8

commit v10 on v9

--- a/solution.py
+++ b/solution.py
@@ -33,36 +33,37 @@
     return jnp.repeat(picked, levels, axis=2)
 
 
-def attention_kernel(x_ref, base_ref, o_ref, bias_ref, *, heads, head_dim, levels):
+def attention_kernel(x_ref, base_ref, o_ref, *, heads, head_dim, levels, chunk):
     width = heads * head_dim
     lon_total = x_ref.shape[0] // levels
     for h in range(heads):
         base = base_ref[h]
-        for i in range(lon_total):
-            rotated = base if i == 0 else pltpu.roll(base, i * levels, 1)
-            bias_ref[h, i * levels : (i + 1) * levels, :] = rotated
-    for h in range(heads):
-        cols = slice(h * head_dim, (h + 1) * head_dim)
-        q = x_ref[:, cols]
         k = x_ref[:, width + h * head_dim : width + (h + 1) * head_dim]
         v = x_ref[:, 2 * width + h * head_dim : 2 * width + (h + 1) * head_dim]
-        s = lax.dot_general(q, k, (((1,), (1,)), ((), ())), preferred_element_type=jnp.float32)
-        s = s * (head_dim ** (-0.5)) + bias_ref[h]
-        row_max = jnp.max(s, axis=-1, keepdims=True)
-        weights = jnp.exp(s - row_max)
-        total = jnp.sum(weights, axis=-1, keepdims=True)
-        summed = jnp.dot(weights.astype(jnp.bfloat16), v, preferred_element_type=jnp.float32)
-        o_ref[:, cols] = (summed / total).astype(o_ref.dtype)
+        for start in range(0, lon_total, chunk):
+            rows = slice(start * levels, (start + chunk) * levels)
+            cols = slice(h * head_dim, (h + 1) * head_dim)
+            bias = jnp.concatenate(
+                [base if i == 0 else pltpu.roll(base, i * levels, 1) for i in range(start, start + chunk)],
+                axis=0,
+            )
+            q = x_ref[rows, cols]
+            s = lax.dot_general(q, k, (((1,), (1,)), ((), ())), preferred_element_type=jnp.float32)
+            s = s * (head_dim ** (-0.5)) + bias
+            row_max = jnp.max(s, axis=-1, keepdims=True)
+            weights = jnp.exp(s - row_max)
+            total = jnp.sum(weights, axis=-1, keepdims=True)
+            summed = jnp.dot(weights.astype(jnp.bfloat16), v, preferred_element_type=jnp.float32)
+            o_ref[rows, cols] = (summed / total).astype(o_ref.dtype)
 
 
 def attend(x, bias_base, head_dim):
     heads, levels, keys = bias_base.shape
     return pl.pallas_call(
-        functools.partial(attention_kernel, heads=heads, head_dim=head_dim, levels=levels),
+        functools.partial(attention_kernel, heads=heads, head_dim=head_dim, levels=levels, chunk=8),
         out_shape=jax.ShapeDtypeStruct((x.shape[0], heads * head_dim), jnp.bfloat16),
         in_specs=[pl.BlockSpec(memory_space=pltpu.VMEM)] * 2,
         out_specs=pl.BlockSpec(memory_space=pltpu.VMEM),
-        scratch_shapes=[pltpu.VMEM((heads, x.shape[0], keys), jnp.float32)],
     )(x, bias_base)
 
 

time: 240 us -> 257 us (1.071)
  Pallas kernels: 15.6 us -> 32.8 us
    pallas_call x4, Pallas kernels: 15.6 us -> 32.8 us  [attend(): pl.pallas_call(functools.partial(attention_kernel, heads=heads, head_dim=...]
where the time goes in v10:
time: 257 us; the launch traced here: 255 us
  blocking collectives  106 us (41%)
  starting transfers between devices  51.1 us (20%)
  waiting for transfers between devices  33 us (13%)
  Pallas kernels  32.8 us (13%)
  local copies, waits for them, and re-layouts  11.6 us (5%)
  other arithmetic  9.03 us (4%)
  matrix products  6.77 us (3%)
  between operations  4.74 us (2%)
    all_to_all x4, blocking collectives, block(): returned = lax.all_to_all(back, 'lon', 0, 0, tiled=True)  55.1 us
    all_to_all x3, blocking collectives, block(): incoming = lax.all_to_all(outgoing, 'lon', 0, 0, tiled=True)  50.4 us
    pallas_call x4, Pallas kernels, attend(): pl.pallas_call(functools.partial(attention_kernel, heads=heads, head_dim=...  32.8 us
    ppermute x4, starting transfers between devices, lat_halo(): before = lax.ppermute(array[:, length - width:], 'lat', up)  24.3 us
    ppermute x4, waiting for transfers between devices, lat_halo(): after = lax.ppermute(array[:, :width], 'lat', down)  12.1 us
    all_to_all x1, waiting for transfers between devices, block(): incoming = lax.all_to_all(outgoing, 'lon', 0, 0, tiled=True)  10.3 us
    all_to_all x1, starting transfers between devices, block(): incoming = lax.all_to_all(outgoing, 'lon', 0, 0, tiled=True)  10.3 us
    ppermute x4, starting transfers between devices, lat_halo(): after = lax.ppermute(array[:, :width], 'lat', down)  9.84 us
  transfers between devices with their start and end apart: 12, of which 9 were waited for; matrix products, arithmetic and copies ran while one was open for 1% of the time, Pallas kernels for 0%

profile of v10, /device:TPU:1, one launch (start us, length us, event | category | flops | bytes accessed | tf_op | source)
XLA Modules:
  0.0 254.6 jit_solution(9545887251810983776)
XLA Ops:
  0.0 1.5 fusion.125
  14.2 10.3 %all-to-all-start = ((bf16[16,32,288]{2,1,0:T(8,128)(2,1)}), bf16[16,32,288]{2,1,0:T(8,128)(2,1)}, u32[]{:S(2)}, u32[]{:S(2)}) async-start(bf16[16,32,288]{2,1,0:T(8,128)(2,1)} %bitcast.7), calls=%async_computation | async-start | bytes 786432 | tf_op jit(solution)/shard_map/all_to_all | solution.py:91
  26.5 10.3 %all-to-all-done = bf16[16,32,288]{2,1,0:T(8,128)(2,1)} async-done(((bf16[16,32,288]{2,1,0:T(8,128)(2,1)}), bf16[16,32,288]{2,1,0:T(8,128)(2,1)}, u32[]{:S(2)}, u32[]{:S(2)}) %all-to-all-start) | async-done | bytes 294944 | tf_op jit(solution)/shard_map/all_to_all | solution.py:91
  36.8 8.2 %shard_map.118 = bf16[512,96]{1,0:T(8,128)(2,1)} custom-call(bf16[512,288]{1,0:T(8,128)(2,1)} %bitcast.8.x_ref, f32[3,8,512]{2,1,0:T(8,128)} %reshape.272.base_ref), custom_call_target="tpu_custom_call" | custom-call | tf_op jit(solution)/shard_map/pallas_call | solution.py:62
  45.0 15.3 %all_to_all.40 = bf16[16,32,96]{2,1,0:T(8,128)(2,1)S(1)} all-to-all(bf16[16,32,96]{2,1,0:T(8,128)(2,1)} %bitcast.193), channel_id=1, replica_groups=mesh['lon'=16,'lat'=16,'segment'=2] {'lon'}, dimensions={0} | all-to-all | bytes 196608 | tf_op jit(solution)/shard_map/all_to_all | solution.py:94
  61.0 6.3 %collective-permute-start = (bf16[2,2,4,8,384]{4,3,1,0,2:T(8,128)(2,1)S(1)}, bf16[2,2,4,8,384]{4,3,1,0,2:T(8,128)(2,1)S(1)}, u32[]{:S(2)}, u32[]{:S(2)}) collective-permute-start(bf16[2,2,4,8,384]{4,3,1,0,2:T(8,128)(2,1)S(1)} %multiply_convert_fusion.9), channel_id=1, source_target_pairs={{0,2},{2,4},{4,6},{6,8},{8,10},{10,12},{12,14},{14,16},{16,18},{18... | collective-permute-start | bytes 294920 | tf_op jit(solution)/shard_map/ppermute | solution.py:24
  67.4 1.9 collective-permute-start.1
  69.4 4.0 %collective-permute-done.1 = bf16[2,2,4,8,384]{4,3,1,0,2:T(8,128)(2,1)S(1)} collective-permute-done((bf16[2,2,4,8,384]{4,3,1,0,2:T(8,128)(2,1)S(1)}, bf16[2,2,4,8,384]{4,3,1,0,2:T(8,128)(2,1)S(1)}, u32[]{:S(2)}, u32[]{:S(2)}) %collective-permute-start.1) | collective-permute-done | bytes 98336 | tf_op jit(solution)/shard_map/ppermute | solution.py:25
  75.5 2.2 collective-permute-start.2
  77.7 3.1 %collective-permute-done.2 = bf16[2,2,4,8,384]{4,3,1,0,2:T(8,128)(2,1)S(1)} collective-permute-done((bf16[2,2,4,8,384]{4,3,1,0,2:T(8,128)(2,1)S(1)}, bf16[2,2,4,8,384]{4,3,1,0,2:T(8,128)(2,1)S(1)}, u32[]{:S(2)}, u32[]{:S(2)}) %collective-permute-start.2) | collective-permute-done | bytes 98336 | tf_op jit(solution)/shard_map/ppermute | solution.py:115
  81.9 16.6 %all_to_all.41 = bf16[16,32,288]{2,1,0:T(8,128)(2,1)} all-to-all(bf16[16,32,288]{2,1,0:T(8,128)(2,1)S(1)} %bitcast.185), channel_id=1, replica_groups=mesh['lon'=16,'lat'=16,'segment'=2] {'lon'}, dimensions={0} | all-to-all | bytes 589824 | tf_op jit(solution)/shard_map/all_to_all | solution.py:91
  98.5 8.2 %shard_map.119 = bf16[512,96]{1,0:T(8,128)(2,1)} custom-call(bf16[512,288]{1,0:T(8,128)(2,1)} %bitcast.183, f32[3,8,512]{2,1,0:T(8,128)} %reshape.272.base_ref), custom_call_target="tpu_custom_call" | custom-call | tf_op jit(solution)/shard_map/pallas_call | solution.py:62
  106.7 13.4 %all_to_all.42 = bf16[16,32,96]{2,1,0:T(8,128)(2,1)S(1)} all-to-all(bf16[16,32,96]{2,1,0:T(8,128)(2,1)} %bitcast.194), channel_id=1, replica_groups=mesh['lon'=16,'lat'=16,'segment'=2] {'lon'}, dimensions={0} | all-to-all | bytes 196608 | tf_op jit(solution)/shard_map/all_to_all | solution.py:94
  120.9 6.7 %collective-permute-start.3 = (bf16[2,2,4,8,384]{4,3,1,0,2:T(8,128)(2,1)S(1)}, bf16[2,2,4,8,384]{4,3,1,0,2:T(8,128)(2,1)S(1)}, u32[]{:S(2)}, u32[]{:S(2)}) collective-permute-start(bf16[2,2,4,8,384]{4,3,1,0,2:T(8,128)(2,1)S(1)} %multiply_convert_fusion.6), channel_id=1, source_target_pairs={{0,2},{2,4},{4,6},{6,8},{8,10},{10,12},{12,14},{14,16},{16,18},{18... | collective-permute-start | bytes 294920 | tf_op jit(solution)/shard_map/ppermute | solution.py:24
  127.6 2.1 collective-permute-start.4
  129.7 3.8 %collective-permute-done.4 = bf16[2,2,4,8,384]{4,3,1,0,2:T(8,128)(2,1)S(1)} collective-permute-done((bf16[2,2,4,8,384]{4,3,1,0,2:T(8,128)(2,1)S(1)}, bf16[2,2,4,8,384]{4,3,1,0,2:T(8,128)(2,1)S(1)}, u32[]{:S(2)}, u32[]{:S(2)}) %collective-permute-start.4) | collective-permute-done | bytes 98336 | tf_op jit(solution)/shard_map/ppermute | solution.py:25
  135.8 2.2 collective-permute-start.5
  138.0 3.1 %collective-permute-done.5 = bf16[2,2,4,8,384]{4,3,1,0,2:T(8,128)(2,1)S(1)} collective-permute-done((bf16[2,2,4,8,384]{4,3,1,0,2:T(8,128)(2,1)S(1)}, bf16[2,2,4,8,384]{4,3,1,0,2:T(8,128)(2,1)S(1)}, u32[]{:S(2)}, u32[]{:S(2)}) %collective-permute-start.5) | collective-permute-done | bytes 98336 | tf_op jit(solution)/shard_map/ppermute | solution.py:115
  142.2 17.1 %all_to_all.43 = bf16[16,32,288]{2,1,0:T(8,128)(2,1)} all-to-all(bf16[16,32,288]{2,1,0:T(8,128)(2,1)S(1)} %bitcast.186), channel_id=1, replica_groups=mesh['lon'=16,'lat'=16,'segment'=2] {'lon'}, dimensions={0} | all-to-all | bytes 589824 | tf_op jit(solution)/shard_map/all_to_all | solution.py:91
  159.3 8.2 %shard_map.120 = bf16[512,96]{1,0:T(8,128)(2,1)} custom-call(bf16[512,288]{1,0:T(8,128)(2,1)} %bitcast.184, f32[3,8,512]{2,1,0:T(8,128)} %reshape.272.base_ref), custom_call_target="tpu_custom_call" | custom-call | tf_op jit(solution)/shard_map/pallas_call | solution.py:62
  167.5 13.1 %all_to_all.44 = bf16[16,32,96]{2,1,0:T(8,128)(2,1)S(1)} all-to-all(bf16[16,32,96]{2,1,0:T(8,128)(2,1)} %bitcast.195), channel_id=1, replica_groups=mesh['lon'=16,'lat'=16,'segment'=2] {'lon'}, dimensions={0} | all-to-all | bytes 196608 | tf_op jit(solution)/shard_map/all_to_all | solution.py:94
  181.4 6.5 %collective-permute-start.6 = (bf16[2,2,4,8,384]{4,3,1,0,2:T(8,128)(2,1)S(1)}, bf16[2,2,4,8,384]{4,3,1,0,2:T(8,128)(2,1)S(1)}, u32[]{:S(2)}, u32[]{:S(2)}) collective-permute-start(bf16[2,2,4,8,384]{4,3,1,0,2:T(8,128)(2,1)S(1)} %multiply_convert_fusion.4), channel_id=1, source_target_pairs={{0,2},{2,4},{4,6},{6,8},{8,10},{10,12},{12,14},{14,16},{16,18},{18... | collective-permute-start | bytes 294920 | tf_op jit(solution)/shard_map/ppermute | solution.py:24
  187.9 1.9 collective-permute-start.7
  189.8 4.0 %collective-permute-done.7 = bf16[2,2,4,8,384]{4,3,1,0,2:T(8,128)(2,1)S(1)} collective-permute-done((bf16[2,2,4,8,384]{4,3,1,0,2:T(8,128)(2,1)S(1)}, bf16[2,2,4,8,384]{4,3,1,0,2:T(8,128)(2,1)S(1)}, u32[]{:S(2)}, u32[]{:S(2)}) %collective-permute-start.7) | collective-permute-done | bytes 98336 | tf_op jit(solution)/shard_map/ppermute | solution.py:25
  196.0 2.2 collective-permute-start.8
  198.3 3.1 %collective-permute-done.8 = bf16[2,2,4,8,384]{4,3,1,0,2:T(8,128)(2,1)S(1)} collective-permute-done((bf16[2,2,4,8,384]{4,3,1,0,2:T(8,128)(2,1)S(1)}, bf16[2,2,4,8,384]{4,3,1,0,2:T(8,128)(2,1)S(1)}, u32[]{:S(2)}, u32[]{:S(2)}) %collective-permute-start.8) | collective-permute-done | bytes 98336 | tf_op jit(solution)/shard_map/ppermute | solution.py:115
  202.5 16.8 %all_to_all.45 = bf16[16,32,288]{2,1,0:T(8,128)(2,1)} all-to-all(bf16[16,32,288]{2,1,0:T(8,128)(2,1)S(1)} %bitcast.187), channel_id=1, replica_groups=mesh['lon'=16,'lat'=16,'segment'=2] {'lon'}, dimensions={0} | all-to-all | bytes 589824 | tf_op jit(solution)/shard_map/all_to_all | solution.py:91
  219.2 8.2 %shard_map.121 = bf16[512,96]{1,0:T(8,128)(2,1)} custom-call(bf16[512,288]{1,0:T(8,128)(2,1)} %bitcast.182, f32[3,8,512]{2,1,0:T(8,128)} %reshape.272.base_ref), custom_call_target="tpu_custom_call" | custom-call | tf_op jit(solution)/shard_map/pallas_call | solution.py:62
  227.4 13.3 %all_to_all.46 = bf16[16,32,96]{2,1,0:T(8,128)(2,1)S(1)} all-to-all(bf16[16,32,96]{2,1,0:T(8,128)(2,1)} %bitcast.192), channel_id=1, replica_groups=mesh['lon'=16,'lat'=16,'segment'=2] {'lon'}, dimensions={0} | all-to-all | bytes 196608 | tf_op jit(solution)/shard_map/all_to_all | solution.py:94
  241.4 3.9 %collective-permute-start.10 = (bf16[2,2,4,8,384]{4,3,1,0,2:T(8,128)(2,1)S(1)}, bf16[2,2,4,8,384]{4,3,1,0,2:T(8,128)(2,1)S(1)}, u32[]{:S(2)}, u32[]{:S(2)}) collective-permute-start(bf16[2,2,4,8,384]{4,3,1,0,2:T(8,128)(2,1)S(1)} %multiply_convert_fusion.1), channel_id=1, source_target_pairs={{2,0},{4,2},{6,4},{8,6},{10,8},{12,10},{14,12},{16,14},{18,16},{20... | collective-permute-start | bytes 294920 | tf_op jit(solution)/shard_map/ppermute | solution.py:25
  245.4 4.7 %collective-permute-start.9 = (bf16[2,2,4,8,384]{4,3,1,0,2:T(8,128)(2,1)S(1)}, bf16[2,2,4,8,384]{4,3,1,0,2:T(8,128)(2,1)S(1)}, u32[]{:S(2)}, u32[]{:S(2)}) collective-permute-start(bf16[2,2,4,8,384]{4,3,1,0,2:T(8,128)(2,1)S(1)} %multiply_convert_fusion.1), channel_id=1, source_target_pairs={{0,2},{2,4},{4,6},{6,8},{8,10},{10,12},{12,14},{14,16},{16,18},{18... | collective-permute-start | bytes 294920 | tf_op jit(solution)/shard_map/ppermute | solution.py:24
  250.4 1.3 collective-permute-done.9
  (121 shorter events, 26.3 us)
Async XLA Ops:
  0.0 73.8 %copy-start = (bf16[1,384,1536]{2,1,0:T(8,128)(2,1)S(1)}, bf16[1,384,1536]{2,1,0:T(8,128)(2,1)}, u32[]{:S(2)}) copy-start(bf16[1,384,1536]{2,1,0:T(8,128)(2,1)} %param.19) | copy-start | bytes 3538948
  0.0 11.9 %copy-start.3 = (bf16[1,384,1152]{2,1,0:T(8,128)(2,1)S(1)}, bf16[1,384,1152]{2,1,0:T(8,128)(2,1)}, u32[]{:S(2)}) copy-start(bf16[1,384,1152]{2,1,0:T(8,128)(2,1)} %param.17) | copy-start | bytes 2654212
  14.2 22.5 %all-to-all-start = ((bf16[16,32,288]{2,1,0:T(8,128)(2,1)}), bf16[16,32,288]{2,1,0:T(8,128)(2,1)}, u32[]{:S(2)}, u32[]{:S(2)}) async-start(bf16[16,32,288]{2,1,0:T(8,128)(2,1)} %bitcast.7), calls=%async_computation | async-start | bytes 786432 | tf_op jit(solution)/shard_map/all_to_all | solution.py:91
  25.2 35.1 %copy-start.1 = (bf16[1,384,384]{2,1,0:T(8,128)(2,1)S(1)}, bf16[1,384,384]{2,1,0:T(8,128)(2,1)}, u32[]{:S(2)}) copy-start(bf16[1,384,384]{2,1,0:T(8,128)(2,1)} %param.18) | copy-start | bytes 884740
  25.5 35.1 %copy-start.2 = (f32[2,2,4,8,384]{4,3,2,1,0:T(8,128)S(1)}, f32[2,2,4,8,384]{4,3,2,1,0:T(8,128)}, u32[]{:S(2)}) copy-start(f32[2,2,4,8,384]{4,3,2,1,0:T(8,128)} %param.12) | copy-start | bytes 589828
  36.8 32.5 %copy-start.4 = (f32[1,5,384]{2,0,1:T(1,128)S(1)}, f32[1,5,384]{2,0,1:T(1,128)}, u32[]{:S(2)}) copy-start(f32[1,5,384]{2,0,1:T(1,128)} %param.22) | copy-start | bytes 23044
  61.0 8.3 %collective-permute-start = (bf16[2,2,4,8,384]{4,3,1,0,2:T(8,128)(2,1)S(1)}, bf16[2,2,4,8,384]{4,3,1,0,2:T(8,128)(2,1)S(1)}, u32[]{:S(2)}, u32[]{:S(2)}) collective-permute-start(bf16[2,2,4,8,384]{4,3,1,0,2:T(8,128)(2,1)S(1)} %multiply_convert_fusion.9), channel_id=1, source_target_pairs={{0,2},{2,4},{4,6},{6,8},{8,10},{10,12},{12,14},{14,16},{16,18},{18... | collective-permute-start | bytes 294920 | tf_op jit(solution)/shard_map/ppermute | solution.py:24
  67.4 5.9 %collective-permute-start.1 = (bf16[2,2,4,8,384]{4,3,1,0,2:T(8,128)(2,1)S(1)}, bf16[2,2,4,8,384]{4,3,1,0,2:T(8,128)(2,1)S(1)}, u32[]{:S(2)}, u32[]{:S(2)}) collective-permute-start(bf16[2,2,4,8,384]{4,3,1,0,2:T(8,128)(2,1)S(1)} %multiply_convert_fusion.9), channel_id=1, source_target_pairs={{2,0},{4,2},{6,4},{8,6},{10,8},{12,10},{14,12},{16,14},{18,16},{20... | collective-permute-start | bytes 294920 | tf_op jit(solution)/shard_map/ppermute | solution.py:25
  73.8 1.3 copy-start.5
  75.5 5.4 %collective-permute-start.2 = (bf16[2,2,4,8,384]{4,3,1,0,2:T(8,128)(2,1)S(1)}, bf16[2,2,4,8,384]{4,3,1,0,2:T(8,128)(2,1)S(1)}, u32[]{:S(2)}, u32[]{:S(2)}) collective-permute-start(bf16[2,2,4,8,384]{4,3,1,0,2:T(8,128)(2,1)S(1)} %fusion.40), channel_id=1, source_target_pairs={{0,1},{1,0},{2,3},{3,2},{4,5},{5,4},{6,7},{7,6},{8,9},{9,8},{10,11... | collective-permute-start | bytes 294920 | tf_op jit(solution)/shard_map/ppermute | solution.py:115
  120.9 8.8 %collective-permute-start.3 = (bf16[2,2,4,8,384]{4,3,1,0,2:T(8,128)(2,1)S(1)}, bf16[2,2,4,8,384]{4,3,1,0,2:T(8,128)(2,1)S(1)}, u32[]{:S(2)}, u32[]{:S(2)}) collective-permute-start(bf16[2,2,4,8,384]{4,3,1,0,2:T(8,128)(2,1)S(1)} %multiply_convert_fusion.6), channel_id=1, source_target_pairs={{0,2},{2,4},{4,6},{6,8},{8,10},{10,12},{12,14},{14,16},{16,18},{18... | collective-permute-start | bytes 294920 | tf_op jit(solution)/shard_map/ppermute | solution.py:24
  127.6 5.9 %collective-permute-start.4 = (bf16[2,2,4,8,384]{4,3,1,0,2:T(8,128)(2,1)S(1)}, bf16[2,2,4,8,384]{4,3,1,0,2:T(8,128)(2,1)S(1)}, u32[]{:S(2)}, u32[]{:S(2)}) collective-permute-start(bf16[2,2,4,8,384]{4,3,1,0,2:T(8,128)(2,1)S(1)} %multiply_convert_fusion.6), channel_id=1, source_target_pairs={{2,0},{4,2},{6,4},{8,6},{10,8},{12,10},{14,12},{16,14},{18,16},{20... | collective-permute-start | bytes 294920 | tf_op jit(solution)/shard_map/ppermute | solution.py:25
  134.1 1.3 copy-start.6
  135.8 5.4 %collective-permute-start.5 = (bf16[2,2,4,8,384]{4,3,1,0,2:T(8,128)(2,1)S(1)}, bf16[2,2,4,8,384]{4,3,1,0,2:T(8,128)(2,1)S(1)}, u32[]{:S(2)}, u32[]{:S(2)}) collective-permute-start(bf16[2,2,4,8,384]{4,3,1,0,2:T(8,128)(2,1)S(1)} %fusion.37), channel_id=1, source_target_pairs={{0,1},{1,0},{2,3},{3,2},{4,5},{5,4},{6,7},{7,6},{8,9},{9,8},{10,11... | collective-permute-start | bytes 294920 | tf_op jit(solution)/shard_map/ppermute | solution.py:115
  181.4 8.5 %collective-permute-start.6 = (bf16[2,2,4,8,384]{4,3,1,0,2:T(8,128)(2,1)S(1)}, bf16[2,2,4,8,384]{4,3,1,0,2:T(8,128)(2,1)S(1)}, u32[]{:S(2)}, u32[]{:S(2)}) collective-permute-start(bf16[2,2,4,8,384]{4,3,1,0,2:T(8,128)(2,1)S(1)} %multiply_convert_fusion.4), channel_id=1, source_target_pairs={{0,2},{2,4},{4,6},{6,8},{8,10},{10,12},{12,14},{14,16},{16,18},{18... | collective-permute-start | bytes 294920 | tf_op jit(solution)/shard_map/ppermute | solution.py:24
  187.9 5.9 %collective-permute-start.7 = (bf16[2,2,4,8,384]{4,3,1,0,2:T(8,128)(2,1)S(1)}, bf16[2,2,4,8,384]{4,3,1,0,2:T(8,128)(2,1)S(1)}, u32[]{:S(2)}, u32[]{:S(2)}) collective-permute-start(bf16[2,2,4,8,384]{4,3,1,0,2:T(8,128)(2,1)S(1)} %multiply_convert_fusion.4), channel_id=1, source_target_pairs={{2,0},{4,2},{6,4},{8,6},{10,8},{12,10},{14,12},{16,14},{18,16},{20... | collective-permute-start | bytes 294920 | tf_op jit(solution)/shard_map/ppermute | solution.py:25
  194.4 1.3 copy-start.7
  196.0 5.4 %collective-permute-start.8 = (bf16[2,2,4,8,384]{4,3,1,0,2:T(8,128)(2,1)S(1)}, bf16[2,2,4,8,384]{4,3,1,0,2:T(8,128)(2,1)S(1)}, u32[]{:S(2)}, u32[]{:S(2)}) collective-permute-start(bf16[2,2,4,8,384]{4,3,1,0,2:T(8,128)(2,1)S(1)} %fusion.34), channel_id=1, source_target_pairs={{0,1},{1,0},{2,3},{3,2},{4,5},{5,4},{6,7},{7,6},{8,9},{9,8},{10,11... | collective-permute-start | bytes 294920 | tf_op jit(solution)/shard_map/ppermute | solution.py:115
  241.4 9.0 %collective-permute-start.10 = (bf16[2,2,4,8,384]{4,3,1,0,2:T(8,128)(2,1)S(1)}, bf16[2,2,4,8,384]{4,3,1,0,2:T(8,128)(2,1)S(1)}, u32[]{:S(2)}, u32[]{:S(2)}) collective-permute-start(bf16[2,2,4,8,384]{4,3,1,0,2:T(8,128)(2,1)S(1)} %multiply_convert_fusion.1), channel_id=1, source_target_pairs={{2,0},{4,2},{6,4},{8,6},{10,8},{12,10},{14,12},{16,14},{18,16},{20... | collective-permute-start | bytes 294920 | tf_op jit(solution)/shard_map/ppermute | solution.py:25
  245.4 6.4 %collective-permute-start.9 = (bf16[2,2,4,8,384]{4,3,1,0,2:T(8,128)(2,1)S(1)}, bf16[2,2,4,8,384]{4,3,1,0,2:T(8,128)(2,1)S(1)}, u32[]{:S(2)}, u32[]{:S(2)}) collective-permute-start(bf16[2,2,4,8,384]{4,3,1,0,2:T(8,128)(2,1)S(1)} %multiply_convert_fusion.1), channel_id=1, source_target_pairs={{0,2},{2,4},{4,6},{6,8},{8,10},{10,12},{12,14},{14,16},{16,18},{18... | collective-permute-start | bytes 294920 | tf_op jit(solution)/shard_map/ppermute | solution.py:24
  252.3 1.3 copy-start.8
